TPU v7x, 256 devices: a whole 4x4x8 slice. The times are simulated.
256 devices in a mesh: orb: 8 (over z_lo, core), box: 32 (over x, y, z_hi).
Axes of the slice: x: 4, y: 4, z: 8 (z_hi: 2, z_lo: 4; z = z_hi * 4 + z_lo), core: 2. Of those that a mesh axis runs over, the one named last changes fastest.
Arguments:
- orbitals: bfloat16 [768, 256, 1000], P('orb', 'box'), may hold values from -6 to 6
- exchange_values: bfloat16 [768, 256, 1000], P('orb', 'box'), may hold values from -6 to 6
- local_values: float32 [256, 1000], P('box'), may hold values from -6 to 6
- coupling: bfloat16 [768, 768], P('orb'), may hold values from -0.21875 to 0.21875
- to_values_mat: float32 [10, 10], replicated, may hold values from -2 to 2
- to_coeffs_mat: float32 [10, 10], replicated, may hold values from -2 to 2
- laplace_blocks: float32 [3, 10, 10], replicated, may hold values from -2 to 2
- box_counts: int32 [32], P('box'), may hold values from 2 to 8, as said below
- kept_mask: int32 [256], P('box'), may hold values from 0 to 1, as said below
- send_list: int32 [32, 32], P('box'), may hold values from -1 to 7, as said below
- neighbour_pos: int32 [6, 256], P(None, 'box'), may hold values from -1 to 39, as said below
Outputs:
- h_orbitals: bfloat16 [768, 256, 1000], P('orb', 'box')
Inputs may be any that keep to these rules, and one draw needn't show every extreme that they name: Device d of box holds live boxes in slots 0 to box_counts[d] - 1 of its 8; some device holds 8. `kept_mask`: 1 only on live boxes; at most 4 ones in one device's range, and exactly 4 in some device's range. `send_list`: row q, entries p * 1 to p + 1 - 1: live slots of device q's range passed to device p, -1 for an empty entry; nothing to its own device; at most 1 to one device, exactly 1 to the devices whose index differs by one. `neighbour_pos`: Boxes that are not live have -1 on every face.
All inputs are finite; a program needn't handle non-finite values.
Results may differ from a plain program's by a relative error of at most 0.0031.
Values may be sent and summed in bfloat16 or wider, within the bound.
No kernel may reach another device: no remote copies, remote signals or barrier semaphores. Data moves between devices by JAX's collectives and lax.ppermute only.
A program may use at most 256 MiB of HBM per device.

v0:
```python
import jax
import jax.numpy as jnp
from jax import lax
from jax.sharding import PartitionSpec as P


def along_axis(flat, matrix, which):
    order_k = matrix.shape[0]
    width = flat.shape[-1]
    if which == 0:
        shaped = flat.reshape(-1, order_k, width // order_k)
        result = jnp.einsum("ax,nxr->nar", matrix, shaped, precision=lax.Precision.HIGHEST)
        return result.reshape(flat.shape)
    ident = jnp.eye(order_k, dtype=jnp.float32)
    if which == 1:
        square = jnp.kron(matrix, ident)
    else:
        square = jnp.kron(ident, matrix)
    inner = order_k * order_k
    result = jnp.dot(flat.reshape(-1, inner), square.T, precision=lax.Precision.HIGHEST)
    return result.reshape(flat.shape)


def three_way(flat, matrix):
    order_k = matrix.shape[0]
    inner = order_k * order_k
    first = along_axis(flat, matrix, 0)
    square = jnp.kron(matrix, matrix)
    result = jnp.dot(first.reshape(-1, inner), square.T, precision=lax.Precision.HIGHEST)
    return result.reshape(flat.shape)


def shards(
    orbitals,
    exchange_values,
    local_values,
    coupling,
    to_values_mat,
    to_coeffs_mat,
    laplace_blocks,
    box_counts,
    kept_mask,
    send_list,
    neighbour_pos,
):
    orb_dev, box_dev, width = orbitals.shape
    live = lax.iota(jnp.int32, box_dev) < box_counts[0]
    kept = kept_mask > 0
    slots = send_list[0]
    picked = jnp.take(orbitals, jnp.maximum(slots, 0), axis=1)
    outgoing = jnp.where((slots >= 0)[None, :, None], picked, jnp.zeros_like(picked))
    incoming = lax.all_to_all(outgoing, "box", split_axis=1, concat_axis=1, tiled=True)
    center = orbitals.astype(jnp.float32)
    values = three_way(center, to_values_mat)
    products = jnp.where(
        kept[None, :, None], exchange_values.astype(jnp.float32) * values, 0.0
    ).astype(jnp.bfloat16)
    mixed = jnp.dot(
        coupling,
        lax.all_gather(products.reshape(orb_dev, box_dev * width), "orb", axis=0, tiled=True),
        preferred_element_type=jnp.float32,
    )
    exchange = mixed.reshape(orb_dev, box_dev, width)
    weighted = local_values[None, :, :] * values - exchange
    potential_part = three_way(weighted, to_coeffs_mat)
    pool = jnp.concatenate([orbitals, incoming], axis=1)
    kinetic = jnp.zeros_like(center)
    for which in range(3):
        kinetic = kinetic + along_axis(center, laplace_blocks[0], which)
        for side in range(2):
            face_pos = neighbour_pos[2 * which + side]
            moved = jnp.take(pool, jnp.maximum(face_pos, 0), axis=1)
            moved = jnp.where((face_pos >= 0)[None, :, None], moved, jnp.zeros_like(moved))
            kinetic = kinetic + along_axis(
                moved.astype(jnp.float32), laplace_blocks[1 + side], which
            )
    total = potential_part - 0.5 * kinetic
    total = jnp.where(live[None, :, None], total, 0.0)
    return total.astype(jnp.bfloat16)


def solution(mesh):
    return jax.shard_map(
        shards,
        mesh=mesh,
        in_specs=(
            P("orb", "box", None),
            P("orb", "box", None),
            P("box", None),
            P("orb", None),
            P(),
            P(),
            P(),
            P("box"),
            P("box"),
            P("box", None),
            P(None, "box"),
        ),
        out_specs=P("orb", "box", None),
        check_vma=False,
    )
```

profile of v0, /device:TPU:64, one launch (start us, length us, event | category | flops | bytes accessed | tf_op | source)
XLA Modules:
  0.0 524.5 jit_solution(15945661767373708049)
XLA Ops:
  8.4 6.4 %reshape.298 = bf16[768,10,100]{2,1,0:T(8,128)(2,1)} reshape(bf16[96,8,1000]{2,1,0:T(8,128)(2,1)} %param.13) | data formatting | bytes 3072000 | tf_op jit(solution)/shard_map/reshape | solution.py:11
  23.7 6.4 %copy.54 = f32[768,10,100]{2,1,0:T(8,128)} copy(f32[768,10,100]{0,1,2:T(8,128)} %convolution_bitcast_fusion.4) | data formatting | bytes 6144000 | tf_op jit(solution)/shard_map/ax,nxr->nar/transpose | solution.py:12
  30.1 6.3 %reshape_reshape.6 = f32[7680,100]{1,0:T(8,128)} reshape(f32[768,10,100]{2,1,0:T(8,128)} %copy.54) | data formatting | bytes 6144000 | tf_op jit(solution)/shard_map/reshape;reshape | solution.py:29
  36.4 6.3 %fusion.6 = f32[7680,100]{1,0:T(8,128)} fusion(f32[7680,100]{1,0:T(8,128)} %reshape_reshape.6, f32[100,100]{1,0:T(8,128)S(1)} %mul.216), kind=kOutput, calls=%fused_computation.76 | convolution fusion | flops 921600000 | bytes 6184000 | tf_op jit(solution)/shard_map/dot_general | solution.py:29
  53.8 21.3 %gather_fusion = bf16[32,96,1000]{2,0,1:T(8,128)(2,1)} fusion(bf16[96,8,1000]{2,1,0:T(8,128)(2,1)S(1)} %copy-done.1, s32[1024]{0:T(1024)S(1)} %pad_clamp_fusion.6), kind=kCustom, calls=%fused_computation.6 | custom fusion | bytes 12288128 | tf_op jit(solution)/shard_map/jit(_take)/gather | solution.py:50
  78.7 6.1 %copy.62 = bf16[96,32,1000]{2,0,1:T(8,128)(2,1)} copy(bf16[96,32,1000]{2,1,0:T(8,128)(2,1)S(1)} %select_bitcast_fusion) | data formatting | bytes 12288000 | tf_op jit(solution)/shard_map/jit(_where)/select_n | solution.py:51
  84.8 12.6 %all-to-all-start = ((bf16[96,32,1000]{2,0,1:T(8,128)(2,1)}), bf16[96,32,1000]{2,0,1:T(8,128)(2,1)}, u32[]{:S(2)}, u32[]{:S(2)}) async-start(bf16[96,32,1000]{2,0,1:T(8,128)(2,1)} %copy.62), calls=%async_computation | async-start | bytes 12582912 | tf_op jit(solution)/shard_map/all_to_all | solution.py:52
  101.3 5.9 %reshape.299 = f32[768,10,100]{2,1,0:T(8,128)} reshape(f32[7680,100]{1,0:T(8,128)} %fusion.6) | data formatting | bytes 6144000 | tf_op jit(solution)/shard_map/reshape | solution.py:30
  110.3 6.8 %mul.212 = f32[768,10,100]{2,1,0:T(8,128)} reshape(f32[96,8,1000]{2,1,0:T(8,128)} %mul.211) | data formatting | bytes 6144000 | tf_op jit(solution)/shard_map/mul | solution.py:64
  132.7 5.1 copy.76
  148.0 5.2 copy.71
  153.1 5.1 reshape.307
  164.8 146.4 %all-to-all-done = bf16[96,32,1000]{2,0,1:T(8,128)(2,1)} async-done(((bf16[96,32,1000]{2,0,1:T(8,128)(2,1)}), bf16[96,32,1000]{2,0,1:T(8,128)(2,1)}, u32[]{:S(2)}, u32[]{:S(2)}) %all-to-all-start) | async-done | bytes 6144032 | tf_op jit(solution)/shard_map/all_to_all | solution.py:52
  311.3 6.5 %constant_dynamic-update-slice_fusion = bf16[96,40,1000]{2,0,1:T(8,128)(2,1)} fusion(bf16[96,40,1000]{2,0,1:T(8,128)(2,1)} %copy_dynamic-update-slice_fusion, bf16[96,32,1000]{2,0,1:T(8,128)(2,1)} %all-to-all-done), kind=kLoop, calls=%fused_computation.51 | loop fusion | bytes 12582912 | tf_op jit(solution)/shard_map/concatenate | solution.py:66
  365.6 5.4 %reshape.304 = bf16[768,10,100]{2,1,0:T(8,128)(2,1)S(1)} reshape(bf16[96,8,1000]{2,1,0:T(8,128)(2,1)} %copy.64) | data formatting | bytes 3072000 | tf_op jit(solution)/shard_map/reshape | solution.py:11
  375.1 5.4 %reshape.305 = bf16[768,10,100]{2,1,0:T(8,128)(2,1)S(1)} reshape(bf16[96,8,1000]{2,1,0:T(8,128)(2,1)} %copy.67) | data formatting | bytes 3072000 | tf_op jit(solution)/shard_map/reshape | solution.py:11
  398.3 5.5 %reshape.311 = f32[96,8,1000]{2,1,0:T(8,128)} reshape(f32[7680,100]{1,0:T(8,128)} %fusion.9) | data formatting | bytes 6144000 | tf_op jit(solution)/shard_map/reshape | solution.py:21
  407.4 5.2 reshape.314
  416.1 5.1 reshape.316
  423.4 7.4 %add_bitcast_fusion = f32[768,10,100]{0,1,2:T(8,128)} fusion(f32[768,100,10]{0,2,1:T(8,128)} %fusion, f32[768,100,10]{0,2,1:T(8,128)S(1)} %fusion.1, bf16[768,10,100]{0,1,2:T(8,128)(2,1)S(1)} %copy-done.6, f32[1,10,10]{2,0,1:T(1,128)S(1)} %get-tuple-element.20), kind=kOutput, calls=%fused_computation.12 | convolution fusion | flops 93696000 | bytes 10752400 | tf_op jit(solution)/shard_map/ax,nxr->nar/dot_general | solution.py:12
  430.8 6.4 %copy.70 = f32[768,10,100]{2,1,0:T(8,128)} copy(f32[768,10,100]{0,1,2:T(8,128)} %add_bitcast_fusion) | data formatting | bytes 6144000 | tf_op jit(solution)/shard_map/add | solution.py:74
  437.2 6.4 %add.42 = f32[96,8,1000]{2,1,0:T(8,128)} reshape(f32[768,10,100]{2,1,0:T(8,128)} %copy.70) | data formatting | bytes 6144000 | tf_op jit(solution)/shard_map/add | solution.py:74
  443.5 6.6 %convolution_bitcast_fusion.2 = f32[96,8000]{1,0:T(8,128)S(1)} fusion(bf16[96,768]{1,0:T(8,128)(2,1)S(1)} %copy-done, bf16[768,8000]{1,0:T(8,128)(2,1)} %all-gather.2.cloned.1.call-done), kind=kOutput, calls=%fused_computation.9 | convolution fusion | flops 1179648000 | bytes 15507456 | tf_op jit(solution)/shard_map/dot_general | solution.py:58
  450.2 5.8 %reshape.302 = f32[768,10,100]{2,1,0:T(8,128)} reshape(f32[96,8000]{1,0:T(8,128)S(1)} %convolution_bitcast_fusion.2) | data formatting | bytes 6144000 | tf_op jit(solution)/shard_map/reshape | solution.py:63
  456.0 10.2 %multiply_subtract_fusion = f32[768,10,100]{2,1,0:T(8,128)} fusion(f32[768,10,100]{2,1,0:T(8,128)} %reshape.302, f32[768,10,100]{2,1,0:T(8,128)} %mul.212, f32[768,10,100]{2,1,0:T(8,128)} %reshape.299), kind=kLoop, calls=%fused_computation.11 | loop fusion | flops 1536000 | bytes 12288000 | tf_op jit(solution)/shard_map/sub | solution.py:64
  466.2 6.4 %copy.57 = f32[768,10,100]{0,1,2:T(8,128)} copy(f32[768,10,100]{2,1,0:T(8,128)} %multiply_subtract_fusion) | data formatting | bytes 6144000 | tf_op jit(solution)/shard_map/sub | solution.py:64
  472.6 8.9 %convolution_bitcast_fusion.3 = f32[768,10,100]{0,1,2:T(8,128)} fusion(f32[768,10,100]{0,1,2:T(8,128)} %copy.57, f32[10,10]{1,0:T(8,128)S(1)} %copy-done.14), kind=kOutput, calls=%fused_computation.15 | convolution fusion | flops 92160000 | bytes 6144400 | tf_op jit(solution)/shard_map/ax,nxr->nar/dot_general | solution.py:12
  481.5 6.4 %copy.58 = f32[768,10,100]{2,1,0:T(8,128)} copy(f32[768,10,100]{0,1,2:T(8,128)} %convolution_bitcast_fusion.3) | data formatting | bytes 6144000 | tf_op jit(solution)/shard_map/ax,nxr->nar/transpose | solution.py:12
  487.9 6.3 %reshape_reshape.7 = f32[7680,100]{1,0:T(8,128)} reshape(f32[768,10,100]{2,1,0:T(8,128)} %copy.58) | data formatting | bytes 6144000 | tf_op jit(solution)/shard_map/reshape;reshape | solution.py:29
  494.2 6.2 %fusion.7 = f32[7680,100]{1,0:T(8,128)} fusion(f32[7680,100]{1,0:T(8,128)} %reshape_reshape.7, f32[100,100]{1,0:T(8,128)S(1)} %mul.222), kind=kOutput, calls=%fused_computation.77 | convolution fusion | flops 921600000 | bytes 6184000 | tf_op jit(solution)/shard_map/dot_general | solution.py:29
  500.5 5.3 %reshape.303 = f32[96,8,1000]{2,1,0:T(8,128)} reshape(f32[7680,100]{1,0:T(8,128)} %fusion.7) | data formatting | bytes 6144000 | tf_op jit(solution)/shard_map/reshape | solution.py:30
  505.8 11.5 %select_convert_fusion = bf16[96,8,1000]{2,1,0:T(8,128)(2,1)} fusion(f32[96,8,1000]{2,1,0:T(8,128)} %reshape.303, f32[96,8,1000]{2,1,0:T(8,128)} %reshape.316, f32[96,8,1000]{2,1,0:T(8,128)} %reshape.314, f32[96,8,1000]{2,1,0:T(8,128)S(1)} %copy-done.4, f32[96,8,1000]{2,1,0:T(8,128)} %reshape.311, f32[96,8,1000]{2,1,0:T(8,128)} %reshape.309, ...), kind=kLoop, calls=%fused_computation.13 | loop fusion | flops 7680000 | bytes 26112008 | tf_op jit(solution)/shard_map/convert_element_type | solution.py:79
  (109 shorter events, 142.6 us)
Async XLA Ops:
  6.5 437.0 %copy-start = (bf16[96,768]{1,0:T(8,128)(2,1)S(1)}, bf16[96,768]{1,0:T(8,128)(2,1)}, u32[]{:S(2)}) copy-start(bf16[96,768]{1,0:T(8,128)(2,1)} %param.16) | copy-start | bytes 442372
  6.5 437.0 %all-gather.2.cloned.1.call-start = ((), (), s32[]{:S(2)}) async-start(), calls=%async_computation.1 | async-start | bytes 13934592 | tf_op jit(solution)/shard_map/all_gather | solution.py:60
  14.8 4.5 copy-start.13
  19.4 4.3 copy-start.2
  49.3 4.5 copy-start.18
  49.3 4.5 copy-start.1
  84.8 226.4 %all-to-all-start = ((bf16[96,32,1000]{2,0,1:T(8,128)(2,1)}), bf16[96,32,1000]{2,0,1:T(8,128)(2,1)}, u32[]{:S(2)}, u32[]{:S(2)}) async-start(bf16[96,32,1000]{2,0,1:T(8,128)(2,1)} %copy.62), calls=%async_computation | async-start | bytes 12582912 | tf_op jit(solution)/shard_map/all_to_all | solution.py:52
  101.3 6.5 %copy-start.16 = (f32[3,10,10]{2,0,1:T(4,128)S(1)}, f32[3,10,10]{2,0,1:T(4,128)}, u32[]{:S(2)}) copy-start(f32[3,10,10]{2,0,1:T(4,128)} %param.19) | copy-start | bytes 3604
  101.3 6.6 %copy-start.14 = (f32[10,10]{1,0:T(8,128)S(1)}, f32[10,10]{1,0:T(8,128)}, u32[]{:S(2)}) copy-start(f32[10,10]{1,0:T(8,128)} %param.18) | copy-start | bytes 1204
  101.3 7.0 %copy-start.15 = (f32[8,1000]{1,0:T(8,128)S(1)}, f32[8,1000]{1,0:T(8,128)}, u32[]{:S(2)}) copy-start(f32[8,1000]{1,0:T(8,128)} %param.15) | copy-start | bytes 96004
  137.8 5.0 copy-start.12
  153.1 5.2 copy-start.17
  158.3 2.2 copy-start.3
  380.5 4.0 copy-start.10
  389.6 5.1 copy-start.9
  389.7 5.1 copy-start.11
  398.3 5.5 %copy-start.8 = (bf16[7680,100]{1,0:T(8,128)(2,1)S(1)}, bf16[7680,100]{1,0:T(8,128)(2,1)}, u32[]{:S(2)}) copy-start(bf16[7680,100]{1,0:T(8,128)(2,1)} %reshape.313) | copy-start | bytes 4608004
  407.4 5.2 copy-start.7
  416.1 5.1 copy-start.5
  421.3 2.1 copy-start.6
  500.5 5.4 %copy-start.4 = (f32[96,8,1000]{2,1,0:T(8,128)S(1)}, f32[96,8,1000]{2,1,0:T(8,128)}, u32[]{:S(2)}) copy-start(f32[96,8,1000]{2,1,0:T(8,128)} %reshape.312) | copy-start | bytes 9216004
Sparse Core Ops, SparseCore 0:
  53.9 265.6 all-gather.1
where the time goes:
time: 535 us; the launch traced here: 524 us
  local copies, waits for them, and re-layouts  245 us (46%)
  waiting for transfers between devices  146 us (27%)
  matrix products  72.2 us (13%)
  other arithmetic  33.8 us (6%)
  between operations  14.7 us (3%)
  starting transfers between devices  12.6 us (2%)
    all_to_all x1, waiting for transfers between devices, shards(): lax.all_to_all(outgoing, 'box', split_axis=1, concat_axis=1, tiled=True)  146 us
    reshape x6, local copies, waits for them, and re-layouts, along_axis(): return result.reshape(flat.shape)  31.1 us
    reshape x6, local copies, waits for them, and re-layouts, along_axis(): shaped = flat.reshape(-1, order_k, width // order_k)  29.9 us
    dot_general x5, matrix products, along_axis(): jnp.einsum('ax,nxr->nar', matrix, shaped, precision=lax.Precision.HIGHEST)  27.1 us
    dot_general x6, matrix products, along_axis(): jnp.dot(flat.reshape(-1, inner), square.T, precision=lax.Precision.HIGHEST)  26 us
    gather x6, local copies, waits for them, and re-layouts, shards(): moved = jnp.take(pool, jnp.maximum(face_pos, 0), axis=1)  23.3 us
    gather x1, local copies, waits for them, and re-layouts, shards(): picked = jnp.take(orbitals, jnp.maximum(slots, 0), axis=1)  21.3 us
    reshape x5, local copies, waits for them, and re-layouts, along_axis(): flat.reshape(-1, inner)  19.3 us
  transfers between devices with their start and end apart: 2, of which 1 were waited for; matrix products, arithmetic and copies ran while one was open for 44% of the time, Pallas kernels for 0%

commit v1 on v0

v1 whole, which is shorter than its diff:
```python
import jax
import jax.numpy as jnp
from jax import lax
from jax.sharding import PartitionSpec as P

KEEP = 4


def digit_of(width, order_k, place):
    idx = lax.iota(jnp.int32, width)
    return (idx // (order_k ** (2 - place))) % order_k


def expand(mat, width, place):
    order_k = mat.shape[0]
    digit = digit_of(width, order_k, place)
    ks = lax.iota(jnp.int32, order_k)
    left = (digit[:, None] == ks[None, :]).astype(jnp.float32)
    right = (ks[:, None] == digit[None, :]).astype(jnp.float32)
    hp = lax.Precision.HIGHEST
    return jnp.dot(jnp.dot(left, mat, precision=hp), right, precision=hp)


def same_digit(width, order_k, place):
    digit = digit_of(width, order_k, place)
    return (digit[:, None] == digit[None, :]).astype(jnp.float32)


def kron3(a, b, c):
    width = a.shape[0] * b.shape[0] * c.shape[0]
    return expand(a, width, 0) * expand(b, width, 1) * expand(c, width, 2)


def at_place(mat, width, place):
    order_k = mat.shape[0]
    out = expand(mat, width, place)
    for other in range(3):
        if other != place:
            out = out * same_digit(width, order_k, other)
    return out


def split_bf16(mat):
    hi = lax.reduce_precision(mat, exponent_bits=8, mantissa_bits=7)
    lo = (mat - hi).astype(jnp.bfloat16)
    return hi.astype(jnp.bfloat16), lo


def dot_f32(a, b):
    return jnp.dot(a, b, preferred_element_type=jnp.float32)


def apply_bf16(rows, parts):
    hi, lo = parts
    return dot_f32(rows, hi) + dot_f32(rows, lo)


def apply_f32(rows, parts):
    hi, lo = parts
    rows_hi_f = lax.reduce_precision(rows, exponent_bits=8, mantissa_bits=7)
    rows_lo = (rows - rows_hi_f).astype(jnp.bfloat16)
    rows_hi = rows_hi_f.astype(jnp.bfloat16)
    return dot_f32(rows_hi, hi) + dot_f32(rows_hi, lo) + dot_f32(rows_lo, hi)


def pick(onehot, block):
    return jnp.einsum(
        "sb,nbc->nsc", onehot, block, preferred_element_type=jnp.float32
    ).astype(jnp.bfloat16)


def shards(
    orbitals,
    exchange_values,
    local_values,
    coupling,
    to_values_mat,
    to_coeffs_mat,
    laplace_blocks,
    box_counts,
    kept_mask,
    send_list,
    neighbour_pos,
):
    orb_dev, box_dev, width = orbitals.shape
    order_k = to_values_mat.shape[0]
    n_box = send_list.shape[1]
    rows = orb_dev * box_dev

    slots = send_list[0]
    box_ids = lax.iota(jnp.int32, box_dev)
    send_hot = (slots[:, None] == box_ids[None, :]).astype(jnp.bfloat16)
    outgoing = pick(send_hot, orbitals)
    incoming = lax.all_to_all(outgoing, "box", split_axis=1, concat_axis=1, tiled=True)

    values_t = split_bf16(kron3(to_values_mat, to_values_mat, to_values_mat).T)
    flat = orbitals.reshape(rows, width)
    values = apply_bf16(flat, values_t).reshape(orb_dev, box_dev, width)

    kept = kept_mask > 0
    rank = jnp.cumsum(kept.astype(jnp.int32)) - 1
    keep_ids = lax.iota(jnp.int32, KEEP)
    sel = kept[None, :] & (rank[None, :] == keep_ids[:, None])
    products = jnp.where(
        kept[None, :, None], exchange_values.astype(jnp.float32) * values, 0.0
    ).astype(jnp.bfloat16)
    compact = pick(sel.astype(jnp.bfloat16), products)
    gathered = lax.all_gather(
        compact.reshape(orb_dev, KEEP * width), "orb", axis=0, tiled=True
    )
    mixed = dot_f32(coupling, gathered).reshape(orb_dev, KEEP, width)
    self_f = sel.astype(jnp.float32)
    exchange = mixed[:, 0:1, :] * self_f[0][None, :, None]
    for k in range(1, KEEP):
        exchange = exchange + mixed[:, k : k + 1, :] * self_f[k][None, :, None]

    weighted = local_values[None, :, :] * values - exchange
    coeffs_t = split_bf16(kron3(to_coeffs_mat, to_coeffs_mat, to_coeffs_mat).T)
    potential = apply_f32(weighted.reshape(rows, width), coeffs_t)

    lap0 = laplace_blocks[0]
    centre = sum(at_place(lap0, width, place) for place in range(3))
    kinetic = apply_bf16(flat, split_bf16(centre.T))
    remote_ids = lax.iota(jnp.int32, n_box)
    for which in range(3):
        for side in range(2):
            face_pos = neighbour_pos[2 * which + side]
            local_hot = (face_pos[:, None] == box_ids[None, :]).astype(jnp.bfloat16)
            remote_hot = ((face_pos[:, None] - box_dev) == remote_ids[None, :]).astype(
                jnp.bfloat16
            )
            moved = pick(local_hot, orbitals) + pick(remote_hot, incoming)
            face_mat = at_place(laplace_blocks[1 + side], width, which)
            kinetic = kinetic + apply_bf16(
                moved.reshape(rows, width), split_bf16(face_mat.T)
            )

    total = (potential - 0.5 * kinetic).reshape(orb_dev, box_dev, width)
    live = box_ids < box_counts[0]
    total = jnp.where(live[None, :, None], total, 0.0)
    return total.astype(jnp.bfloat16)


def solution(mesh):
    return jax.shard_map(
        shards,
        mesh=mesh,
        in_specs=(
            P("orb", "box", None),
            P("orb", "box", None),
            P("box", None),
            P("orb", None),
            P(),
            P(),
            P(),
            P("box"),
            P("box"),
            P("box", None),
            P(None, "box"),
        ),
        out_specs=P("orb", "box", None),
        check_vma=False,
    )
```

time: 535 us -> 411 us (0.77)
  the two profiles are of different devices: /device:TPU:64 before, /device:TPU:66 now
where the time goes in v1:
time: 411 us; the launch traced here: 403 us
  matrix products  190 us (46%)
  waiting for transfers between devices  118 us (29%)
  local copies, waits for them, and re-layouts  56.1 us (14%)
  between operations  14.9 us (4%)
  starting transfers between devices  12.6 us (3%)
  other arithmetic  10.9 us (3%)
    all_gather x1, waiting for transfers between devices, shards(): lax.all_gather(compact.reshape(orb_dev, KEEP * width), 'orb', axis=0, til...  118 us
    dot_general x20, matrix products, dot_f32(): return jnp.dot(a, b, preferred_element_type=jnp.float32)  89.9 us
    dot_general x30, matrix products, expand(): return jnp.dot(jnp.dot(left, mat, precision=hp), right, precision=hp)  53.4 us
    dot_general x14, matrix products, pick(): jnp.einsum('sb,nbc->nsc', onehot, block, preferred_element_type=jnp.float32)  47.2 us
    mul x12, local copies, waits for them, and re-layouts, shards(): exchange = exchange + mixed[:, k:k + 1, :] * self_f[k][None, :, None]  17.1 us
    all_to_all x1, starting transfers between devices, shards(): lax.all_to_all(outgoing, 'box', split_axis=1, concat_axis=1, tiled=True)  12.6 us
    unnamed x40, local copies, waits for them, and re-layouts  9.54 us
  transfers between devices with their start and end apart: 2, of which 1 were waited for; matrix products, arithmetic and copies ran while one was open for 28% of the time, Pallas kernels for 0%

profile of v1, /device:TPU:66, one launch (start us, length us, event | category | flops | bytes accessed | tf_op | source)
XLA Modules:
  0.0 403.2 jit_solution(18097941252706797543)
XLA Ops:
  33.7 6.2 %copy.39 = bf16[96,32,1000]{2,0,1:T(8,128)(2,1)} copy(bf16[96,32,1000]{2,1,0:T(8,128)(2,1)S(1)} %convert_bitcast_fusion) | data formatting | bytes 12288000 | tf_op jit(solution)/shard_map/convert_element_type | solution.py:69
  39.9 12.6 %all-to-all-start = ((bf16[96,32,1000]{2,0,1:T(8,128)(2,1)}), bf16[96,32,1000]{2,0,1:T(8,128)(2,1)}, u32[]{:S(2)}, u32[]{:S(2)}) async-start(bf16[96,32,1000]{2,0,1:T(8,128)(2,1)} %copy.39), calls=%async_computation | async-start | bytes 12582912 | tf_op jit(solution)/shard_map/all_to_all | solution.py:94
  57.3 3.8 copy.32
  66.1 3.8 fusion.203
  70.0 3.8 fusion.196
  73.8 3.8 fusion.198
  77.6 3.7 fusion.204
  85.1 4.2 %fusion.199 = f32[1000,1000]{1,0:T(8,128)} fusion(f32[1000,10]{0,1:T(8,128)S(1)} %fusion.172, s32[1000]{0:T(1024)S(1)} %get-tuple-element.30), kind=kOutput, calls=%fused_computation.245 | convolution fusion | flops 120010000 | bytes 4044000 | tf_op jit(solution)/shard_map/dot_general | solution.py:21
  99.9 3.9 fusion.53
  103.8 4.2 %multiply_multiply_fusion = f32[1000,1000]{1,0:T(8,128)} fusion(f32[1000,1000]{1,0:T(8,128)S(1)} %fusion.206, f32[1000,1000]{1,0:T(8,128)S(1)} %fusion.201, f32[1000,10]{0,1:T(8,128)S(1)} %fusion.169, s32[1000]{0:T(1024)S(1)} %add_select_fusion), kind=kOutput, calls=%fused_computation.51 | convolution fusion | flops 122010000 | bytes 12044000 | tf_op jit(solution)/shard_map/dot_general | solution.py:21
  111.6 118.3 %all-gather.2.cloned.1.call-done = bf16[768,4000]{1,0:T(8,128)(2,1)} async-done(((bf16[96,4000]{1,0:T(8,128)(2,1)}), bf16[768,4000]{1,0:T(8,128)(2,1)}) %all-gather.2.cloned.1.call-update) | async-done | bytes 6144016 | tf_op jit(solution)/shard_map/all_gather | solution.py:108
  229.9 5.1 %convolution_bitcast_fusion = f32[96,4000]{1,0:T(8,128)} fusion(bf16[96,768]{1,0:T(8,128)(2,1)S(1)} %copy-done.11, bf16[768,4000]{1,0:T(8,128)(2,1)} %all-gather.2.cloned.1.call-done), kind=kOutput, calls=%fused_computation.37 | convolution fusion | flops 589824000 | bytes 7827456 | tf_op jit(solution)/shard_map/dot_general | solution.py:50
  258.1 3.7 copy.34
  261.9 7.7 %add_subtract_fusion = f32[768,1000]{0,1:T(8,128)S(1)} fusion(f32[768,1000]{0,1:T(8,128)} %copy.37, f32[768,1000]{0,1:T(8,128)} %copy.36, f32[768,1000]{0,1:T(8,128)} %copy.35, f32[768,1000]{0,1:T(8,128)} %copy.34, f32[768,1000]{0,1:T(8,128)} %copy.32, f32[768,1000]{0,1:T(8,128)} %add_bitcast_fusion, f32[768]{0:T(1024)S(1)} %mul.221, f32[768]{0:T(1024)S(1)} %mul.213, ...), kind=kLoop, calls=%fused_computation.67 | loop fusion | flops 6912000 | bytes 21516288 | tf_op jit(solution)/shard_map/sub | solution.py:117
  276.6 6.3 %fusion.135 = bf16[96,1000,8]{1,2,0:T(8,128)(2,1)S(1)} fusion(bf16[96,32,1000]{2,0,1:T(8,128)(2,1)} %all-to-all-done, s32[8]{0:T(128)S(1)} %get-tuple-element.19), kind=kOutput, calls=%fused_computation.163 | convolution fusion | flops 49920256 | bytes 7680032 | tf_op jit(solution)/shard_map/sb,nbc->nsc/dot_general | solution.py:67
  285.1 3.9 fusion.34
  288.9 4.1 %fusion.59 = f32[768,1000]{0,1:T(8,128)} fusion(f32[1000,1000]{1,0:T(8,128)S(1)} %copy-done.10, s32[1000]{0:T(1024)S(1)} %get-tuple-element.31, s32[1000]{0:T(1024)S(1)} %get-tuple-element.30, bf16[96,8,1000]{2,1,0:T(8,128)(2,1)S(1)} %bitcast_add_fusion.1), kind=kOutput, calls=%fused_computation.97 | convolution fusion | flops 1542000000 | bytes 8616000 | tf_op jit(solution)/shard_map/dot_general | solution.py:50
  293.1 6.3 %fusion.120 = bf16[96,1000,8]{1,2,0:T(8,128)(2,1)S(1)} fusion(bf16[96,32,1000]{2,0,1:T(8,128)(2,1)} %all-to-all-done, s32[8]{0:T(128)S(1)} %get-tuple-element.18), kind=kOutput, calls=%fused_computation.158 | convolution fusion | flops 49920256 | bytes 7680032 | tf_op jit(solution)/shard_map/sb,nbc->nsc/dot_general | solution.py:67
  301.5 3.8 fusion.44
  305.3 3.8 fusion.54
  309.2 6.5 %fusion.132 = bf16[96,1000,8]{1,2,0:T(8,128)(2,1)S(1)} fusion(bf16[96,32,1000]{2,0,1:T(8,128)(2,1)} %all-to-all-done, s32[8]{0:T(128)S(1)} %get-tuple-element.20), kind=kOutput, calls=%fused_computation.162 | convolution fusion | flops 49920256 | bytes 7680032 | tf_op jit(solution)/shard_map/sb,nbc->nsc/dot_general | solution.py:67
  317.8 3.9 fusion.36
  321.7 3.8 fusion.58
  325.5 6.3 %fusion.129 = bf16[96,1000,8]{1,2,0:T(8,128)(2,1)S(1)} fusion(bf16[96,32,1000]{2,0,1:T(8,128)(2,1)} %all-to-all-done, s32[8]{0:T(128)S(1)} %get-tuple-element.21), kind=kOutput, calls=%fused_computation.161 | convolution fusion | flops 49920256 | bytes 7680032 | tf_op jit(solution)/shard_map/sb,nbc->nsc/dot_general | solution.py:67
  334.0 4.0 %fusion.38 = f32[768,1000]{0,1:T(8,128)} fusion(f32[1000,1000]{1,0:T(8,128)S(1)} %copy-done.7, s32[1000]{0:T(1024)S(1)} %get-tuple-element.31, s32[1000]{0:T(1024)S(1)} %add_select_fusion, bf16[96,8,1000]{2,1,0:T(8,128)(2,1)S(1)} %bitcast_add_fusion.3), kind=kOutput, calls=%fused_computation.83 | convolution fusion | flops 1543000064 | bytes 8616000 | tf_op jit(solution)/shard_map/dot_general | solution.py:50
  338.0 3.9 fusion.57
  341.9 6.3 %fusion.126 = bf16[96,1000,8]{1,2,0:T(8,128)(2,1)S(1)} fusion(bf16[96,32,1000]{2,0,1:T(8,128)(2,1)} %all-to-all-done, s32[8]{0:T(128)S(1)} %get-tuple-element.22), kind=kOutput, calls=%fused_computation.160 | convolution fusion | flops 49920256 | bytes 7680032 | tf_op jit(solution)/shard_map/sb,nbc->nsc/dot_general | solution.py:67
  350.3 3.8 fusion.40
  357.9 6.6 %fusion.123 = bf16[96,1000,8]{1,2,0:T(8,128)(2,1)S(1)} fusion(bf16[96,32,1000]{2,0,1:T(8,128)(2,1)} %all-to-all-done, s32[8]{0:T(128)S(1)} %get-tuple-element.23), kind=kOutput, calls=%fused_computation.159 | convolution fusion | flops 49920256 | bytes 7680032 | tf_op jit(solution)/shard_map/sb,nbc->nsc/dot_general | solution.py:67
  366.6 3.9 fusion.42
  370.5 3.7 fusion.55
  374.3 18.2 %fusion.21 = bf16[768,1000]{0,1:T(8,128)(2,1)} fusion(f32[768,1000]{0,1:T(8,128)} %fusion.59, f32[768,1000]{0,1:T(8,128)} %fusion.34, f32[768,1000]{0,1:T(8,128)} %fusion.58, f32[768,1000]{0,1:T(8,128)} %fusion.36, f32[768,1000]{0,1:T(8,128)} %fusion.57, f32[768,1000]{0,1:T(8,128)} %fusion.38, f32[768,1000]{0,1:T(8,128)} %fusion.56, ...), kind=kOutput, calls=%fused_computation.66 | convolution fusion | flops 1554128000 | bytes 57760000 | tf_op jit(solution)/shard_map/dot_general | solution.py:50
  (114 shorter events, 104.2 us)
Async XLA Ops:
  6.5 10.5 %copy-start = (bf16[96,8,1000]{2,1,0:T(8,128)(2,1)S(1)}, bf16[96,8,1000]{2,1,0:T(8,128)(2,1)}, u32[]{:S(2)}) copy-start(bf16[96,8,1000]{2,1,0:T(8,128)(2,1)} %param.11) | copy-start | bytes 4608004
  6.5 223.4 %all-gather.2.cloned.1.call-start = ((), (), s32[]{:S(2)}) async-start(), calls=%async_computation.1 | async-start | bytes 7077888 | tf_op jit(solution)/shard_map/all_gather | solution.py:108
  26.3 5.3 %copy-start.15 = (s32[1,32]{1,0:T(1,128)S(1)}, s32[1,32]{1,0:T(1,128)}, u32[]{:S(2)}) copy-start(s32[1,32]{1,0:T(1,128)} %param.20) | copy-start | bytes 388
  39.9 13.3 %copy-start.14 = (s32[6,8]{1,0:T(8,128)S(1)}, s32[6,8]{1,0:T(8,128)}, u32[]{:S(2)}) copy-start(s32[6,8]{1,0:T(8,128)} %param.21) | copy-start | bytes 580
  39.9 13.4 %copy-start.13 = (f32[3,10,10]{2,0,1:T(4,128)S(1)}, f32[3,10,10]{2,0,1:T(4,128)}, u32[]{:S(2)}) copy-start(f32[3,10,10]{2,0,1:T(4,128)} %param.17) | copy-start | bytes 3604
  39.9 14.4 %copy-start.12 = (f32[8,1000]{1,0:T(8,128)S(1)}, f32[8,1000]{1,0:T(8,128)}, u32[]{:S(2)}) copy-start(f32[8,1000]{1,0:T(8,128)} %param.13) | copy-start | bytes 96004
  39.9 236.7 %all-to-all-start = ((bf16[96,32,1000]{2,0,1:T(8,128)(2,1)}), bf16[96,32,1000]{2,0,1:T(8,128)(2,1)}, u32[]{:S(2)}, u32[]{:S(2)}) async-start(bf16[96,32,1000]{2,0,1:T(8,128)(2,1)} %copy.39), calls=%async_computation | async-start | bytes 12582912 | tf_op jit(solution)/shard_map/all_to_all | solution.py:94
  57.3 7.4 %copy-start.17 = (f32[10,10]{1,0:T(8,128)S(1)}, f32[10,10]{1,0:T(8,128)}, u32[]{:S(2)}) copy-start(f32[10,10]{1,0:T(8,128)} %param.16) | copy-start | bytes 1204
  108.0 121.9 %copy-start.11 = (bf16[96,768]{1,0:T(8,128)(2,1)S(1)}, bf16[96,768]{1,0:T(8,128)(2,1)}, u32[]{:S(2)}) copy-start(bf16[96,768]{1,0:T(8,128)(2,1)} %param.14) | copy-start | bytes 442372
  261.9 7.7 %copy-start.1 = (f32[1000,1000]{1,0:T(8,128)S(1)}, f32[1000,1000]{1,0:T(8,128)}, u32[]{:S(2)}) copy-start(f32[1000,1000]{1,0:T(8,128)} %multiply_multiply_fusion) | copy-start | bytes 12000004
  269.6 3.5 copy-start.3
  282.9 2.2 copy-start.10
  299.4 2.2 copy-start.9
  315.6 2.2 copy-start.8
  331.8 2.2 copy-start.7
  348.2 2.2 copy-start.6
  364.5 2.2 copy-start.5
  370.5 3.7 copy-start.2
  370.5 3.8 copy-start.4
  392.5 1.7 copy-start.16
Sparse Core Ops, SparseCore 0:
  31.7 198.1 all-gather.1

commit v2 on v1

--- a/solution.py
+++ b/solution.py
@@ -108,32 +108,29 @@
     gathered = lax.all_gather(
         compact.reshape(orb_dev, KEEP * width), "orb", axis=0, tiled=True
     )
+    lap0 = laplace_blocks[0]
+    centre = sum(at_place(lap0, width, place) for place in range(3))
+    kinetic = apply_bf16(flat, split_bf16(centre.T))
+    faces = [at_place(laplace_blocks[1 + side], width, which).T
+             for which in range(3) for side in range(2)]
+    face_hi, face_lo = split_bf16(jnp.stack(faces))
+    pool = jnp.concatenate([orbitals, incoming], axis=1)
+    pool_ids = lax.iota(jnp.int32, pool.shape[1])
+    face_pos = neighbour_pos.reshape(-1)
+    face_hot = (face_pos[:, None] == pool_ids[None, :]).astype(jnp.bfloat16)
+    moved = pick(face_hot, pool).reshape(orb_dev, len(faces), box_dev, width)
+    kinetic_faces = jnp.einsum(
+        "nfbc,fcd->nbd", moved, face_hi, preferred_element_type=jnp.float32
+    ) + jnp.einsum("nfbc,fcd->nbd", moved, face_lo, preferred_element_type=jnp.float32)
+    kinetic = kinetic + kinetic_faces.reshape(rows, width)
+    gathered, kinetic = lax.optimization_barrier((gathered, kinetic))
     mixed = dot_f32(coupling, gathered).reshape(orb_dev, KEEP, width)
-    self_f = sel.astype(jnp.float32)
-    exchange = mixed[:, 0:1, :] * self_f[0][None, :, None]
-    for k in range(1, KEEP):
-        exchange = exchange + mixed[:, k : k + 1, :] * self_f[k][None, :, None]
+    spread = jnp.take(mixed, jnp.clip(rank, 0, KEEP - 1), axis=1)
+    exchange = jnp.where(kept[None, :, None], spread, 0.0)
 
     weighted = local_values[None, :, :] * values - exchange
     coeffs_t = split_bf16(kron3(to_coeffs_mat, to_coeffs_mat, to_coeffs_mat).T)
     potential = apply_f32(weighted.reshape(rows, width), coeffs_t)
-
-    lap0 = laplace_blocks[0]
-    centre = sum(at_place(lap0, width, place) for place in range(3))
-    kinetic = apply_bf16(flat, split_bf16(centre.T))
-    remote_ids = lax.iota(jnp.int32, n_box)
-    for which in range(3):
-        for side in range(2):
-            face_pos = neighbour_pos[2 * which + side]
-            local_hot = (face_pos[:, None] == box_ids[None, :]).astype(jnp.bfloat16)
-            remote_hot = ((face_pos[:, None] - box_dev) == remote_ids[None, :]).astype(
-                jnp.bfloat16
-            )
-            moved = pick(local_hot, orbitals) + pick(remote_hot, incoming)
-            face_mat = at_place(laplace_blocks[1 + side], width, which)
-            kinetic = kinetic + apply_bf16(
-                moved.reshape(rows, width), split_bf16(face_mat.T)
-            )
 
     total = (potential - 0.5 * kinetic).reshape(orb_dev, box_dev, width)
     live = box_ids < box_counts[0]

time: 411 us -> 349 us (0.85)
  the two profiles are of different devices: /device:TPU:66 before, /device:TPU:64 now
where the time goes in v2:
time: 349 us; the launch traced here: 345 us
  waiting for transfers between devices  137 us (39%)
  matrix products  122 us (35%)
  local copies, waits for them, and re-layouts  51 us (15%)
  between operations  14.7 us (4%)
  starting transfers between devices  12.7 us (4%)
  other arithmetic  6.35 us (2%)
    all_to_all x1, waiting for transfers between devices, shards(): lax.all_to_all(outgoing, 'box', split_axis=1, concat_axis=1, tiled=True)  137 us
    dot_general x30, matrix products, expand(): return jnp.dot(jnp.dot(left, mat, precision=hp), right, precision=hp)  45.8 us
    dot_general x8, matrix products, dot_f32(): return jnp.dot(a, b, preferred_element_type=jnp.float32)  27.3 us
    dot_general x1, matrix products, shards(): jnp.einsum('nfbc,fcd->nbd', moved, face_hi, preferred_element_type=jnp.fl...  19.1 us
    dot_general x1, matrix products, shards(): jnp.einsum('nfbc,fcd->nbd', moved, face_lo, preferred_element_type=jnp.fl...  18.5 us
    all_to_all x1, starting transfers between devices, shards(): lax.all_to_all(outgoing, 'box', split_axis=1, concat_axis=1, tiled=True)  12.4 us
    dot_general x3, matrix products, pick(): jnp.einsum('sb,nbc->nsc', onehot, block, preferred_element_type=jnp.float32)  11.7 us
    gather x3, local copies, waits for them, and re-layouts, shards(): spread = jnp.take(mixed, jnp.clip(rank, 0, KEEP - 1), axis=1)  11.6 us
  transfers between devices with their start and end apart: 2, of which 1 were waited for; matrix products, arithmetic and copies ran while one was open for 38% of the time, Pallas kernels for 0%

profile of v2, /device:TPU:64, one launch (start us, length us, event | category | flops | bytes accessed | tf_op | source)
XLA Modules:
  0.0 344.5 jit_solution(1964728319889122130)
XLA Ops:
  6.5 3.3 convert_bitcast_fusion
  9.8 6.2 %copy.32 = bf16[96,32,1000]{2,0,1:T(8,128)(2,1)} copy(bf16[96,32,1000]{2,1,0:T(8,128)(2,1)S(1)} %convert_bitcast_fusion) | data formatting | bytes 12288000 | tf_op jit(solution)/shard_map/convert_element_type | solution.py:69
  16.0 12.4 %all-to-all-start = ((bf16[96,32,1000]{2,0,1:T(8,128)(2,1)}), bf16[96,32,1000]{2,0,1:T(8,128)(2,1)}, u32[]{:S(2)}, u32[]{:S(2)}) async-start(bf16[96,32,1000]{2,0,1:T(8,128)(2,1)} %copy.32), calls=%async_computation | async-start | bytes 12582912 | tf_op jit(solution)/shard_map/all_to_all | solution.py:94
  34.0 2.2 multiply_multiply_fusion.1
  38.2 3.6 %add_bitcast_fusion = f32[768,1000]{0,1:T(8,128)} fusion(f32[1000,768]{1,0:T(8,128)S(1)} %fusion.42, f32[1000,1000]{1,0:T(8,128)S(1)} %multiply_multiply_fusion.1, bf16[96,8,1000]{2,1,0:T(8,128)(2,1)S(1)} %copy-done.2), kind=kOutput, calls=%fused_computation.74 | convolution fusion | flops 1538768000 | bytes 11680000 | tf_op jit(solution)/shard_map/dot_general | solution.py:50
  41.8 4.0 %copy.30 = f32[768,1000]{1,0:T(8,128)} copy(f32[768,1000]{0,1:T(8,128)} %add_bitcast_fusion) | data formatting | bytes 6144000 | tf_op jit(solution)/shard_map/add | solution.py:55
  46.1 3.1 fusion.64
  59.6 3.8 %fusion.99 = f32[1000,1000]{1,0:T(8,128)} fusion(f32[1000,10]{0,1:T(8,128)S(1)} %fusion.76, s32[1000]{0:T(1024)S(1)} %get-tuple-element.17), kind=kOutput, calls=%fused_computation.127 | convolution fusion | flops 120010000 | bytes 4044000 | tf_op jit(solution)/shard_map/dot_general | solution.py:21
  63.4 3.8 %fusion.102 = f32[1000,1000]{1,0:T(8,128)} fusion(f32[1000,10]{0,1:T(8,128)S(1)} %fusion.81, s32[1000]{0:T(1024)S(1)} %add_select_fusion.3), kind=kOutput, calls=%fused_computation.131 | convolution fusion | flops 120010000 | bytes 4044000 | tf_op jit(solution)/shard_map/dot_general | solution.py:21
  67.6 3.7 %copy.29 = f32[768,1000]{0,1:T(8,128)} copy(f32[768,1000]{1,0:T(8,128)} %broadcast_bitcast_fusion) | data formatting | bytes 6144000 | tf_op jit(solution)/shard_map/mul | solution.py:131
  75.5 2.2 fusion.22
  77.7 2.2 fusion.24
  79.9 2.2 fusion.26
  84.3 2.6 fusion.30
  86.9 2.2 fusion.32
  89.1 4.2 %multiply_multiply_fusion = f32[1000,1000]{1,0:T(8,128)} fusion(f32[1000,1000]{1,0:T(8,128)S(1)} %fusion.101, f32[1000,1000]{1,0:T(8,128)S(1)} %fusion.98, f32[1000,10]{0,1:T(8,128)S(1)} %fusion.68, s32[1000]{0:T(1024)S(1)} %get-tuple-element.16), kind=kOutput, calls=%fused_computation.60 | convolution fusion | flops 122010000 | bytes 12044000 | tf_op jit(solution)/shard_map/dot_general | solution.py:21
  94.3 4.1 %copy-done.6 = f32[1000,1000]{1,0:T(8,128)S(1)} copy-done((f32[1000,1000]{1,0:T(8,128)S(1)}, f32[1000,1000]{1,0:T(8,128)}, u32[]{:S(2)}) %copy-start.6) | copy-done | bytes 4000024
  98.4 3.4 fusion.20
  103.8 3.6 %fusion.40 = f32[1000,768]{1,0:T(8,128)} fusion(f32[1000,1000]{1,0:T(8,128)S(1)} %fusion.20, bf16[96,8,1000]{2,1,0:T(8,128)(2,1)S(1)} %copy-done.2), kind=kOutput, calls=%fused_computation.76 | convolution fusion | flops 1539000064 | bytes 8608000 | tf_op jit(solution)/shard_map/dot_general | solution.py:50
  107.4 137.3 %all-to-all-done = bf16[96,32,1000]{2,0,1:T(8,128)(2,1)} async-done(((bf16[96,32,1000]{2,0,1:T(8,128)(2,1)}), bf16[96,32,1000]{2,0,1:T(8,128)(2,1)}, u32[]{:S(2)}, u32[]{:S(2)}) %all-to-all-start) | async-done | bytes 6144032 | tf_op jit(solution)/shard_map/all_to_all | solution.py:94
  244.7 6.5 %copy.33 = bf16[96,32,1000]{2,1,0:T(8,128)(2,1)S(1)} copy(bf16[96,32,1000]{2,0,1:T(8,128)(2,1)} %all-to-all-done) | data formatting | bytes 12288000 | tf_op jit(solution)/shard_map/all_to_all | solution.py:94
  251.2 5.4 %fusion.13 = bf16[96,1000,48]{1,2,0:T(8,128)(2,1)} fusion(bf16[96,32,1000]{2,1,0:T(8,128)(2,1)S(1)} %copy.33, bf16[96,8,1000]{2,1,0:T(8,128)(2,1)S(1)} %copy-done.2, s32[48]{0:T(128)S(1)} %eq.750), kind=kOutput, calls=%fused_computation.32 | convolution fusion | flops 388609920 | bytes 16896192 | tf_op jit(solution)/shard_map/sb,nbc->nsc/dot_general | solution.py:67
  256.6 18.5 %fusion.2 = f32[96,8,1000,1]{2,1,3,0:T(8,128)} fusion(f32[6,1000,1000]{2,1,0:T(8,128)} %copy-done.13, bf16[96,1000,48]{1,2,0:T(8,128)(2,1)} %fusion.13), kind=kOutput, calls=%fused_computation.5 | convolution fusion | flops 9233999872 | bytes 36288000 | tf_op jit(solution)/shard_map/nfbc,fcd->nbd/dot_general | solution.py:124
  275.1 19.1 %fusion.34 = f32[768,1000]{1,0:T(8,128)} fusion(f32[96,8,1000,1]{2,1,3,0:T(8,128)} %fusion.2, f32[6,1000,1000]{2,1,0:T(8,128)} %copy-done.13, bf16[96,1000,48]{1,2,0:T(8,128)(2,1)} %fusion.13), kind=kOutput, calls=%fused_computation.65 | convolution fusion | flops 9228768256 | bytes 39360000 | tf_op jit(solution)/shard_map/nfbc,fcd->nbd/dot_general | solution.py:122
  294.2 3.8 %copy.36 = f32[768,1000]{0,1:T(8,128)} copy(f32[768,1000]{1,0:T(8,128)} %fusion.34) | data formatting | bytes 6144000 | tf_op jit(solution)/shard_map/reshape | solution.py:125
  298.0 7.5 %bitcast_add_fusion.1 = f32[768,1000]{0,1:T(8,128)} fusion(f32[768,1000]{0,1:T(8,128)} %copy.36, f32[1000,768]{1,0:T(8,128)} %fusion.40, bf16[96,8,1000]{2,1,0:T(8,128)(2,1)S(1)} %copy-done.2, f32[1000,1000]{1,0:T(8,128)} %copy-done.4), kind=kOutput, calls=%fused_computation.71 | convolution fusion | flops 1539536000 | bytes 14752000 | tf_op jit(solution)/shard_map/dot_general | solution.py:50
  305.6 3.9 %convolution_bitcast_fusion = f32[96,4000]{1,0:T(8,128)S(1)} fusion(bf16[96,768]{1,0:T(8,128)(2,1)S(1)} %copy-done, bf16[768,4000]{1,0:T(8,128)(2,1)} %all-gather.2.cloned.1.call-done), kind=kOutput, calls=%fused_computation.40 | convolution fusion | flops 589824000 | bytes 7827456 | tf_op jit(solution)/shard_map/dot_general | solution.py:50
  311.9 2.4 gather_fusion
  314.4 5.4 %copy.59 = f32[96,8,1000]{2,1,0:T(8,128)} copy(f32[96,8,1000]{2,0,1:T(8,128)} %bitcast.152) | data formatting | bytes 6144000 | tf_op jit(solution)/shard_map/jit(_take)/gather | solution.py:128
  319.7 3.8 %copy.39 = f32[768,1000]{0,1:T(8,128)} copy(f32[768,1000]{1,0:T(8,128)} %bitcast.153) | data formatting | bytes 6144000 | tf_op jit(solution)/shard_map/jit(_take)/gather | solution.py:128
  323.5 4.4 %select_subtract_fusion = f32[768,1000]{0,1:T(8,128)S(1)} fusion(f32[768,1000]{0,1:T(8,128)} %copy.39, f32[768,1000]{0,1:T(8,128)} %copy.29, f32[768,1000]{0,1:T(8,128)} %add_bitcast_fusion, pred[768]{0:T(1024)(128)(4,1)S(1)} %broadcast_in_dim.46, pred[768]{0:T(1024)(128)(4,1)S(1)} %broadcast_in_dim.43), kind=kLoop, calls=%fused_computation.73 | loop fusion | flops 3072000 | bytes 12289536 | tf_op jit(solution)/shard_map/sub | solution.py:131
  332.4 2.6 multiply_subtract_fusion
  (73 shorter events, 36.5 us)
Async XLA Ops:
  6.5 299.0 %copy-start = (bf16[96,768]{1,0:T(8,128)(2,1)S(1)}, bf16[96,768]{1,0:T(8,128)(2,1)}, u32[]{:S(2)}) copy-start(bf16[96,768]{1,0:T(8,128)(2,1)} %param.14) | copy-start | bytes 442372
  16.0 12.8 %copy-start.10 = (f32[10,10]{1,0:T(8,128)S(1)}, f32[10,10]{1,0:T(8,128)}, u32[]{:S(2)}) copy-start(f32[10,10]{1,0:T(8,128)} %param.15) | copy-start | bytes 1204
  16.0 228.7 %all-to-all-start = ((bf16[96,32,1000]{2,0,1:T(8,128)(2,1)}), bf16[96,32,1000]{2,0,1:T(8,128)(2,1)}, u32[]{:S(2)}, u32[]{:S(2)}) async-start(bf16[96,32,1000]{2,0,1:T(8,128)(2,1)} %copy.32), calls=%async_computation | async-start | bytes 12582912 | tf_op jit(solution)/shard_map/all_to_all | solution.py:94
  28.4 277.2 %all-gather.2.cloned.1.call-start = ((), (), s32[]{:S(2)}) async-start(), calls=%async_computation.1 | async-start | bytes 7077888 | tf_op jit(solution)/shard_map/all_gather | solution.py:108
  34.0 2.2 copy-start.2
  41.8 4.0 %copy-start.12 = (s32[8]{0:T(128)S(1)}, s32[8]{0:T(128)}, u32[]{:S(2)}) copy-start(s32[8]{0:T(128)} %param.19) | copy-start | bytes 100
  45.9 6.2 %copy-start.8 = (f32[3,10,10]{2,0,1:T(4,128)S(1)}, f32[3,10,10]{2,0,1:T(4,128)}, u32[]{:S(2)}) copy-start(f32[3,10,10]{2,0,1:T(4,128)} %param.17) | copy-start | bytes 3604
  46.1 10.5 %copy-start.11 = (f32[10,10]{1,0:T(8,128)S(1)}, f32[10,10]{1,0:T(8,128)}, u32[]{:S(2)}) copy-start(f32[10,10]{1,0:T(8,128)} %param.16) | copy-start | bytes 1204
  46.1 11.5 %copy-start.7 = (f32[8,1000]{1,0:T(8,128)S(1)}, f32[8,1000]{1,0:T(8,128)}, u32[]{:S(2)}) copy-start(f32[8,1000]{1,0:T(8,128)} %param.13) | copy-start | bytes 96004
  59.6 7.6 %copy-start.9 = (s32[6,8]{1,0:T(8,128)S(1)}, s32[6,8]{1,0:T(8,128)}, u32[]{:S(2)}) copy-start(s32[6,8]{1,0:T(8,128)} %param.21) | copy-start | bytes 580
  89.1 12.7 %copy-start.13 = (f32[6,1000,1000]{2,1,0:T(8,128)}, f32[6,1000,1000]{2,1,0:T(8,128)S(1)}, u32[]{:S(2)}) copy-start(f32[6,1000,1000]{2,1,0:T(8,128)S(1)} %fusion.32) | copy-start | bytes 72000000
  89.1 5.1 %copy-start.5 = (f32[1000,1000]{1,0:T(8,128)S(1)}, f32[1000,1000]{1,0:T(8,128)}, u32[]{:S(2)}) copy-start(f32[1000,1000]{1,0:T(8,128)} %fusion.99) | copy-start | bytes 12000004
  89.1 9.3 %copy-start.6 = (f32[1000,1000]{1,0:T(8,128)S(1)}, f32[1000,1000]{1,0:T(8,128)}, u32[]{:S(2)}) copy-start(f32[1000,1000]{1,0:T(8,128)} %fusion.102) | copy-start | bytes 12000004
  101.8 2.0 copy-start.4
  323.5 4.8 %copy-start.1 = (f32[1000,1000]{1,0:T(8,128)S(1)}, f32[1000,1000]{1,0:T(8,128)}, u32[]{:S(2)}) copy-start(f32[1000,1000]{1,0:T(8,128)} %multiply_multiply_fusion) | copy-start | bytes 12000004
  330.4 2.0 copy-start.3
Sparse Core Ops, SparseCore 0:
  51.5 168.9 all-gather.1

commit v3 on v2

--- a/solution.py
+++ b/solution.py
@@ -90,10 +90,13 @@
     slots = send_list[0]
     box_ids = lax.iota(jnp.int32, box_dev)
     send_hot = (slots[:, None] == box_ids[None, :]).astype(jnp.bfloat16)
-    outgoing = pick(send_hot, orbitals)
-    incoming = lax.all_to_all(outgoing, "box", split_axis=1, concat_axis=1, tiled=True)
+    outgoing = jnp.einsum(
+        "sb,nbc->snc", send_hot, orbitals, preferred_element_type=jnp.float32
+    ).astype(jnp.bfloat16)
+    incoming = lax.all_to_all(outgoing, "box", split_axis=0, concat_axis=0, tiled=True)
 
-    values_t = split_bf16(kron3(to_values_mat, to_values_mat, to_values_mat).T)
+    tv = to_values_mat.T
+    values_t = split_bf16(kron3(tv, tv, tv))
     flat = orbitals.reshape(rows, width)
     values = apply_bf16(flat, values_t).reshape(orb_dev, box_dev, width)
 
@@ -108,31 +111,37 @@
     gathered = lax.all_gather(
         compact.reshape(orb_dev, KEEP * width), "orb", axis=0, tiled=True
     )
-    lap0 = laplace_blocks[0]
-    centre = sum(at_place(lap0, width, place) for place in range(3))
-    kinetic = apply_bf16(flat, split_bf16(centre.T))
-    faces = [at_place(laplace_blocks[1 + side], width, which).T
+
+    tc = to_coeffs_mat.T
+    coeffs_t = split_bf16(kron3(tc, tc, tc))
+    local_part = apply_f32((local_values[None, :, :] * values).reshape(rows, width), coeffs_t)
+
+    lap0_t = laplace_blocks[0].T
+    centre = sum(at_place(lap0_t, width, place) for place in range(3))
+    kinetic = apply_bf16(flat, split_bf16(centre))
+    faces = [at_place(laplace_blocks[1 + side].T, width, which)
              for which in range(3) for side in range(2)]
     face_hi, face_lo = split_bf16(jnp.stack(faces))
-    pool = jnp.concatenate([orbitals, incoming], axis=1)
-    pool_ids = lax.iota(jnp.int32, pool.shape[1])
     face_pos = neighbour_pos.reshape(-1)
-    face_hot = (face_pos[:, None] == pool_ids[None, :]).astype(jnp.bfloat16)
-    moved = pick(face_hot, pool).reshape(orb_dev, len(faces), box_dev, width)
+    local_hot = (face_pos[:, None] == box_ids[None, :]).astype(jnp.bfloat16)
+    remote_ids = lax.iota(jnp.int32, n_box)
+    remote_hot = ((face_pos[:, None] - box_dev) == remote_ids[None, :]).astype(jnp.bfloat16)
+    moved = jnp.einsum(
+        "gb,nbc->ngc", local_hot, orbitals, preferred_element_type=jnp.float32
+    ) + jnp.einsum("gr,rnc->ngc", remote_hot, incoming, preferred_element_type=jnp.float32)
+    moved = moved.astype(jnp.bfloat16).reshape(orb_dev, len(faces), box_dev, width)
     kinetic_faces = jnp.einsum(
         "nfbc,fcd->nbd", moved, face_hi, preferred_element_type=jnp.float32
     ) + jnp.einsum("nfbc,fcd->nbd", moved, face_lo, preferred_element_type=jnp.float32)
     kinetic = kinetic + kinetic_faces.reshape(rows, width)
     gathered, kinetic = lax.optimization_barrier((gathered, kinetic))
-    mixed = dot_f32(coupling, gathered).reshape(orb_dev, KEEP, width)
-    spread = jnp.take(mixed, jnp.clip(rank, 0, KEEP - 1), axis=1)
-    exchange = jnp.where(kept[None, :, None], spread, 0.0)
 
-    weighted = local_values[None, :, :] * values - exchange
-    coeffs_t = split_bf16(kron3(to_coeffs_mat, to_coeffs_mat, to_coeffs_mat).T)
-    potential = apply_f32(weighted.reshape(rows, width), coeffs_t)
-
-    total = (potential - 0.5 * kinetic).reshape(orb_dev, box_dev, width)
+    mixed = dot_f32(coupling, gathered).reshape(orb_dev * KEEP, width)
+    exchange_part = apply_f32(mixed, coeffs_t).reshape(orb_dev, KEEP, width)
+    sel_f = sel.astype(jnp.float32)
+    total = (local_part - 0.5 * kinetic).reshape(orb_dev, box_dev, width)
+    for k in range(KEEP):
+        total = total - exchange_part[:, k : k + 1, :] * sel_f[k][None, :, None]
     live = box_ids < box_counts[0]
     total = jnp.where(live[None, :, None], total, 0.0)
     return total.astype(jnp.bfloat16)

time: 349 us -> 366 us (1.049)
  matrix products: 122 us -> 170 us
  waiting for transfers between devices: 137 us -> 122 us
  local copies, waits for them, and re-layouts: 51 us -> 37.9 us
    dot_general x0 -> x3, matrix products: none -> 29.5 us  [the longest x1 18.4 us: shards(): jnp.einsum('gr,rnc->ngc', remote_hot, incoming, preferred_element_type=jn...]
    dot_general x8 -> x11, matrix products: 27.3 us -> 51 us  [dot_f32(): return jnp.dot(a, b, preferred_element_type=jnp.float32)]
    all_to_all x1, waiting for transfers between devices: 137 us -> 122 us  [shards(): lax.all_to_all(outgoing, 'box', split_axis=0, concat_axis=0, tiled=True)]
    gather x3 -> x0, local copies, waits for them, and re-layouts: 11.6 us -> none  [shards(): spread = jnp.take(mixed, jnp.clip(rank, 0, KEEP - 1), axis=1)]
    dot_general x3 -> x1, matrix products: 11.7 us -> 3.06 us  [pick(): jnp.einsum('sb,nbc->nsc', onehot, block, preferred_element_type=jnp.float32)]
    all_to_all x1 -> x0, local copies, waits for them, and re-layouts: 6.46 us -> none  [shards(): lax.all_to_all(outgoing, 'box', split_axis=1, concat_axis=1, tiled=True)]
    sub x1 -> x2, other arithmetic: 4.43 us -> 0.01 us  [the longest x1 0.01 us: shards(): rank = jnp.cumsum(kept.astype(jnp.int32)) - 1]
    unnamed x28 -> x36, local copies, waits for them, and re-layouts: 7.54 us -> 4.76 us
  transfers between devices with their start and end apart: 2 -> 2, of which waited for: 1 -> 1; matrix products, arithmetic and copies ran while one was open for 38% -> 45% of each run, Pallas kernels for 0% -> 0%
where the time goes in v3:
time: 366 us; the launch traced here: 361 us
  matrix products  170 us (46%)
  waiting for transfers between devices  122 us (33%)
  local copies, waits for them, and re-layouts  37.9 us (10%)
  between operations  14.7 us (4%)
  starting transfers between devices  12.6 us (3%)
  other arithmetic  3.71 us (1%)
    all_to_all x1, waiting for transfers between devices, shards(): lax.all_to_all(outgoing, 'box', split_axis=0, concat_axis=0, tiled=True)  122 us
    dot_general x11, matrix products, dot_f32(): return jnp.dot(a, b, preferred_element_type=jnp.float32)  51 us
    dot_general x30, matrix products, expand(): return jnp.dot(jnp.dot(left, mat, precision=hp), right, precision=hp)  48.9 us
    dot_general x1, matrix products, shards(): jnp.einsum('nfbc,fcd->nbd', moved, face_hi, preferred_element_type=jnp.fl...  19.3 us
    dot_general x1, matrix products, shards(): jnp.einsum('nfbc,fcd->nbd', moved, face_lo, preferred_element_type=jnp.fl...  18.5 us
    dot_general x1, matrix products, shards(): jnp.einsum('gr,rnc->ngc', remote_hot, incoming, preferred_element_type=jn...  18.4 us
    all_to_all x1, starting transfers between devices, shards(): lax.all_to_all(outgoing, 'box', split_axis=0, concat_axis=0, tiled=True)  12.4 us
    dot_general x1, matrix products, shards(): jnp.einsum('gb,nbc->ngc', local_hot, orbitals, preferred_element_type=jnp...  8.43 us
  transfers between devices with their start and end apart: 2, of which 1 were waited for; matrix products, arithmetic and copies ran while one was open for 45% of the time, Pallas kernels for 0%

profile of v3, /device:TPU:64, one launch (start us, length us, event | category | flops | bytes accessed | tf_op | source)
XLA Modules:
  0.0 361.4 jit_solution(3497622593195775224)
XLA Ops:
  7.9 2.7 convolution_convert_fusion
  10.7 6.1 %copy.34 = bf16[32,96,1000]{2,1,0:T(8,128)(2,1)} copy(bf16[32,96,1000]{2,0,1:T(8,128)(2,1)S(1)} %convolution_convert_fusion) | data formatting | bytes 12288000 | tf_op jit(solution)/shard_map/convert_element_type | solution.py:95
  16.8 12.4 %all-to-all-start = ((bf16[32,96,1000]{2,1,0:T(8,128)(2,1)}), bf16[32,96,1000]{2,1,0:T(8,128)(2,1)}, u32[]{:S(2)}, u32[]{:S(2)}) async-start(bf16[32,96,1000]{2,1,0:T(8,128)(2,1)} %copy.34), calls=%async_computation | async-start | bytes 12582912 | tf_op jit(solution)/shard_map/all_to_all | solution.py:96
  36.9 3.7 %fusion.38 = f32[1000,768]{1,0:T(8,128)} fusion(f32[1000,1000]{1,0:T(8,128)S(1)} %multiply_multiply_fusion.1, bf16[96,8,1000]{2,1,0:T(8,128)(2,1)S(1)} %copy-done), kind=kOutput, calls=%fused_computation.76 | convolution fusion | flops 1539000064 | bytes 8608000 | tf_op jit(solution)/shard_map/dot_general | solution.py:50
  42.6 3.6 copy.31
  46.2 8.0 %reduce-precision_convert_fusion.4 = (bf16[768,1000]{0,1:T(8,128)(2,1)}, f32[768,1000]{0,1:T(8,128)}) fusion(f32[768,1000]{0,1:T(8,128)} %copy.31, f32[1000,768]{1,0:T(8,128)} %fusion.38, bf16[96,8,1000]{2,1,0:T(8,128)(2,1)S(1)} %copy-done, f32[1000,1000]{1,0:T(8,128)} %copy-done.5), kind=kOutput, calls=%fused_computation.37 | convolution fusion | flops 1541072000 | bytes 16288000 | tf_op jit(solution)/shard_map/dot_general | solution.py:50
  54.2 3.9 %copy.32 = f32[768,1000]{1,0:T(8,128)} copy(f32[768,1000]{0,1:T(8,128)} %get-tuple-element.25) | data formatting | bytes 6144000 | tf_op jit(solution)/shard_map/add | solution.py:55
  58.4 3.1 fusion.60
  77.6 4.0 %fusion.16 = f32[6,1000,1000]{2,1,0:T(8,128)} fusion(f32[1000,10]{0,1:T(8,128)S(1)} %fusion.79, s32[1000]{0:T(1024)S(1)} %get-tuple-element.27, s32[1000]{0:T(1024)S(1)} %get-tuple-element.26, s32[1000]{0:T(1024)S(1)} %add_select_fusion.3), kind=kOutput, calls=%fused_computation.44 | convolution fusion | flops 124010000 | bytes 4182016 | tf_op jit(solution)/shard_map/dot_general | solution.py:21
  81.6 3.8 %fusion.18 = f32[6,1000,1000]{2,1,0:T(8,128)} fusion(f32[6,1000,1000]{2,1,0:T(8,128)} %fusion.16, f32[1000,10]{0,1:T(8,128)S(1)} %fusion.78, s32[1000]{0:T(1024)S(1)} %get-tuple-element.27, s32[1000]{0:T(1024)S(1)} %get-tuple-element.26, s32[1000]{0:T(1024)S(1)} %add_select_fusion.3), kind=kOutput, calls=%fused_computation.46 | convolution fusion | flops 124010000 | bytes 4182016 | tf_op jit(solution)/shard_map/dot_general | solution.py:21
  85.4 3.8 %fusion.20 = f32[6,1000,1000]{2,1,0:T(8,128)} fusion(f32[6,1000,1000]{2,1,0:T(8,128)} %fusion.18, f32[1000,10]{0,1:T(8,128)S(1)} %fusion.74, s32[1000]{0:T(1024)S(1)} %add_select_fusion.3, s32[1000]{0:T(1024)S(1)} %get-tuple-element.26, s32[1000]{0:T(1024)S(1)} %get-tuple-element.27), kind=kOutput, calls=%fused_computation.48 | convolution fusion | flops 124010000 | bytes 4182016 | tf_op jit(solution)/shard_map/dot_general | solution.py:21
  89.2 3.8 %fusion.22 = f32[6,1000,1000]{2,1,0:T(8,128)} fusion(f32[6,1000,1000]{2,1,0:T(8,128)} %fusion.20, f32[1000,10]{0,1:T(8,128)S(1)} %fusion.73, s32[1000]{0:T(1024)S(1)} %add_select_fusion.3, s32[1000]{0:T(1024)S(1)} %get-tuple-element.26, s32[1000]{0:T(1024)S(1)} %get-tuple-element.27), kind=kOutput, calls=%fused_computation.50 | convolution fusion | flops 124010000 | bytes 4182016 | tf_op jit(solution)/shard_map/dot_general | solution.py:21
  93.0 3.8 %fusion.24 = f32[6,1000,1000]{2,1,0:T(8,128)} fusion(f32[6,1000,1000]{2,1,0:T(8,128)} %fusion.22, f32[1000,10]{0,1:T(8,128)S(1)} %fusion.69, s32[1000]{0:T(1024)S(1)} %add_select_fusion.3, s32[1000]{0:T(1024)S(1)} %get-tuple-element.27, s32[1000]{0:T(1024)S(1)} %get-tuple-element.26), kind=kOutput, calls=%fused_computation.52 | convolution fusion | flops 124010000 | bytes 4182016 | tf_op jit(solution)/shard_map/dot_general | solution.py:21
  96.7 3.8 %fusion.26 = f32[6,1000,1000]{2,1,0:T(8,128)} fusion(f32[6,1000,1000]{2,1,0:T(8,128)} %fusion.24, f32[1000,10]{0,1:T(8,128)S(1)} %fusion.68, s32[1000]{0:T(1024)S(1)} %add_select_fusion.3, s32[1000]{0:T(1024)S(1)} %get-tuple-element.27, s32[1000]{0:T(1024)S(1)} %get-tuple-element.26), kind=kOutput, calls=%fused_computation.54 | convolution fusion | flops 124010000 | bytes 4182016 | tf_op jit(solution)/shard_map/dot_general | solution.py:21
  102.8 3.6 fusion.148
  106.4 3.5 fusion.66
  109.9 3.3 fusion.14
  115.2 3.6 %fusion.36 = f32[1000,768]{1,0:T(8,128)} fusion(f32[1000,1000]{1,0:T(8,128)S(1)} %fusion.14, bf16[96,8,1000]{2,1,0:T(8,128)(2,1)S(1)} %copy-done), kind=kOutput, calls=%fused_computation.75 | convolution fusion | flops 1539000064 | bytes 8608000 | tf_op jit(solution)/shard_map/dot_general | solution.py:50
  118.9 8.4 %fusion.133 = f32[48,96,1000]{2,0,1:T(8,128)} fusion(bf16[96,8,1000]{2,1,0:T(8,128)(2,1)S(1)} %copy-done, s32[48]{0:T(128)S(1)} %eq.744), kind=kOutput, calls=%fused_computation.184 | convolution fusion | flops 73728384 | bytes 19968192 | tf_op jit(solution)/shard_map/gb,nbc->ngc/dot_general | solution.py:129
  127.3 122.2 %all-to-all-done = bf16[32,96,1000]{2,1,0:T(8,128)(2,1)} async-done(((bf16[32,96,1000]{2,1,0:T(8,128)(2,1)}), bf16[32,96,1000]{2,1,0:T(8,128)(2,1)}, u32[]{:S(2)}, u32[]{:S(2)}) %all-to-all-start) | async-done | bytes 6144032 | tf_op jit(solution)/shard_map/all_to_all | solution.py:96
  249.5 18.4 %fusion.8 = bf16[96,6,8,1000]{3,2,1,0:T(8,128)(2,1)} fusion(f32[48,96,1000]{2,0,1:T(8,128)} %fusion.133, bf16[32,96,1000]{2,1,0:T(8,128)(2,1)} %all-to-all-done, s32[48]{0:T(128)S(1)} %broadcast_add_fusion), kind=kOutput, calls=%fused_computation.27 | convolution fusion | flops 304129536 | bytes 33792192 | tf_op jit(solution)/shard_map/gr,rnc->ngc/dot_general | solution.py:131
  267.9 18.5 %fusion.3 = f32[96,8,1000,1]{2,1,3,0:T(8,128)} fusion(bf16[96,6,8,1000]{3,2,1,0:T(8,128)(2,1)} %fusion.8, f32[6,1000,1000]{2,1,0:T(8,128)} %fusion.26), kind=kOutput, calls=%fused_computation.6 | convolution fusion | flops 9233999872 | bytes 36288000 | tf_op jit(solution)/shard_map/nfbc,fcd->nbd/dot_general | solution.py:135
  286.4 19.3 %fusion.32 = f32[768,1000]{1,0:T(8,128)} fusion(f32[96,8,1000,1]{2,1,3,0:T(8,128)} %fusion.3, bf16[96,6,8,1000]{3,2,1,0:T(8,128)(2,1)} %fusion.8, f32[6,1000,1000]{2,1,0:T(8,128)} %fusion.26), kind=kOutput, calls=%fused_computation.65 | convolution fusion | flops 9228768256 | bytes 39360000 | tf_op jit(solution)/shard_map/nfbc,fcd->nbd/dot_general | solution.py:133
  305.8 3.6 copy.38
  309.3 7.6 %bitcast_add_fusion.2 = f32[768,1000]{0,1:T(8,128)} fusion(f32[768,1000]{0,1:T(8,128)} %copy.38, f32[1000,768]{1,0:T(8,128)} %fusion.36, bf16[96,8,1000]{2,1,0:T(8,128)(2,1)S(1)} %copy-done, f32[1000,1000]{1,0:T(8,128)} %copy-done.7), kind=kOutput, calls=%fused_computation.70 | convolution fusion | flops 1539536000 | bytes 14752000 | tf_op jit(solution)/shard_map/dot_general | solution.py:50
  316.9 5.1 %convolution_bitcast_fusion = f32[96,4000]{1,0:T(8,128)} fusion(bf16[96,768]{1,0:T(8,128)(2,1)S(1)} %copy-done.9, bf16[768,4000]{1,0:T(8,128)(2,1)} %all-gather.2.cloned.1.call-done), kind=kOutput, calls=%fused_computation.35 | convolution fusion | flops 589824000 | bytes 7827456 | tf_op jit(solution)/shard_map/dot_general | solution.py:50
  324.2 3.6 fusion.64
  329.1 2.5 add_add_fusion
  331.6 3.0 copy.40
  338.9 8.5 %multiply_subtract_fusion = f32[768,1000]{0,1:T(8,128)} fusion(f32[768,1000]{0,1:T(8,128)} %bitcast_add_fusion.2, f32[768,1000]{0,1:T(8,128)} %fusion.148, f32[768,1000]{0,1:T(8,128)} %fusion.66, bf16[1000,1000]{1,0:T(8,128)(2,1)S(1)} %copy-done.3, f32[768,1000]{0,1:T(8,128)S(1)} %copy-done.4, f32[768,1000]{0,1:T(8,128)} %get-tuple-element.25), kind=kOutput, calls=%fused_computation.71 | convolution fusion | flops 1542144000 | bytes 20432000 | tf_op jit(solution)/shard_map/dot_general | solution.py:50
  347.4 3.5 copy.39
  350.9 3.5 fusion.31
  (79 shorter events, 38.7 us)
Async XLA Ops:
  6.5 1.4 copy-start
  16.8 12.7 %copy-start.13 = (f32[10,10]{1,0:T(8,128)S(1)}, f32[10,10]{1,0:T(8,128)}, u32[]{:S(2)}) copy-start(f32[10,10]{1,0:T(8,128)} %param.15) | copy-start | bytes 1204
  16.8 232.7 %all-to-all-start = ((bf16[32,96,1000]{2,1,0:T(8,128)(2,1)}), bf16[32,96,1000]{2,1,0:T(8,128)(2,1)}, u32[]{:S(2)}, u32[]{:S(2)}) async-start(bf16[32,96,1000]{2,1,0:T(8,128)(2,1)} %copy.34), calls=%async_computation | async-start | bytes 12582912 | tf_op jit(solution)/shard_map/all_to_all | solution.py:96
  29.2 287.7 %all-gather.2.cloned.1.call-start = ((), (), s32[]{:S(2)}) async-start(), calls=%async_computation.1 | async-start | bytes 7077888 | tf_op jit(solution)/shard_map/all_gather | solution.py:111
  36.8 3.8 %copy-start.5 = (f32[1000,1000]{1,0:T(8,128)}, f32[1000,1000]{1,0:T(8,128)S(1)}, u32[]{:S(2)}) copy-start(f32[1000,1000]{1,0:T(8,128)S(1)} %multiply_multiply_fusion.1) | copy-start | bytes 12000004
  36.8 3.7 %copy-start.10 = (f32[8,1000]{1,0:T(8,128)S(1)}, f32[8,1000]{1,0:T(8,128)}, u32[]{:S(2)}) copy-start(f32[8,1000]{1,0:T(8,128)} %param.13) | copy-start | bytes 96004
  54.2 3.9 %copy-start.15 = (s32[8]{0:T(128)S(1)}, s32[8]{0:T(128)}, u32[]{:S(2)}) copy-start(s32[8]{0:T(128)} %param.19) | copy-start | bytes 100
  58.1 5.5 %copy-start.12 = (s32[6,8]{1,0:T(8,128)S(1)}, s32[6,8]{1,0:T(8,128)}, u32[]{:S(2)}) copy-start(s32[6,8]{1,0:T(8,128)} %param.21) | copy-start | bytes 580
  58.1 6.3 %copy-start.11 = (f32[3,10,10]{2,0,1:T(4,128)S(1)}, f32[3,10,10]{2,0,1:T(4,128)}, u32[]{:S(2)}) copy-start(f32[3,10,10]{2,0,1:T(4,128)} %param.17) | copy-start | bytes 3604
  58.4 10.4 %copy-start.14 = (f32[10,10]{1,0:T(8,128)S(1)}, f32[10,10]{1,0:T(8,128)}, u32[]{:S(2)}) copy-start(f32[10,10]{1,0:T(8,128)} %param.16) | copy-start | bytes 1204
  100.5 2.3 copy-start.8
  102.8 3.6 %copy-start.1 = (bf16[1000,1000]{1,0:T(8,128)(2,1)}, bf16[1000,1000]{1,0:T(8,128)(2,1)S(1)}, u32[]{:S(2)}) copy-start(bf16[1000,1000]{1,0:T(8,128)(2,1)S(1)} %get-tuple-element.22) | copy-start | bytes 6000004
  102.8 3.6 %copy-start.6 = (f32[1000,1000]{1,0:T(8,128)}, f32[1000,1000]{1,0:T(8,128)S(1)}, u32[]{:S(2)}) copy-start(f32[1000,1000]{1,0:T(8,128)S(1)} %get-tuple-element.23) | copy-start | bytes 12000004
  113.2 2.0 copy-start.7
  309.3 7.6 %copy-start.9 = (bf16[96,768]{1,0:T(8,128)(2,1)S(1)}, bf16[96,768]{1,0:T(8,128)(2,1)}, u32[]{:S(2)}) copy-start(bf16[96,768]{1,0:T(8,128)(2,1)} %param.14) | copy-start | bytes 442372
  324.2 3.6 copy-start.2
  336.4 1.6 copy-start.3
  336.4 2.5 copy-start.4
Sparse Core Ops, SparseCore 0:
  63.8 159.6 all-gather.1

commit v4 on v2

--- a/solution.py
+++ b/solution.py
@@ -91,7 +91,12 @@
     box_ids = lax.iota(jnp.int32, box_dev)
     send_hot = (slots[:, None] == box_ids[None, :]).astype(jnp.bfloat16)
     outgoing = pick(send_hot, orbitals)
-    incoming = lax.all_to_all(outgoing, "box", split_axis=1, concat_axis=1, tiled=True)
+    half = orb_dev // 2
+    incoming_a = lax.all_to_all(
+        outgoing[:half], "box", split_axis=1, concat_axis=1, tiled=True
+    )
+    later, incoming_a = lax.optimization_barrier((outgoing[half:], incoming_a))
+    incoming_b = lax.all_to_all(later, "box", split_axis=1, concat_axis=1, tiled=True)
 
     values_t = split_bf16(kron3(to_values_mat, to_values_mat, to_values_mat).T)
     flat = orbitals.reshape(rows, width)
@@ -114,16 +119,21 @@
     faces = [at_place(laplace_blocks[1 + side], width, which).T
              for which in range(3) for side in range(2)]
     face_hi, face_lo = split_bf16(jnp.stack(faces))
-    pool = jnp.concatenate([orbitals, incoming], axis=1)
-    pool_ids = lax.iota(jnp.int32, pool.shape[1])
+    pool_ids = lax.iota(jnp.int32, box_dev + n_box)
     face_pos = neighbour_pos.reshape(-1)
     face_hot = (face_pos[:, None] == pool_ids[None, :]).astype(jnp.bfloat16)
-    moved = pick(face_hot, pool).reshape(orb_dev, len(faces), box_dev, width)
-    kinetic_faces = jnp.einsum(
-        "nfbc,fcd->nbd", moved, face_hi, preferred_element_type=jnp.float32
-    ) + jnp.einsum("nfbc,fcd->nbd", moved, face_lo, preferred_element_type=jnp.float32)
-    kinetic = kinetic + kinetic_faces.reshape(rows, width)
-    gathered, kinetic = lax.optimization_barrier((gathered, kinetic))
+
+    def face_part(own, arrived):
+        pool = jnp.concatenate([own, arrived], axis=1)
+        moved = pick(face_hot, pool).reshape(own.shape[0], len(faces), box_dev, width)
+        return jnp.einsum(
+            "nfbc,fcd->nbd", moved, face_hi, preferred_element_type=jnp.float32
+        ) + jnp.einsum("nfbc,fcd->nbd", moved, face_lo, preferred_element_type=jnp.float32)
+
+    first = face_part(orbitals[:half], incoming_a)
+    gathered, first = lax.optimization_barrier((gathered, first))
+    second = face_part(orbitals[half:], incoming_b)
+    kinetic = kinetic + jnp.concatenate([first, second], axis=0).reshape(rows, width)
     mixed = dot_f32(coupling, gathered).reshape(orb_dev, KEEP, width)
     spread = jnp.take(mixed, jnp.clip(rank, 0, KEEP - 1), axis=1)
     exchange = jnp.where(kept[None, :, None], spread, 0.0)

time: 349 us -> 311 us (0.89)
  the two profiles are of different devices: /device:TPU:64 before, /device:TPU:90 now
where the time goes in v4:
time: 311 us; the launch traced here: 306 us
  matrix products  150 us (48%)
  local copies, waits for them, and re-layouts  54.6 us (18%)
  waiting for transfers between devices  49.9 us (16%)
  starting transfers between devices  24.9 us (8%)
  between operations  14.8 us (5%)
  other arithmetic  12.1 us (4%)
    dot_general x30, matrix products, expand(): return jnp.dot(jnp.dot(left, mat, precision=hp), right, precision=hp)  58.4 us
    all_gather x1, waiting for transfers between devices, shards(): lax.all_gather(compact.reshape(orb_dev, KEEP * width), 'orb', axis=0, til...  49.9 us
    dot_general x8, matrix products, dot_f32(): return jnp.dot(a, b, preferred_element_type=jnp.float32)  33.6 us
    dot_general x2, matrix products, face_part(): jnp.einsum('nfbc,fcd->nbd', moved, face_hi, preferred_element_type=jnp.fl...  24.3 us
    dot_general x2, matrix products, face_part(): jnp.einsum('nfbc,fcd->nbd', moved, face_lo, preferred_element_type=jnp.fl...  22.1 us
    all_to_all x1, starting transfers between devices, shards(): lax.all_to_all(later, 'box', split_axis=1, concat_axis=1, tiled=True)  12.5 us
    all_to_all x1, starting transfers between devices, shards(): lax.all_to_all(outgoing[:half], 'box', split_axis=1, concat_axis=1, tiled...  12.2 us
    dot_general x4, matrix products, pick(): jnp.einsum('sb,nbc->nsc', onehot, block, preferred_element_type=jnp.float32)  11.5 us
  transfers between devices with their start and end apart: 3, of which 1 were waited for; matrix products, arithmetic and copies ran while one was open for 53% of the time, Pallas kernels for 0%

profile of v4, /device:TPU:90, one launch (start us, length us, event | category | flops | bytes accessed | tf_op | source)
XLA Modules:
  0.0 306.4 jit_solution(10764925760638404198)
XLA Ops:
  6.5 3.3 %convert_bitcast_fusion = bf16[96,32,1000]{2,1,0:T(8,128)(2,1)S(1)} fusion(bf16[96,8,1000]{2,1,0:T(8,128)(2,1)} %param.11, s32[32]{0:T(128)} %bitcast.174), kind=kOutput, calls=%fused_computation.24 | convolution fusion | flops 52224256 | bytes 7680128 | tf_op jit(solution)/shard_map/sb,nbc->nsc/dot_general | solution.py:67
  12.3 3.4 %copy.31 = bf16[48,32,1000]{2,0,1:T(8,128)(2,1)} copy(bf16[48,32,1000]{2,1,0:T(8,128)(2,1)S(1)} %get-tuple-element.13) | data formatting | bytes 6144000 | tf_op jit(solution)/shard_map/slice | solution.py:96
  15.7 12.2 %all-to-all-start = ((bf16[48,32,1000]{2,0,1:T(8,128)(2,1)}), bf16[48,32,1000]{2,0,1:T(8,128)(2,1)S(1)}, u32[]{:S(2)}, u32[]{:S(2)}) async-start(bf16[48,32,1000]{2,0,1:T(8,128)(2,1)} %copy.31), calls=%async_computation | async-start | bytes 6291456 | tf_op jit(solution)/shard_map/all_to_all | solution.py:95
  37.7 3.6 %add_bitcast_fusion = f32[768,1000]{0,1:T(8,128)} fusion(f32[1000,768]{1,0:T(8,128)S(1)} %fusion.56, f32[1000,1000]{1,0:T(8,128)S(1)} %multiply_multiply_fusion.1, bf16[96,8,1000]{2,1,0:T(8,128)(2,1)S(1)} %copy-done.5), kind=kOutput, calls=%fused_computation.81 | convolution fusion | flops 1538768000 | bytes 11680000 | tf_op jit(solution)/shard_map/dot_general | solution.py:50
  41.3 3.8 %copy.30 = f32[768,1000]{1,0:T(8,128)} copy(f32[768,1000]{0,1:T(8,128)} %add_bitcast_fusion) | data formatting | bytes 6144000 | tf_op jit(solution)/shard_map/add | solution.py:55
  45.9 3.9 %fusion.80 = bf16[96,4,1000]{2,1,0:T(4,128)(2,1)} fusion(f32[768,1000]{1,0:T(8,128)} %copy.30, bf16[96,8,1000]{2,1,0:T(8,128)(2,1)} %param.12, pred[8]{0:T(512)(128)(4,1)S(1)} %get-tuple-element.23, s32[8]{0:T(128)S(1)} %get-tuple-element.21), kind=kOutput, calls=%fused_computation.100 | convolution fusion | flops 9600064 | bytes 5376040 | tf_op jit(solution)/shard_map/sb,nbc->nsc/dot_general | solution.py:67
  78.3 4.0 %copy.29 = f32[768,1000]{0,1:T(8,128)} copy(f32[768,1000]{1,0:T(8,128)} %broadcast_bitcast_fusion) | data formatting | bytes 6144000 | tf_op jit(solution)/shard_map/mul | solution.py:141
  93.1 3.8 %fusion.15 = f32[6,1000,1000]{2,1,0:T(8,128)} fusion(f32[1000,10]{0,1:T(8,128)S(1)} %copy-done.29, s32[1000]{0:T(1024)S(1)} %copy-done.12, s32[1000]{0:T(1024)S(1)} %copy-done.14, s32[1000]{0:T(1024)S(1)} %copy-done.10), kind=kOutput, calls=%fused_computation.46 | convolution fusion | flops 124010000 | bytes 4182016 | tf_op jit(solution)/shard_map/dot_general | solution.py:21
  97.0 3.8 %fusion.17 = f32[6,1000,1000]{2,1,0:T(8,128)} fusion(f32[6,1000,1000]{2,1,0:T(8,128)} %fusion.15, f32[1000,10]{0,1:T(8,128)S(1)} %copy-done.30, s32[1000]{0:T(1024)S(1)} %copy-done.12, s32[1000]{0:T(1024)S(1)} %copy-done.14, s32[1000]{0:T(1024)S(1)} %copy-done.10), kind=kOutput, calls=%fused_computation.48 | convolution fusion | flops 124010000 | bytes 4182016 | tf_op jit(solution)/shard_map/dot_general | solution.py:21
  100.8 3.9 %fusion.19 = f32[6,1000,1000]{2,1,0:T(8,128)} fusion(f32[6,1000,1000]{2,1,0:T(8,128)} %fusion.17, f32[1000,10]{0,1:T(8,128)S(1)} %copy-done.28, s32[1000]{0:T(1024)S(1)} %copy-done.10, s32[1000]{0:T(1024)S(1)} %copy-done.14, s32[1000]{0:T(1024)S(1)} %copy-done.12), kind=kOutput, calls=%fused_computation.50 | convolution fusion | flops 124010000 | bytes 4182016 | tf_op jit(solution)/shard_map/dot_general | solution.py:21
  104.7 3.8 %fusion.21 = f32[6,1000,1000]{2,1,0:T(8,128)} fusion(f32[6,1000,1000]{2,1,0:T(8,128)} %fusion.19, f32[1000,10]{0,1:T(8,128)S(1)} %copy-done.27, s32[1000]{0:T(1024)S(1)} %copy-done.10, s32[1000]{0:T(1024)S(1)} %copy-done.14, s32[1000]{0:T(1024)S(1)} %copy-done.12), kind=kOutput, calls=%fused_computation.52 | convolution fusion | flops 124010000 | bytes 4182016 | tf_op jit(solution)/shard_map/dot_general | solution.py:21
  108.5 3.8 %fusion.25 = f32[6,1000,1000]{2,1,0:T(8,128)} fusion(f32[6,1000,1000]{2,1,0:T(8,128)} %fusion.21, f32[1000,10]{0,1:T(8,128)S(1)} %copy-done.26, s32[1000]{0:T(1024)S(1)} %copy-done.10, s32[1000]{0:T(1024)S(1)} %copy-done.12, s32[1000]{0:T(1024)S(1)} %copy-done.14), kind=kOutput, calls=%fused_computation.56 | convolution fusion | flops 124010000 | bytes 4182016 | tf_op jit(solution)/shard_map/dot_general | solution.py:21
  112.3 4.0 %fusion.27 = f32[6,1000,1000]{2,1,0:T(8,128)} fusion(f32[6,1000,1000]{2,1,0:T(8,128)} %fusion.25, f32[1000,10]{0,1:T(8,128)S(1)} %copy-done.25, s32[1000]{0:T(1024)S(1)} %copy-done.10, s32[1000]{0:T(1024)S(1)} %copy-done.12, s32[1000]{0:T(1024)S(1)} %copy-done.14), kind=kOutput, calls=%fused_computation.58 | convolution fusion | flops 124010000 | bytes 4182016 | tf_op jit(solution)/shard_map/dot_general | solution.py:21
  116.3 3.4 %fusion.23 = f32[1000,1000]{1,0:T(8,128)S(1)} fusion(f32[1000,1000]{1,0:T(8,128)S(1)} %fusion.117, f32[1000,1000]{1,0:T(8,128)S(1)} %fusion.114, f32[1000,10]{0,1:T(8,128)S(1)} %copy-done.31, s32[1000]{0:T(1024)S(1)} %copy-done.10, s32[1000]{0:T(1024)S(1)} %copy-done.12, s32[1000]{0:T(1024)S(1)} %copy-done.14), kind=kOutput, calls=%fused_computation.54 | convolution fusion | flops 131010000 | bytes 12052000 | tf_op jit(solution)/shard_map/dot_general | solution.py:21
  119.7 3.6 %fusion.59 = f32[1000,768]{1,0:T(8,128)} fusion(f32[1000,1000]{1,0:T(8,128)S(1)} %fusion.23, bf16[96,8,1000]{2,1,0:T(8,128)(2,1)S(1)} %copy-done.6), kind=kOutput, calls=%fused_computation.88 | convolution fusion | flops 1538000000 | bytes 8608000 | tf_op jit(solution)/shard_map/dot_general | solution.py:50
  123.3 4.2 %multiply_multiply_fusion = f32[1000,1000]{1,0:T(8,128)} fusion(f32[1000,1000]{1,0:T(8,128)S(1)} %fusion.118, f32[1000,1000]{1,0:T(8,128)S(1)} %fusion.115, f32[1000,10]{0,1:T(8,128)S(1)} %fusion.85, s32[1000]{0:T(1024)S(1)} %copy-done.14), kind=kOutput, calls=%fused_computation.59 | convolution fusion | flops 122010000 | bytes 12044000 | tf_op jit(solution)/shard_map/dot_general | solution.py:21
  127.5 3.7 %fusion.52 = f32[1000,768]{1,0:T(8,128)} fusion(f32[1000,1000]{1,0:T(8,128)S(1)} %fusion.23, bf16[96,8,1000]{2,1,0:T(8,128)(2,1)S(1)} %copy-done.6), kind=kOutput, calls=%fused_computation.84 | convolution fusion | flops 1539000064 | bytes 8608000 | tf_op jit(solution)/shard_map/dot_general | solution.py:50
  131.2 3.4 %copy.32 = bf16[48,32,1000]{2,1,0:T(8,128)(2,1)} copy(bf16[48,32,1000]{2,0,1:T(8,128)(2,1)S(1)} %all-to-all-done) | data formatting | bytes 6144000 | tf_op jit(solution)/shard_map/optimization_barrier | solution.py:98
  134.6 3.8 %copy.39 = bf16[48,32,1000]{2,0,1:T(8,128)(2,1)} copy(bf16[48,32,1000]{2,1,0:T(8,128)(2,1)S(1)} %copy-done.3) | data formatting | bytes 6144000 | tf_op jit(solution)/shard_map/optimization_barrier | solution.py:98
  138.5 12.5 %all-to-all-start.1 = ((bf16[48,32,1000]{2,0,1:T(8,128)(2,1)}), bf16[48,32,1000]{2,0,1:T(8,128)(2,1)}, u32[]{:S(2)}, u32[]{:S(2)}) async-start(bf16[48,32,1000]{2,0,1:T(8,128)(2,1)} %copy.39), calls=%async_computation.1 | async-start | bytes 6291456 | tf_op jit(solution)/shard_map/all_to_all | solution.py:99
  153.7 11.1 %fusion.7 = f32[48,8,1000,1]{2,1,3,0:T(8,128)S(1)} fusion(bf16[48,1000,48]{1,2,0:T(8,128)(2,1)S(1)} %fusion.49, f32[6,1000,1000]{2,1,0:T(8,128)} %fusion.27), kind=kOutput, calls=%fused_computation.36 | convolution fusion | flops 4625999872 | bytes 30144000 | tf_op jit(solution)/shard_map/nfbc,fcd->nbd/dot_general | solution.py:131
  164.7 12.1 %bitcast_add_fusion.2 = f32[48,8,1000]{2,1,0:T(8,128)} fusion(f32[48,8,1000,1]{2,1,3,0:T(8,128)S(1)} %fusion.7, f32[6,1000,1000]{2,1,0:T(8,128)} %fusion.27, bf16[48,1000,48]{1,2,0:T(8,128)(2,1)S(1)} %fusion.49), kind=kOutput, calls=%fused_computation.91 | convolution fusion | flops 4620384256 | bytes 31680000 | tf_op jit(solution)/shard_map/nfbc,fcd->nbd/dot_general | solution.py:129
  176.8 49.9 %all-gather.2.cloned.1.call-done = bf16[768,4000]{1,0:T(8,128)(2,1)} async-done(((bf16[96,4000]{1,0:T(8,128)(2,1)}), bf16[768,4000]{1,0:T(8,128)(2,1)}) %all-gather.2.cloned.1.call-update) | async-done | bytes 6144016 | tf_op jit(solution)/shard_map/all_gather | solution.py:113
  226.7 3.9 %convolution_bitcast_fusion = f32[96,4000]{1,0:T(8,128)S(1)} fusion(bf16[96,768]{1,0:T(8,128)(2,1)S(1)} %copy-done, bf16[768,4000]{1,0:T(8,128)(2,1)} %all-gather.2.cloned.1.call-done), kind=kOutput, calls=%fused_computation.31 | convolution fusion | flops 589824000 | bytes 7827456 | tf_op jit(solution)/shard_map/dot_general | solution.py:50
  235.6 3.7 %copy.63 = f32[96,8,1000]{2,1,0:T(8,128)S(1)} copy(f32[96,8,1000]{2,0,1:T(8,128)} %bitcast.172) | data formatting | bytes 6144000 | tf_op jit(solution)/shard_map/jit(_take)/gather | solution.py:138
  241.9 4.4 %select_subtract_fusion = f32[768,1000]{0,1:T(8,128)S(1)} fusion(f32[768,1000]{0,1:T(8,128)} %copy.37, f32[768,1000]{0,1:T(8,128)} %copy.29, f32[768,1000]{0,1:T(8,128)} %add_bitcast_fusion, pred[768]{0:T(1024)(128)(4,1)S(1)} %copy-done.18, pred[768]{0:T(1024)(128)(4,1)S(1)} %copy-done.19), kind=kLoop, calls=%fused_computation.80 | loop fusion | flops 3072000 | bytes 12289536 | tf_op jit(solution)/shard_map/sub | solution.py:141
  246.8 3.5 %fusion.83 = f32[768,1000]{0,1:T(8,128)} fusion(f32[1000,1000]{1,0:T(8,128)S(1)} %copy-done.1, f32[768,1000]{0,1:T(8,128)S(1)} %select_subtract_fusion), kind=kOutput, calls=%fused_computation.101 | convolution fusion | flops 1539536000 | bytes 10144000 | tf_op jit(solution)/shard_map/dot_general | solution.py:50
  250.3 3.5 %fusion.54 = f32[768,1000]{0,1:T(8,128)} fusion(f32[1000,1000]{1,0:T(8,128)S(1)} %copy-done.1, f32[768,1000]{0,1:T(8,128)S(1)} %select_subtract_fusion), kind=kOutput, calls=%fused_computation.85 | convolution fusion | flops 1540536064 | bytes 10144000 | tf_op jit(solution)/shard_map/dot_general | solution.py:50
  253.8 3.7 %copy.40 = bf16[48,32,1000]{2,1,0:T(8,128)(2,1)S(1)} copy(bf16[48,32,1000]{2,0,1:T(8,128)(2,1)} %all-to-all-done.1) | data formatting | bytes 6144000 | tf_op jit(solution)/shard_map/all_to_all | solution.py:99
  259.1 11.1 %fusion.3 = f32[48,8,1000,1]{2,1,3,0:T(8,128)S(1)} fusion(bf16[48,1000,48]{1,2,0:T(8,128)(2,1)S(1)} %fusion.46, f32[6,1000,1000]{2,1,0:T(8,128)} %fusion.27), kind=kOutput, calls=%fused_computation.32 | convolution fusion | flops 4625999872 | bytes 30144000 | tf_op jit(solution)/shard_map/nfbc,fcd->nbd/dot_general | solution.py:131
  270.2 12.3 %bitcast_add_fusion.1 = f32[48,8,1000]{2,1,0:T(8,128)} fusion(f32[48,8,1000,1]{2,1,3,0:T(8,128)S(1)} %fusion.3, f32[6,1000,1000]{2,1,0:T(8,128)} %fusion.27, bf16[48,1000,48]{1,2,0:T(8,128)(2,1)S(1)} %fusion.46), kind=kOutput, calls=%fused_computation.90 | convolution fusion | flops 4620384256 | bytes 31680000 | tf_op jit(solution)/shard_map/nfbc,fcd->nbd/dot_general | solution.py:129
  287.1 9.7 %fusion.45 = bf16[768,1000]{0,1:T(8,128)(2,1)S(1)} fusion(f32[768,1000]{0,1:T(8,128)} %copy.41, f32[1000,768]{1,0:T(8,128)} %fusion.59, f32[1000,768]{1,0:T(8,128)} %fusion.52, f32[768,1000]{0,1:T(8,128)} %fusion.83, f32[768,1000]{0,1:T(8,128)} %fusion.54, f32[768,1000]{0,1:T(8,128)} %copy-done.4, f32[1000,1000]{1,0:T(8,128)} %multiply_multiply_fusion), kind=kOutput, calls=%fused_computation.79 | convolution fusion | flops 1545680000 | bytes 23968000 | tf_op jit(solution)/shard_map/dot_general | solution.py:50
  (119 shorter events, 70.7 us)
Async XLA Ops:
  6.5 220.2 %copy-start = (bf16[96,768]{1,0:T(8,128)(2,1)S(1)}, bf16[96,768]{1,0:T(8,128)(2,1)}, u32[]{:S(2)}) copy-start(bf16[96,768]{1,0:T(8,128)(2,1)} %param.14) | copy-start | bytes 442372
  15.7 12.6 %copy-start.21 = (f32[10,10]{1,0:T(8,128)S(1)}, f32[10,10]{1,0:T(8,128)}, u32[]{:S(2)}) copy-start(f32[10,10]{1,0:T(8,128)} %param.15) | copy-start | bytes 1204
  15.7 115.5 %all-to-all-start = ((bf16[48,32,1000]{2,0,1:T(8,128)(2,1)}), bf16[48,32,1000]{2,0,1:T(8,128)(2,1)S(1)}, u32[]{:S(2)}, u32[]{:S(2)}) async-start(bf16[48,32,1000]{2,0,1:T(8,128)(2,1)} %copy.31), calls=%async_computation | async-start | bytes 6291456 | tf_op jit(solution)/shard_map/all_to_all | solution.py:95
  28.0 198.7 %all-gather.2.cloned.1.call-start = ((), (), s32[]{:S(2)}) async-start(), calls=%async_computation.2 | async-start | bytes 7077888 | tf_op jit(solution)/shard_map/all_gather | solution.py:113
  28.3 31.9 %copy-start.9 = (s32[1000]{0:T(1024)}, s32[1000]{0:T(1024)S(1)}, u32[]{:S(2)}) copy-start(s32[1000]{0:T(1024)S(1)} %add_select_fusion.3) | copy-start | bytes 12004
  28.3 32.4 %copy-start.13 = (s32[1000]{0:T(1024)}, s32[1000]{0:T(1024)S(1)}, u32[]{:S(2)}) copy-start(s32[1000]{0:T(1024)S(1)} %get-tuple-element.24) | copy-start | bytes 12004
  28.3 32.9 %copy-start.11 = (s32[1000]{0:T(1024)}, s32[1000]{0:T(1024)S(1)}, u32[]{:S(2)}) copy-start(s32[1000]{0:T(1024)S(1)} %get-tuple-element.25) | copy-start | bytes 12004
  41.3 3.8 %copy-start.23 = (s32[8]{0:T(128)S(1)}, s32[8]{0:T(128)}, u32[]{:S(2)}) copy-start(s32[8]{0:T(128)} %param.19) | copy-start | bytes 100
  45.1 7.9 %copy-start.15 = (f32[3,10,10]{2,0,1:T(4,128)S(1)}, f32[3,10,10]{2,0,1:T(4,128)}, u32[]{:S(2)}) copy-start(f32[3,10,10]{2,0,1:T(4,128)} %param.17) | copy-start | bytes 3604
  45.1 7.8 %copy-start.17 = (pred[8]{0:T(512)(128)(4,1)}, pred[8]{0:T(512)(128)(4,1)S(1)}, u32[]{:S(2)}) copy-start(pred[8]{0:T(512)(128)(4,1)S(1)} %get-tuple-element.23) | copy-start | bytes 28
  45.3 7.6 %copy-start.24 = (s32[8,1]{0,1:T(1,128)}, s32[8,1]{0,1:T(1,128)S(1)}, u32[]{:S(2)}) copy-start(s32[8,1]{0,1:T(1,128)S(1)} %reduce-window.4) | copy-start | bytes 100
  45.9 13.8 %copy-start.22 = (f32[10,10]{1,0:T(8,128)S(1)}, f32[10,10]{1,0:T(8,128)}, u32[]{:S(2)}) copy-start(f32[10,10]{1,0:T(8,128)} %param.16) | copy-start | bytes 1204
  82.2 5.3 %copy-start.10 = (s32[1000]{0:T(1024)S(1)}, s32[1000]{0:T(1024)}, u32[]{:S(2)}) copy-start(s32[1000]{0:T(1024)} %copy-done.9) | copy-start | bytes 12004
  84.9 4.4 %copy-start.8 = (f32[1000,10]{0,1:T(8,128)S(1)}, f32[1000,10]{0,1:T(8,128)}, u32[]{:S(2)}) copy-start(f32[1000,10]{0,1:T(8,128)} %fusion.89) | copy-start | bytes 120004
  84.9 4.4 %copy-start.12 = (s32[1000]{0:T(1024)S(1)}, s32[1000]{0:T(1024)}, u32[]{:S(2)}) copy-start(s32[1000]{0:T(1024)} %copy-done.11) | copy-start | bytes 12004
  89.4 3.7 %copy-start.14 = (s32[1000]{0:T(1024)S(1)}, s32[1000]{0:T(1024)}, u32[]{:S(2)}) copy-start(s32[1000]{0:T(1024)} %copy-done.13) | copy-start | bytes 12004
  89.4 3.7 %copy-start.29 = (f32[1000,10]{0,1:T(8,128)S(1)}, f32[1000,10]{0,1:T(8,128)}, u32[]{:S(2)}) copy-start(f32[1000,10]{0,1:T(8,128)} %fusion.97) | copy-start | bytes 120004
  93.1 3.9 %copy-start.30 = (f32[1000,10]{0,1:T(8,128)S(1)}, f32[1000,10]{0,1:T(8,128)}, u32[]{:S(2)}) copy-start(f32[1000,10]{0,1:T(8,128)} %fusion.96) | copy-start | bytes 120004
  97.0 3.8 %copy-start.28 = (f32[1000,10]{0,1:T(8,128)S(1)}, f32[1000,10]{0,1:T(8,128)}, u32[]{:S(2)}) copy-start(f32[1000,10]{0,1:T(8,128)} %fusion.92) | copy-start | bytes 120004
  100.8 3.9 %copy-start.27 = (f32[1000,10]{0,1:T(8,128)S(1)}, f32[1000,10]{0,1:T(8,128)}, u32[]{:S(2)}) copy-start(f32[1000,10]{0,1:T(8,128)} %fusion.91) | copy-start | bytes 120004
  104.7 3.8 %copy-start.26 = (f32[1000,10]{0,1:T(8,128)S(1)}, f32[1000,10]{0,1:T(8,128)}, u32[]{:S(2)}) copy-start(f32[1000,10]{0,1:T(8,128)} %fusion.87) | copy-start | bytes 120004
  108.5 3.8 %copy-start.25 = (f32[1000,10]{0,1:T(8,128)S(1)}, f32[1000,10]{0,1:T(8,128)}, u32[]{:S(2)}) copy-start(f32[1000,10]{0,1:T(8,128)} %fusion.86) | copy-start | bytes 120004
  112.3 4.0 %copy-start.31 = (f32[1000,10]{0,1:T(8,128)S(1)}, f32[1000,10]{0,1:T(8,128)}, u32[]{:S(2)}) copy-start(f32[1000,10]{0,1:T(8,128)} %fusion.84) | copy-start | bytes 120004
  116.3 3.4 %copy-start.6 = (bf16[96,8,1000]{2,1,0:T(8,128)(2,1)S(1)}, bf16[96,8,1000]{2,1,0:T(8,128)(2,1)}, u32[]{:S(2)}) copy-start(bf16[96,8,1000]{2,1,0:T(8,128)(2,1)} %param.11) | copy-start | bytes 4608004
  131.2 3.4 %copy-start.3 = (bf16[48,32,1000]{2,1,0:T(8,128)(2,1)S(1)}, bf16[48,32,1000]{2,1,0:T(8,128)(2,1)}, u32[]{:S(2)}) copy-start(bf16[48,32,1000]{2,1,0:T(8,128)(2,1)} %get-tuple-element.12) | copy-start | bytes 9216004
  138.5 12.5 %copy-start.2 = (bf16[48,32,1000]{2,1,0:T(8,128)(2,1)S(1)}, bf16[48,32,1000]{2,1,0:T(8,128)(2,1)}, u32[]{:S(2)}) copy-start(bf16[48,32,1000]{2,1,0:T(8,128)(2,1)} %copy.32) | copy-start | bytes 9216004
  138.5 12.5 %copy-start.16 = (s32[48]{0:T(128)S(1)}, s32[48]{0:T(128)}, u32[]{:S(2)}) copy-start(s32[48]{0:T(128)} %eq.741) | copy-start | bytes 580
  138.5 115.3 %all-to-all-start.1 = ((bf16[48,32,1000]{2,0,1:T(8,128)(2,1)}), bf16[48,32,1000]{2,0,1:T(8,128)(2,1)}, u32[]{:S(2)}, u32[]{:S(2)}) async-start(bf16[48,32,1000]{2,0,1:T(8,128)(2,1)} %copy.39), calls=%async_computation.1 | async-start | bytes 6291456 | tf_op jit(solution)/shard_map/all_to_all | solution.py:99
  241.9 4.8 %copy-start.1 = (f32[1000,1000]{1,0:T(8,128)S(1)}, f32[1000,1000]{1,0:T(8,128)}, u32[]{:S(2)}) copy-start(f32[1000,1000]{1,0:T(8,128)} %multiply_multiply_fusion) | copy-start | bytes 12000004
  246.8 3.5 %copy-start.4 = (f32[768,1000]{0,1:T(8,128)}, f32[768,1000]{0,1:T(8,128)S(1)}, u32[]{:S(2)}) copy-start(f32[768,1000]{0,1:T(8,128)S(1)} %select_subtract_fusion) | copy-start | bytes 9216004
  253.8 3.7 %copy-start.7 = (bf16[48,8,1000]{2,1,0:T(8,128)(2,1)S(1)}, bf16[48,8,1000]{2,1,0:T(8,128)(2,1)}, u32[]{:S(2)}) copy-start(bf16[48,8,1000]{2,1,0:T(8,128)(2,1)} %get-tuple-element.16) | copy-start | bytes 2304004
  287.1 10.5 %copy-start.20 = (pred[8]{0:T(512)(128)(4,1)S(1)}, pred[8]{0:T(512)(128)(4,1)}, u32[]{:S(2)}) copy-start(pred[8]{0:T(512)(128)(4,1)} %iota_compare_fusion.39) | copy-start | bytes 28
  (3 other events, 7.3 us)
Sparse Core Ops, SparseCore 0:
  53.1 173.5 all-gather.1

commit v5 on v4

--- a/solution.py
+++ b/solution.py
@@ -91,7 +91,7 @@
     box_ids = lax.iota(jnp.int32, box_dev)
     send_hot = (slots[:, None] == box_ids[None, :]).astype(jnp.bfloat16)
     outgoing = pick(send_hot, orbitals)
-    half = orb_dev // 2
+    half = (orb_dev * 2) // 3
     incoming_a = lax.all_to_all(
         outgoing[:half], "box", split_axis=1, concat_axis=1, tiled=True
     )
@@ -132,8 +132,6 @@
 
     first = face_part(orbitals[:half], incoming_a)
     gathered, first = lax.optimization_barrier((gathered, first))
-    second = face_part(orbitals[half:], incoming_b)
-    kinetic = kinetic + jnp.concatenate([first, second], axis=0).reshape(rows, width)
     mixed = dot_f32(coupling, gathered).reshape(orb_dev, KEEP, width)
     spread = jnp.take(mixed, jnp.clip(rank, 0, KEEP - 1), axis=1)
     exchange = jnp.where(kept[None, :, None], spread, 0.0)
@@ -141,11 +139,19 @@
     weighted = local_values[None, :, :] * values - exchange
     coeffs_t = split_bf16(kron3(to_coeffs_mat, to_coeffs_mat, to_coeffs_mat).T)
     potential = apply_f32(weighted.reshape(rows, width), coeffs_t)
+    potential = potential.reshape(orb_dev, box_dev, width)
+    kinetic = kinetic.reshape(orb_dev, box_dev, width)
+    live = box_ids < box_counts[0]
 
-    total = (potential - 0.5 * kinetic).reshape(orb_dev, box_dev, width)
-    live = box_ids < box_counts[0]
-    total = jnp.where(live[None, :, None], total, 0.0)
-    return total.astype(jnp.bfloat16)
+    def finish(pot, kin):
+        total = jnp.where(live[None, :, None], pot - 0.5 * kin, 0.0)
+        return total.astype(jnp.bfloat16)
+
+    head = finish(potential[:half], kinetic[:half] + first)
+    head, incoming_b = lax.optimization_barrier((head, incoming_b))
+    second = face_part(orbitals[half:], incoming_b)
+    tail = finish(potential[half:], kinetic[half:] + second)
+    return jnp.concatenate([head, tail], axis=0)
 
 
 def solution(mesh):

time: 311 us -> 307 us (0.987)
  the two profiles are of different devices: /device:TPU:90 before, /device:TPU:64 now
where the time goes in v5:
time: 307 us; the launch traced here: 302 us
  matrix products  138 us (45%)
  waiting for transfers between devices  55.3 us (18%)
  local copies, waits for them, and re-layouts  52.4 us (17%)
  starting transfers between devices  30.8 us (10%)
  between operations  14.7 us (5%)
  other arithmetic  11.3 us (4%)
    all_to_all x1, waiting for transfers between devices, shards(): lax.all_to_all(outgoing[:half], 'box', split_axis=1, concat_axis=1, tiled...  55.2 us
    dot_general x30, matrix products, expand(): return jnp.dot(jnp.dot(left, mat, precision=hp), right, precision=hp)  50.9 us
    dot_general x2, matrix products, face_part(): jnp.einsum('nfbc,fcd->nbd', moved, face_hi, preferred_element_type=jnp.fl...  26.9 us
    dot_general x2, matrix products, face_part(): jnp.einsum('nfbc,fcd->nbd', moved, face_lo, preferred_element_type=jnp.fl...  26.2 us
    dot_general x8, matrix products, dot_f32(): return jnp.dot(a, b, preferred_element_type=jnp.float32)  19.6 us
    all_to_all x1, starting transfers between devices, shards(): lax.all_to_all(later, 'box', split_axis=1, concat_axis=1, tiled=True)  18.1 us
    dot_general x4, matrix products, pick(): jnp.einsum('sb,nbc->nsc', onehot, block, preferred_element_type=jnp.float32)  14.4 us
    all_to_all x1, starting transfers between devices, shards(): lax.all_to_all(outgoing[:half], 'box', split_axis=1, concat_axis=1, tiled...  12.4 us
  transfers between devices with their start and end apart: 3, of which 1 were waited for; matrix products, arithmetic and copies ran while one was open for 53% of the time, Pallas kernels for 0%

profile of v5, /device:TPU:64, one launch (start us, length us, event | category | flops | bytes accessed | tf_op | source)
XLA Modules:
  0.0 302.4 jit_solution(14367921388876557911)
XLA Ops:
  6.5 3.3 %convert_bitcast_fusion = bf16[96,32,1000]{2,1,0:T(8,128)(2,1)S(1)} fusion(bf16[96,8,1000]{2,1,0:T(8,128)(2,1)} %param.11, s32[32]{0:T(128)} %bitcast.220), kind=kOutput, calls=%fused_computation.28 | convolution fusion | flops 52224256 | bytes 7680128 | tf_op jit(solution)/shard_map/sb,nbc->nsc/dot_general | solution.py:67
  12.7 4.3 %copy.35 = bf16[64,32,1000]{2,0,1:T(8,128)(2,1)} copy(bf16[64,32,1000]{2,1,0:T(8,128)(2,1)S(1)} %slice.67) | data formatting | bytes 8192000 | tf_op jit(solution)/shard_map/slice | solution.py:96
  16.9 12.4 %all-to-all-start = ((bf16[64,32,1000]{2,0,1:T(8,128)(2,1)}), bf16[64,32,1000]{2,0,1:T(8,128)(2,1)}, u32[]{:S(2)}, u32[]{:S(2)}) async-start(bf16[64,32,1000]{2,0,1:T(8,128)(2,1)} %copy.35), calls=%async_computation | async-start | bytes 8388608 | tf_op jit(solution)/shard_map/all_to_all | solution.py:95
  39.1 3.6 %add_bitcast_fusion.1 = f32[768,1000]{0,1:T(8,128)} fusion(f32[1000,768]{1,0:T(8,128)S(1)} %fusion.57, f32[1000,1000]{1,0:T(8,128)S(1)} %multiply_multiply_fusion.1, bf16[96,8,1000]{2,1,0:T(8,128)(2,1)S(1)} %copy-done.4), kind=kOutput, calls=%fused_computation.74 | convolution fusion | flops 1538768000 | bytes 11680000 | tf_op jit(solution)/shard_map/dot_general | solution.py:50
  45.3 3.0 fusion.112
  48.2 3.5 %reshape.170 = bf16[96,4000]{1,0:T(8,128)(2,1)} reshape(bf16[96,4,1000]{2,1,0:T(4,128)(2,1)} %fusion.112) | data formatting | bytes 1536000 | tf_op jit(solution)/shard_map/reshape | solution.py:114
  56.9 3.2 %fusion.23 = f32[1000,1000]{1,0:T(8,128)S(1)} fusion(f32[1000,1000]{1,0:T(8,128)S(1)} %fusion.154, f32[1000,1000]{1,0:T(8,128)S(1)} %fusion.151, f32[1000,10]{0,1:T(8,128)S(1)} %fusion.121, s32[1000]{0:T(1024)S(1)} %add_select_fusion.3, s32[1000]{0:T(1024)S(1)} %get-tuple-element.25, s32[1000]{0:T(1024)S(1)} %get-tuple-element.24), kind=kOutput, calls=%fused_computation.54 | convolution fusion | flops 131010000 | bytes 12052000 | tf_op jit(solution)/shard_map/dot_general | solution.py:21
  67.0 2.6 copy.33
  69.6 3.0 copy.44
  82.8 3.8 %fusion.15 = f32[6,1000,1000]{2,1,0:T(8,128)} fusion(f32[1000,10]{0,1:T(8,128)S(1)} %fusion.134, s32[1000]{0:T(1024)S(1)} %get-tuple-element.25, s32[1000]{0:T(1024)S(1)} %get-tuple-element.24, s32[1000]{0:T(1024)S(1)} %add_select_fusion.3), kind=kOutput, calls=%fused_computation.46 | convolution fusion | flops 124010000 | bytes 4182016 | tf_op jit(solution)/shard_map/dot_general | solution.py:21
  86.6 3.8 %fusion.17 = f32[6,1000,1000]{2,1,0:T(8,128)} fusion(f32[6,1000,1000]{2,1,0:T(8,128)} %fusion.15, f32[1000,10]{0,1:T(8,128)S(1)} %fusion.133, s32[1000]{0:T(1024)S(1)} %get-tuple-element.25, s32[1000]{0:T(1024)S(1)} %get-tuple-element.24, s32[1000]{0:T(1024)S(1)} %add_select_fusion.3), kind=kOutput, calls=%fused_computation.48 | convolution fusion | flops 124010000 | bytes 4182016 | tf_op jit(solution)/shard_map/dot_general | solution.py:21
  90.4 3.8 %fusion.19 = f32[6,1000,1000]{2,1,0:T(8,128)} fusion(f32[6,1000,1000]{2,1,0:T(8,128)} %fusion.17, f32[1000,10]{0,1:T(8,128)S(1)} %fusion.129, s32[1000]{0:T(1024)S(1)} %add_select_fusion.3, s32[1000]{0:T(1024)S(1)} %get-tuple-element.24, s32[1000]{0:T(1024)S(1)} %get-tuple-element.25), kind=kOutput, calls=%fused_computation.50 | convolution fusion | flops 124010000 | bytes 4182016 | tf_op jit(solution)/shard_map/dot_general | solution.py:21
  94.2 3.8 %fusion.21 = f32[6,1000,1000]{2,1,0:T(8,128)} fusion(f32[6,1000,1000]{2,1,0:T(8,128)} %fusion.19, f32[1000,10]{0,1:T(8,128)S(1)} %fusion.128, s32[1000]{0:T(1024)S(1)} %add_select_fusion.3, s32[1000]{0:T(1024)S(1)} %get-tuple-element.24, s32[1000]{0:T(1024)S(1)} %get-tuple-element.25), kind=kOutput, calls=%fused_computation.52 | convolution fusion | flops 124010000 | bytes 4182016 | tf_op jit(solution)/shard_map/dot_general | solution.py:21
  97.9 4.0 %fusion.25 = f32[6,1000,1000]{2,1,0:T(8,128)} fusion(f32[6,1000,1000]{2,1,0:T(8,128)} %fusion.21, f32[1000,10]{0,1:T(8,128)S(1)} %fusion.124, s32[1000]{0:T(1024)S(1)} %add_select_fusion.3, s32[1000]{0:T(1024)S(1)} %get-tuple-element.25, s32[1000]{0:T(1024)S(1)} %get-tuple-element.24), kind=kOutput, calls=%fused_computation.56 | convolution fusion | flops 124010000 | bytes 4182016 | tf_op jit(solution)/shard_map/dot_general | solution.py:21
  101.9 3.8 %fusion.27 = f32[6,1000,1000]{2,1,0:T(8,128)} fusion(f32[6,1000,1000]{2,1,0:T(8,128)} %fusion.25, f32[1000,10]{0,1:T(8,128)S(1)} %fusion.123, s32[1000]{0:T(1024)S(1)} %add_select_fusion.3, s32[1000]{0:T(1024)S(1)} %get-tuple-element.25, s32[1000]{0:T(1024)S(1)} %get-tuple-element.24), kind=kOutput, calls=%fused_computation.58 | convolution fusion | flops 124010000 | bytes 4182016 | tf_op jit(solution)/shard_map/dot_general | solution.py:21
  105.7 4.1 %multiply_multiply_fusion = f32[1000,1000]{1,0:T(8,128)} fusion(f32[1000,1000]{1,0:T(8,128)S(1)} %fusion.155, f32[1000,1000]{1,0:T(8,128)S(1)} %fusion.152, f32[1000,10]{0,1:T(8,128)S(1)} %fusion.122, s32[1000]{0:T(1024)S(1)} %get-tuple-element.24), kind=kOutput, calls=%fused_computation.59 | convolution fusion | flops 122010000 | bytes 12044000 | tf_op jit(solution)/shard_map/dot_general | solution.py:21
  109.8 55.2 %all-to-all-done = bf16[64,32,1000]{2,0,1:T(8,128)(2,1)} async-done(((bf16[64,32,1000]{2,0,1:T(8,128)(2,1)}), bf16[64,32,1000]{2,0,1:T(8,128)(2,1)}, u32[]{:S(2)}, u32[]{:S(2)}) %all-to-all-start) | async-done | bytes 4096032 | tf_op jit(solution)/shard_map/all_to_all | solution.py:95
  165.1 6.5 %copy.36 = bf16[64,32,1000]{2,1,0:T(8,128)(2,1)} copy(bf16[64,32,1000]{2,0,1:T(8,128)(2,1)} %all-to-all-done) | data formatting | bytes 8192000 | tf_op jit(solution)/shard_map/optimization_barrier | solution.py:98
  174.0 18.1 %all-to-all-start.1 = ((bf16[32,32,1000]{2,0,1:T(8,128)(2,1)}), bf16[32,32,1000]{2,0,1:T(8,128)(2,1)}, u32[]{:S(2)}, u32[]{:S(2)}) async-start(bf16[32,32,1000]{2,0,1:T(8,128)(2,1)} %copy.45), calls=%async_computation.1 | async-start | bytes 4194304 | tf_op jit(solution)/shard_map/all_to_all | solution.py:99
  192.2 7.0 %fusion.28 = bf16[64,1000,48]{1,2,0:T(8,128)(2,1)} fusion(bf16[64,32,1000]{2,1,0:T(8,128)(2,1)} %copy.36, bf16[64,8,1000]{2,1,0:T(8,128)(2,1)S(1)} %slice-done.1, s32[48]{0:T(128)S(1)} %eq.741), kind=kOutput, calls=%fused_computation.61 | convolution fusion | flops 259073920 | bytes 11264192 | tf_op jit(solution)/shard_map/sb,nbc->nsc/dot_general | solution.py:67
  199.2 13.3 %fusion.3 = f32[64,8,1000,1]{2,1,3,0:T(8,128)S(1)} fusion(bf16[64,1000,48]{1,2,0:T(8,128)(2,1)} %fusion.28, f32[6,1000,1000]{2,1,0:T(8,128)} %fusion.27), kind=kOutput, calls=%fused_computation.24 | convolution fusion | flops 6161999872 | bytes 32192000 | tf_op jit(solution)/shard_map/nfbc,fcd->nbd/dot_general | solution.py:131
  212.5 14.7 %bitcast_add_fusion.1 = f32[64,8,1000]{2,1,0:T(8,128)} fusion(f32[64,8,1000,1]{2,1,3,0:T(8,128)S(1)} %fusion.3, f32[6,1000,1000]{2,1,0:T(8,128)} %fusion.27, bf16[64,1000,48]{1,2,0:T(8,128)(2,1)} %fusion.28), kind=kOutput, calls=%fused_computation.85 | convolution fusion | flops 6156512256 | bytes 34240000 | tf_op jit(solution)/shard_map/nfbc,fcd->nbd/dot_general | solution.py:129
  227.2 3.9 %convolution_bitcast_fusion = f32[96,4000]{1,0:T(8,128)S(1)} fusion(bf16[96,768]{1,0:T(8,128)(2,1)S(1)} %copy-done, bf16[768,4000]{1,0:T(8,128)(2,1)} %all-gather.2.cloned.1.call-done), kind=kOutput, calls=%fused_computation.39 | convolution fusion | flops 589824000 | bytes 7827456 | tf_op jit(solution)/shard_map/dot_general | solution.py:50
  236.1 3.7 %copy.69 = f32[96,8,1000]{2,1,0:T(8,128)S(1)} copy(f32[96,8,1000]{2,0,1:T(8,128)} %bitcast.218) | data formatting | bytes 6144000 | tf_op jit(solution)/shard_map/jit(_take)/gather | solution.py:136
  239.8 2.6 copy.41
  242.4 4.4 %select_subtract_fusion = f32[768,1000]{0,1:T(8,128)S(1)} fusion(f32[768,1000]{0,1:T(8,128)} %copy.41, f32[768,1000]{0,1:T(8,128)} %copy.33, f32[768,1000]{0,1:T(8,128)} %add_bitcast_fusion.1, pred[768]{0:T(1024)(128)(4,1)S(1)} %broadcast_in_dim.56, pred[768]{0:T(1024)(128)(4,1)S(1)} %broadcast_in_dim.53), kind=kLoop, calls=%fused_computation.73 | loop fusion | flops 3072000 | bytes 12289536 | tf_op jit(solution)/shard_map/sub | solution.py:139
  255.2 3.2 %copy.42 = f32[512,1000]{1,0:T(8,128)} copy(f32[512,1000]{0,1:T(8,128)} %slice.68) | data formatting | bytes 4096000 | tf_op jit(solution)/shard_map/slice | solution.py:150
  259.7 4.1 %fusion.52 = bf16[64,8,1000]{2,1,0:T(8,128)(2,1)} fusion(f32[64,8,1000]{2,1,0:T(8,128)} %bitcast_add_fusion.1, f32[512,1000]{1,0:T(8,128)S(1)} %copy-done.3, f32[512,1000]{1,0:T(8,128)} %copy.42, pred[8]{0:T(512)(128)(4,1)S(1)} %iota_compare_fusion.39), kind=kLoop, calls=%fused_computation.84 | loop fusion | flops 2560000 | bytes 7168008 | tf_op jit(solution)/shard_map/convert_element_type | solution.py:148
  263.8 2.7 copy.48
  267.7 12.9 %fusion.77 = f32[32,8,1000]{2,1,0:T(8,128)} fusion(f32[6,1000,1000]{2,1,0:T(8,128)} %fusion.27, bf16[32,1000,48]{1,2,0:T(8,128)(2,1)S(1)} %fusion.46), kind=kOutput, calls=%fused_computation.101 | convolution fusion | flops 3089999872 | bytes 28096000 | tf_op jit(solution)/shard_map/nfbc,fcd->nbd/dot_general | solution.py:131
  280.6 12.2 %fusion.115 = bf16[32,8,1000]{2,1,0:T(8,128)(2,1)S(1)} fusion(f32[32,8,1000]{2,1,0:T(8,128)} %fusion.77, f32[6,1000,1000]{2,1,0:T(8,128)} %fusion.27, bf16[32,1000,48]{1,2,0:T(8,128)(2,1)S(1)} %fusion.46, f32[256,1000]{1,0:T(8,128)S(1)} %copy-done.6, f32[256,1000]{1,0:T(8,128)} %copy.46, pred[8]{0:T(512)(128)(4,1)S(1)} %iota_compare_fusion.39), kind=kOutput, calls=%fused_computation.109 | convolution fusion | flops 3085536000 | bytes 30656008 | tf_op jit(solution)/shard_map/nfbc,fcd->nbd/dot_general | solution.py:129
  292.8 2.5 pad_maximum_fusion
  (95 shorter events, 54.7 us)
Async XLA Ops:
  6.5 220.7 %copy-start = (bf16[96,768]{1,0:T(8,128)(2,1)S(1)}, bf16[96,768]{1,0:T(8,128)(2,1)}, u32[]{:S(2)}) copy-start(bf16[96,768]{1,0:T(8,128)(2,1)} %param.14) | copy-start | bytes 442372
  9.8 2.8 copy-start.1
  16.9 12.7 %copy-start.11 = (f32[10,10]{1,0:T(8,128)S(1)}, f32[10,10]{1,0:T(8,128)}, u32[]{:S(2)}) copy-start(f32[10,10]{1,0:T(8,128)} %param.15) | copy-start | bytes 1204
  16.9 148.1 %all-to-all-start = ((bf16[64,32,1000]{2,0,1:T(8,128)(2,1)}), bf16[64,32,1000]{2,0,1:T(8,128)(2,1)}, u32[]{:S(2)}, u32[]{:S(2)}) async-start(bf16[64,32,1000]{2,0,1:T(8,128)(2,1)} %copy.35), calls=%async_computation | async-start | bytes 8388608 | tf_op jit(solution)/shard_map/all_to_all | solution.py:95
  29.3 197.8 %all-gather.2.cloned.1.call-start = ((), (), s32[]{:S(2)}) async-start(), calls=%async_computation.2 | async-start | bytes 7077888 | tf_op jit(solution)/shard_map/all_gather | solution.py:113
  34.8 2.2 copy-start.4
  42.7 2.4 copy-start.13
  45.0 6.7 %copy-start.9 = (f32[3,10,10]{2,0,1:T(4,128)S(1)}, f32[3,10,10]{2,0,1:T(4,128)}, u32[]{:S(2)}) copy-start(f32[3,10,10]{2,0,1:T(4,128)} %param.17) | copy-start | bytes 3604
  56.9 3.2 %copy-start.5 = (bf16[96,8,1000]{2,1,0:T(8,128)(2,1)S(1)}, bf16[96,8,1000]{2,1,0:T(8,128)(2,1)}, u32[]{:S(2)}) copy-start(bf16[96,8,1000]{2,1,0:T(8,128)(2,1)} %param.11) | copy-start | bytes 4608004
  64.0 2.3 copy-start.7
  64.0 2.3 copy-start.10
  64.0 2.6 copy-start.8
  69.6 3.6 %slice-start.3 = ((f32[768,1000]{0,1:T(8,128)}), f32[256,1000]{0,1:T(8,128)S(1)}, s32[]{:S(2)}) async-start(f32[768,1000]{0,1:T(8,128)} %copy-done.7), calls=%async_computation.6 | async-start | bytes 2048000 | tf_op jit(solution)/shard_map/slice | solution.py:153
  69.6 8.0 %copy-start.12 = (f32[10,10]{1,0:T(8,128)S(1)}, f32[10,10]{1,0:T(8,128)}, u32[]{:S(2)}) copy-start(f32[10,10]{1,0:T(8,128)} %param.16) | copy-start | bytes 1204
  109.8 61.7 %slice-start = ((bf16[96,32,1000]{2,1,0:T(8,128)(2,1)}), bf16[32,32,1000]{2,1,0:T(8,128)(2,1)S(1)}, s32[]{:S(2)}) async-start(bf16[96,32,1000]{2,1,0:T(8,128)(2,1)} %copy-done.1), calls=%async_computation.3 | async-start | bytes 4194304 | tf_op jit(solution)/shard_map/slice | solution.py:98
  171.6 20.6 %slice-start.1 = ((bf16[96,8,1000]{2,1,0:T(8,128)(2,1)}), bf16[64,8,1000]{2,1,0:T(8,128)(2,1)S(1)}, s32[]{:S(2)}) async-start(bf16[96,8,1000]{2,1,0:T(8,128)(2,1)} %param.11), calls=%async_computation.4 | async-start | bytes 2097152 | tf_op jit(solution)/shard_map/slice | solution.py:133
  174.0 89.8 %all-to-all-start.1 = ((bf16[32,32,1000]{2,0,1:T(8,128)(2,1)}), bf16[32,32,1000]{2,0,1:T(8,128)(2,1)}, u32[]{:S(2)}, u32[]{:S(2)}) async-start(bf16[32,32,1000]{2,0,1:T(8,128)(2,1)} %copy.45), calls=%async_computation.1 | async-start | bytes 4194304 | tf_op jit(solution)/shard_map/all_to_all | solution.py:99
  242.4 4.8 %copy-start.2 = (f32[1000,1000]{1,0:T(8,128)S(1)}, f32[1000,1000]{1,0:T(8,128)}, u32[]{:S(2)}) copy-start(f32[1000,1000]{1,0:T(8,128)} %multiply_multiply_fusion) | copy-start | bytes 12000004
  255.1 4.6 %copy-start.3 = (f32[512,1000]{1,0:T(8,128)S(1)}, f32[512,1000]{1,0:T(8,128)}, u32[]{:S(2)}) copy-start(f32[512,1000]{1,0:T(8,128)} %copy.44) | copy-start | bytes 6144004
  259.7 6.8 %slice-start.2 = ((bf16[96,8,1000]{2,1,0:T(8,128)(2,1)}), bf16[32,8,1000]{2,1,0:T(8,128)(2,1)S(1)}, s32[]{:S(2)}) async-start(bf16[96,8,1000]{2,1,0:T(8,128)(2,1)} %param.11), calls=%async_computation.5 | async-start | bytes 1048576 | tf_op jit(solution)/shard_map/slice | solution.py:152
  267.7 12.9 %copy-start.6 = (f32[256,1000]{1,0:T(8,128)S(1)}, f32[256,1000]{1,0:T(8,128)}, u32[]{:S(2)}) copy-start(f32[256,1000]{1,0:T(8,128)} %copy.47) | copy-start | bytes 3072004
Sparse Core Ops, SparseCore 0:
  51.9 146.9 all-gather.1

commit v6 on v5

--- a/solution.py
+++ b/solution.py
@@ -110,9 +110,18 @@
         kept[None, :, None], exchange_values.astype(jnp.float32) * values, 0.0
     ).astype(jnp.bfloat16)
     compact = pick(sel.astype(jnp.bfloat16), products)
-    gathered = lax.all_gather(
-        compact.reshape(orb_dev, KEEP * width), "orb", axis=0, tiled=True
+    n_orb = coupling.shape[1] // orb_dev
+    chips = n_orb // 2
+    same_core = [[chip * 2 + core for chip in range(chips)] for core in range(2)]
+    mates = [[chip * 2, chip * 2 + 1] for chip in range(chips)]
+    across = lax.all_gather(
+        compact.reshape(orb_dev, KEEP * width), "orb", axis=0,
+        axis_index_groups=same_core,
     )
+    both = lax.all_gather(across, "orb", axis=0, axis_index_groups=mates)
+    gathered = both.reshape(n_orb * orb_dev, KEEP * width)
+    coupling = coupling.reshape(orb_dev, chips, 2, orb_dev).transpose(0, 2, 1, 3)
+    coupling = coupling.reshape(orb_dev, n_orb * orb_dev)
     lap0 = laplace_blocks[0]
     centre = sum(at_place(lap0, width, place) for place in range(3))
     kinetic = apply_bf16(flat, split_bf16(centre.T))

time: 307 us -> 340 us (1.11)
  waiting for transfers between devices: 55.3 us -> 67.6 us
  matrix products: 138 us -> 146 us
  starting transfers between devices: 30.8 us -> 38.4 us
    all_gather x1 -> x2, waiting for transfers between devices: 0.02 us -> 67.6 us  [the longest x1 67.5 us: shards(): lax.all_gather(compact.reshape(orb_dev, KEEP * width), 'orb', axis=0, axi...]
    all_to_all x1, waiting for transfers between devices: 55.2 us -> 0.01 us  [shards(): lax.all_to_all(outgoing[:half], 'box', split_axis=1, concat_axis=1, tiled...]
    all_to_all x1, starting transfers between devices: 18.1 us -> 25.3 us  [shards(): lax.all_to_all(later, 'box', split_axis=1, concat_axis=1, tiled=True)]
    dot_general x30, matrix products: 50.9 us -> 57.5 us  [expand(): return jnp.dot(jnp.dot(left, mat, precision=hp), right, precision=hp)]
  transfers between devices with their start and end apart: 3 -> 4, of which waited for: 1 -> 1; matrix products, arithmetic and copies ran while one was open for 53% -> 51% of each run, Pallas kernels for 0% -> 0%
where the time goes in v6:
time: 340 us; the launch traced here: 334 us
  matrix products  146 us (43%)
  waiting for transfers between devices  67.6 us (20%)
  local copies, waits for them, and re-layouts  55.5 us (16%)
  starting transfers between devices  38.4 us (11%)
  between operations  14.7 us (4%)
  other arithmetic  11.3 us (3%)
    all_gather x1, waiting for transfers between devices, shards(): lax.all_gather(compact.reshape(orb_dev, KEEP * width), 'orb', axis=0, axi...  67.5 us
    dot_general x30, matrix products, expand(): return jnp.dot(jnp.dot(left, mat, precision=hp), right, precision=hp)  57.5 us
    dot_general x2, matrix products, face_part(): jnp.einsum('nfbc,fcd->nbd', moved, face_hi, preferred_element_type=jnp.fl...  26.8 us
    dot_general x2, matrix products, face_part(): jnp.einsum('nfbc,fcd->nbd', moved, face_lo, preferred_element_type=jnp.fl...  26.2 us
    all_to_all x1, starting transfers between devices, shards(): lax.all_to_all(later, 'box', split_axis=1, concat_axis=1, tiled=True)  25.3 us
    dot_general x8, matrix products, dot_f32(): return jnp.dot(a, b, preferred_element_type=jnp.float32)  21.2 us
    dot_general x4, matrix products, pick(): jnp.einsum('sb,nbc->nsc', onehot, block, preferred_element_type=jnp.float32)  14.4 us
    all_to_all x1, starting transfers between devices, shards(): lax.all_to_all(outgoing[:half], 'box', split_axis=1, concat_axis=1, tiled...  12.4 us
  transfers between devices with their start and end apart: 4, of which 1 were waited for; matrix products, arithmetic and copies ran while one was open for 51% of the time, Pallas kernels for 0%

profile of v6, /device:TPU:64, one launch (start us, length us, event | category | flops | bytes accessed | tf_op | source)
XLA Modules:
  0.0 333.6 jit_solution(6574568432691290473)
XLA Ops:
  6.5 3.3 convert_bitcast_fusion
  12.6 4.2 %copy.36 = bf16[64,32,1000]{2,0,1:T(8,128)(2,1)} copy(bf16[64,32,1000]{2,1,0:T(8,128)(2,1)S(1)} %slice.67) | data formatting | bytes 8192000 | tf_op jit(solution)/shard_map/slice | solution.py:96
  16.9 12.4 %all-to-all-start = ((bf16[64,32,1000]{2,0,1:T(8,128)(2,1)}), bf16[64,32,1000]{2,0,1:T(8,128)(2,1)}, u32[]{:S(2)}, u32[]{:S(2)}) async-start(bf16[64,32,1000]{2,0,1:T(8,128)(2,1)} %copy.36), calls=%async_computation | async-start | bytes 8388608 | tf_op jit(solution)/shard_map/all_to_all | solution.py:95
  39.0 3.6 %add_bitcast_fusion.1 = f32[768,1000]{0,1:T(8,128)} fusion(f32[1000,768]{1,0:T(8,128)S(1)} %fusion.57, f32[1000,1000]{1,0:T(8,128)S(1)} %multiply_multiply_fusion.1, bf16[96,8,1000]{2,1,0:T(8,128)(2,1)S(1)} %copy-done.7), kind=kOutput, calls=%fused_computation.74 | convolution fusion | flops 1538768000 | bytes 11680000 | tf_op jit(solution)/shard_map/dot_general | solution.py:50
  45.3 3.0 fusion.112
  48.2 3.1 all_gather_reshape.3
  61.4 3.7 %fusion.152 = f32[1000,1000]{1,0:T(8,128)} fusion(f32[1000,10]{0,1:T(8,128)S(1)} %fusion.127, s32[1000]{0:T(1024)S(1)} %get-tuple-element.25), kind=kOutput, calls=%fused_computation.148 | convolution fusion | flops 120010000 | bytes 4044000 | tf_op jit(solution)/shard_map/dot_general | solution.py:21
  65.2 3.8 %fusion.155 = f32[1000,1000]{1,0:T(8,128)} fusion(f32[1000,10]{0,1:T(8,128)S(1)} %fusion.132, s32[1000]{0:T(1024)S(1)} %add_select_fusion.3), kind=kOutput, calls=%fused_computation.152 | convolution fusion | flops 120010000 | bytes 4044000 | tf_op jit(solution)/shard_map/dot_general | solution.py:21
  72.6 4.0 %fusion.15 = f32[6,1000,1000]{2,1,0:T(8,128)} fusion(f32[1000,10]{0,1:T(8,128)S(1)} %fusion.134, s32[1000]{0:T(1024)S(1)} %get-tuple-element.25, s32[1000]{0:T(1024)S(1)} %get-tuple-element.24, s32[1000]{0:T(1024)S(1)} %add_select_fusion.3), kind=kOutput, calls=%fused_computation.46 | convolution fusion | flops 124010000 | bytes 4182016 | tf_op jit(solution)/shard_map/dot_general | solution.py:21
  76.6 3.9 %fusion.17 = f32[6,1000,1000]{2,1,0:T(8,128)} fusion(f32[6,1000,1000]{2,1,0:T(8,128)} %fusion.15, f32[1000,10]{0,1:T(8,128)S(1)} %fusion.133, s32[1000]{0:T(1024)S(1)} %get-tuple-element.25, s32[1000]{0:T(1024)S(1)} %get-tuple-element.24, s32[1000]{0:T(1024)S(1)} %add_select_fusion.3), kind=kOutput, calls=%fused_computation.48 | convolution fusion | flops 124010000 | bytes 4182016 | tf_op jit(solution)/shard_map/dot_general | solution.py:21
  80.5 3.8 %fusion.19 = f32[6,1000,1000]{2,1,0:T(8,128)} fusion(f32[6,1000,1000]{2,1,0:T(8,128)} %fusion.17, f32[1000,10]{0,1:T(8,128)S(1)} %fusion.129, s32[1000]{0:T(1024)S(1)} %add_select_fusion.3, s32[1000]{0:T(1024)S(1)} %get-tuple-element.24, s32[1000]{0:T(1024)S(1)} %get-tuple-element.25), kind=kOutput, calls=%fused_computation.50 | convolution fusion | flops 124010000 | bytes 4182016 | tf_op jit(solution)/shard_map/dot_general | solution.py:21
  84.2 3.1 fusion.23
  89.3 3.5 %add_bitcast_fusion = f32[768,1000]{0,1:T(8,128)} fusion(f32[1000,768]{1,0:T(8,128)S(1)} %fusion.53, f32[1000,1000]{1,0:T(8,128)S(1)} %fusion.23, bf16[96,8,1000]{2,1,0:T(8,128)(2,1)S(1)} %copy-done.8), kind=kOutput, calls=%fused_computation.71 | convolution fusion | flops 1538768000 | bytes 11680000 | tf_op jit(solution)/shard_map/dot_general | solution.py:50
  92.9 67.5 %all-gather.4.cloned.1.call-done = bf16[4,96,4000]{2,1,0:T(8,128)(2,1)} async-done(((bf16[1,96,4000]{2,1,0:T(8,128)(2,1)}), bf16[4,96,4000]{2,1,0:T(8,128)(2,1)}) %all-gather.4.cloned.1.call-update) | async-done | bytes 3072016 | tf_op jit(solution)/shard_map/all_gather | solution.py:117
  168.7 3.0 copy.46
  173.0 4.0 %fusion.21 = f32[6,1000,1000]{2,1,0:T(8,128)} fusion(f32[6,1000,1000]{2,1,0:T(8,128)} %fusion.19, f32[1000,10]{0,1:T(8,128)S(1)} %copy-done.20, s32[1000]{0:T(1024)S(1)} %add_select_fusion.3, s32[1000]{0:T(1024)S(1)} %get-tuple-element.24, s32[1000]{0:T(1024)S(1)} %get-tuple-element.25), kind=kOutput, calls=%fused_computation.52 | convolution fusion | flops 124010000 | bytes 4182016 | tf_op jit(solution)/shard_map/dot_general | solution.py:21
  177.0 3.8 %fusion.25 = f32[6,1000,1000]{2,1,0:T(8,128)} fusion(f32[6,1000,1000]{2,1,0:T(8,128)} %fusion.21, f32[1000,10]{0,1:T(8,128)S(1)} %copy-done.18, s32[1000]{0:T(1024)S(1)} %add_select_fusion.3, s32[1000]{0:T(1024)S(1)} %get-tuple-element.25, s32[1000]{0:T(1024)S(1)} %get-tuple-element.24), kind=kOutput, calls=%fused_computation.56 | convolution fusion | flops 124010000 | bytes 4182016 | tf_op jit(solution)/shard_map/dot_general | solution.py:21
  180.8 3.8 %fusion.27 = f32[6,1000,1000]{2,1,0:T(8,128)} fusion(f32[6,1000,1000]{2,1,0:T(8,128)} %fusion.25, f32[1000,10]{0,1:T(8,128)S(1)} %copy-done.19, s32[1000]{0:T(1024)S(1)} %add_select_fusion.3, s32[1000]{0:T(1024)S(1)} %get-tuple-element.25, s32[1000]{0:T(1024)S(1)} %get-tuple-element.24), kind=kOutput, calls=%fused_computation.58 | convolution fusion | flops 124010000 | bytes 4182016 | tf_op jit(solution)/shard_map/dot_general | solution.py:21
  184.6 4.1 %multiply_multiply_fusion = f32[1000,1000]{1,0:T(8,128)} fusion(f32[1000,1000]{1,0:T(8,128)S(1)} %copy-done.4, f32[1000,1000]{1,0:T(8,128)S(1)} %copy-done.3, f32[1000,10]{0,1:T(8,128)S(1)} %copy-done.12, s32[1000]{0:T(1024)S(1)} %get-tuple-element.24), kind=kOutput, calls=%fused_computation.59 | convolution fusion | flops 122010000 | bytes 12044000 | tf_op jit(solution)/shard_map/dot_general | solution.py:21
  188.8 7.0 %copy.37 = bf16[64,32,1000]{2,1,0:T(8,128)(2,1)} copy(bf16[64,32,1000]{2,0,1:T(8,128)(2,1)} %all-to-all-done) | data formatting | bytes 8192000 | tf_op jit(solution)/shard_map/optimization_barrier | solution.py:98
  198.3 25.3 %all-to-all-start.1 = ((bf16[32,32,1000]{2,0,1:T(8,128)(2,1)}), bf16[32,32,1000]{2,0,1:T(8,128)(2,1)}, u32[]{:S(2)}, u32[]{:S(2)}) async-start(bf16[32,32,1000]{2,0,1:T(8,128)(2,1)} %copy.47), calls=%async_computation.1 | async-start | bytes 4194304 | tf_op jit(solution)/shard_map/all_to_all | solution.py:99
  223.6 7.0 %fusion.28 = bf16[64,1000,48]{1,2,0:T(8,128)(2,1)} fusion(bf16[64,32,1000]{2,1,0:T(8,128)(2,1)} %copy.37, bf16[64,8,1000]{2,1,0:T(8,128)(2,1)S(1)} %slice-done.1, s32[48]{0:T(128)S(1)} %eq.741), kind=kOutput, calls=%fused_computation.61 | convolution fusion | flops 259073920 | bytes 11264192 | tf_op jit(solution)/shard_map/sb,nbc->nsc/dot_general | solution.py:67
  230.6 13.3 %fusion.3 = f32[64,8,1000,1]{2,1,3,0:T(8,128)S(1)} fusion(bf16[64,1000,48]{1,2,0:T(8,128)(2,1)} %fusion.28, f32[6,1000,1000]{2,1,0:T(8,128)} %fusion.27), kind=kOutput, calls=%fused_computation.24 | convolution fusion | flops 6161999872 | bytes 32192000 | tf_op jit(solution)/shard_map/nfbc,fcd->nbd/dot_general | solution.py:140
  244.0 14.7 %bitcast_add_fusion.1 = f32[64,8,1000]{2,1,0:T(8,128)} fusion(f32[64,8,1000,1]{2,1,3,0:T(8,128)S(1)} %fusion.3, f32[6,1000,1000]{2,1,0:T(8,128)} %fusion.27, bf16[64,1000,48]{1,2,0:T(8,128)(2,1)} %fusion.28), kind=kOutput, calls=%fused_computation.85 | convolution fusion | flops 6156512256 | bytes 34240000 | tf_op jit(solution)/shard_map/nfbc,fcd->nbd/dot_general | solution.py:138
  258.7 3.9 %convolution_bitcast_fusion = f32[96,4000]{1,0:T(8,128)S(1)} fusion(bf16[96,768]{1,0:T(8,128)(2,1)S(1)} %reshape.179, bf16[768,4000]{1,0:T(8,128)(2,1)} %bitcast.222), kind=kOutput, calls=%fused_computation.39 | convolution fusion | flops 589824000 | bytes 7827456 | tf_op jit(solution)/shard_map/dot_general | solution.py:50
  267.5 3.7 %copy.72 = f32[96,8,1000]{2,1,0:T(8,128)S(1)} copy(f32[96,8,1000]{2,0,1:T(8,128)} %bitcast.223) | data formatting | bytes 6144000 | tf_op jit(solution)/shard_map/jit(_take)/gather | solution.py:145
  273.7 4.4 %select_subtract_fusion = f32[768,1000]{0,1:T(8,128)S(1)} fusion(f32[768,1000]{0,1:T(8,128)} %copy.43, f32[768,1000]{0,1:T(8,128)} %copy.34, f32[768,1000]{0,1:T(8,128)} %add_bitcast_fusion.1, pred[768]{0:T(1024)(128)(4,1)S(1)} %broadcast_in_dim.56, pred[768]{0:T(1024)(128)(4,1)S(1)} %broadcast_in_dim.53), kind=kLoop, calls=%fused_computation.73 | loop fusion | flops 3072000 | bytes 12289536 | tf_op jit(solution)/shard_map/sub | solution.py:148
  286.4 3.2 copy.44
  290.9 4.1 %fusion.52 = bf16[64,8,1000]{2,1,0:T(8,128)(2,1)} fusion(f32[64,8,1000]{2,1,0:T(8,128)} %bitcast_add_fusion.1, f32[512,1000]{1,0:T(8,128)S(1)} %copy-done.6, f32[512,1000]{1,0:T(8,128)} %copy.44, pred[8]{0:T(512)(128)(4,1)S(1)} %iota_compare_fusion.39), kind=kLoop, calls=%fused_computation.84 | loop fusion | flops 2560000 | bytes 7168008 | tf_op jit(solution)/shard_map/convert_element_type | solution.py:157
  295.1 2.7 copy.50
  299.0 12.9 %fusion.77 = f32[32,8,1000]{2,1,0:T(8,128)} fusion(f32[6,1000,1000]{2,1,0:T(8,128)} %fusion.27, bf16[32,1000,48]{1,2,0:T(8,128)(2,1)S(1)} %fusion.46), kind=kOutput, calls=%fused_computation.101 | convolution fusion | flops 3089999872 | bytes 28096000 | tf_op jit(solution)/shard_map/nfbc,fcd->nbd/dot_general | solution.py:140
  311.9 12.2 %fusion.115 = bf16[32,8,1000]{2,1,0:T(8,128)(2,1)S(1)} fusion(f32[32,8,1000]{2,1,0:T(8,128)} %fusion.77, f32[6,1000,1000]{2,1,0:T(8,128)} %fusion.27, bf16[32,1000,48]{1,2,0:T(8,128)(2,1)S(1)} %fusion.46, f32[256,1000]{1,0:T(8,128)S(1)} %copy-done.9, f32[256,1000]{1,0:T(8,128)} %copy.48, pred[8]{0:T(512)(128)(4,1)S(1)} %iota_compare_fusion.39), kind=kOutput, calls=%fused_computation.109 | convolution fusion | flops 3085536000 | bytes 30656008 | tf_op jit(solution)/shard_map/nfbc,fcd->nbd/dot_general | solution.py:138
  (115 shorter events, 62.7 us)
Async XLA Ops:
  6.5 54.5 %copy-start = (f32[8,1000]{1,0:T(8,128)S(1)}, f32[8,1000]{1,0:T(8,128)}, u32[]{:S(2)}) copy-start(f32[8,1000]{1,0:T(8,128)} %param.13) | copy-start | bytes 96004
  9.8 2.8 copy-start.2
  16.9 12.7 %copy-start.15 = (f32[10,10]{1,0:T(8,128)S(1)}, f32[10,10]{1,0:T(8,128)}, u32[]{:S(2)}) copy-start(f32[10,10]{1,0:T(8,128)} %param.15) | copy-start | bytes 1204
  16.9 171.9 %all-to-all-start = ((bf16[64,32,1000]{2,0,1:T(8,128)(2,1)}), bf16[64,32,1000]{2,0,1:T(8,128)(2,1)}, u32[]{:S(2)}, u32[]{:S(2)}) async-start(bf16[64,32,1000]{2,0,1:T(8,128)(2,1)} %copy.36), calls=%async_computation | async-start | bytes 8388608 | tf_op jit(solution)/shard_map/all_to_all | solution.py:95
  29.3 131.1 %all-gather.4.cloned.1.call-start = ((), (), s32[]{:S(2)}) async-start(), calls=%async_computation.2 | async-start | bytes 3932160 | tf_op jit(solution)/shard_map/all_gather | solution.py:117
  34.8 2.2 copy-start.7
  42.6 2.4 copy-start.17
  45.0 6.8 %copy-start.13 = (f32[3,10,10]{2,0,1:T(4,128)S(1)}, f32[3,10,10]{2,0,1:T(4,128)}, u32[]{:S(2)}) copy-start(f32[3,10,10]{2,0,1:T(4,128)} %param.17) | copy-start | bytes 3604
  45.3 12.1 %copy-start.16 = (f32[10,10]{1,0:T(8,128)S(1)}, f32[10,10]{1,0:T(8,128)}, u32[]{:S(2)}) copy-start(f32[10,10]{1,0:T(8,128)} %param.16) | copy-start | bytes 1204
  51.4 207.3 %all-gather.6.cloned.1.call-start = ((), (), s32[]{:S(2)}) async-start(), calls=%async_computation.3 | async-start | bytes 9437184 | tf_op jit(solution)/shard_map/all_gather | solution.py:121
  84.2 3.1 copy-start.8
  160.4 1.9 copy-start.10
  160.4 3.5 %copy-start.14 = (s32[6,8]{1,0:T(8,128)S(1)}, s32[6,8]{1,0:T(8,128)}, u32[]{:S(2)}) copy-start(s32[6,8]{1,0:T(8,128)} %param.21) | copy-start | bytes 580
  160.4 3.5 %copy-start.11 = (bf16[96,768]{1,0:T(8,128)(2,1)S(1)}, bf16[96,768]{1,0:T(8,128)(2,1)}, u32[]{:S(2)}) copy-start(bf16[96,768]{1,0:T(8,128)(2,1)} %param.14) | copy-start | bytes 442372
  168.7 3.0 slice-start.3
  168.7 4.3 %copy-start.20 = (f32[1000,10]{0,1:T(8,128)S(1)}, f32[1000,10]{0,1:T(8,128)}, u32[]{:S(2)}) copy-start(f32[1000,10]{0,1:T(8,128)} %fusion.128) | copy-start | bytes 120004
  171.7 5.3 %copy-start.18 = (f32[1000,10]{0,1:T(8,128)S(1)}, f32[1000,10]{0,1:T(8,128)}, u32[]{:S(2)}) copy-start(f32[1000,10]{0,1:T(8,128)} %fusion.124) | copy-start | bytes 120004
  177.0 3.8 %copy-start.19 = (f32[1000,10]{0,1:T(8,128)S(1)}, f32[1000,10]{0,1:T(8,128)}, u32[]{:S(2)}) copy-start(f32[1000,10]{0,1:T(8,128)} %fusion.123) | copy-start | bytes 120004
  177.0 7.6 %copy-start.4 = (f32[1000,1000]{1,0:T(8,128)S(1)}, f32[1000,1000]{1,0:T(8,128)}, u32[]{:S(2)}) copy-start(f32[1000,1000]{1,0:T(8,128)} %fusion.155) | copy-start | bytes 12000004
  180.8 3.8 %copy-start.3 = (f32[1000,1000]{1,0:T(8,128)S(1)}, f32[1000,1000]{1,0:T(8,128)}, u32[]{:S(2)}) copy-start(f32[1000,1000]{1,0:T(8,128)} %fusion.152) | copy-start | bytes 12000004
  180.8 3.8 %copy-start.12 = (f32[1000,10]{0,1:T(8,128)S(1)}, f32[1000,10]{0,1:T(8,128)}, u32[]{:S(2)}) copy-start(f32[1000,10]{0,1:T(8,128)} %fusion.122) | copy-start | bytes 120004
  188.8 7.0 %slice-start = ((bf16[96,32,1000]{2,1,0:T(8,128)(2,1)}), bf16[32,32,1000]{2,1,0:T(8,128)(2,1)S(1)}, s32[]{:S(2)}) async-start(bf16[96,32,1000]{2,1,0:T(8,128)(2,1)} %copy-done.2), calls=%async_computation.4 | async-start | bytes 4194304 | tf_op jit(solution)/shard_map/slice | solution.py:98
  195.8 27.8 %slice-start.1 = ((bf16[96,8,1000]{2,1,0:T(8,128)(2,1)}), bf16[64,8,1000]{2,1,0:T(8,128)(2,1)S(1)}, s32[]{:S(2)}) async-start(bf16[96,8,1000]{2,1,0:T(8,128)(2,1)} %param.11), calls=%async_computation.5 | async-start | bytes 2097152 | tf_op jit(solution)/shard_map/slice | solution.py:142
  198.3 96.8 %all-to-all-start.1 = ((bf16[32,32,1000]{2,0,1:T(8,128)(2,1)}), bf16[32,32,1000]{2,0,1:T(8,128)(2,1)}, u32[]{:S(2)}, u32[]{:S(2)}) async-start(bf16[32,32,1000]{2,0,1:T(8,128)(2,1)} %copy.47), calls=%async_computation.1 | async-start | bytes 4194304 | tf_op jit(solution)/shard_map/all_to_all | solution.py:99
  273.7 4.8 %copy-start.5 = (f32[1000,1000]{1,0:T(8,128)S(1)}, f32[1000,1000]{1,0:T(8,128)}, u32[]{:S(2)}) copy-start(f32[1000,1000]{1,0:T(8,128)} %multiply_multiply_fusion) | copy-start | bytes 12000004
  286.3 4.6 %copy-start.6 = (f32[512,1000]{1,0:T(8,128)S(1)}, f32[512,1000]{1,0:T(8,128)}, u32[]{:S(2)}) copy-start(f32[512,1000]{1,0:T(8,128)} %copy.46) | copy-start | bytes 6144004
  290.9 6.9 %slice-start.2 = ((bf16[96,8,1000]{2,1,0:T(8,128)(2,1)}), bf16[32,8,1000]{2,1,0:T(8,128)(2,1)S(1)}, s32[]{:S(2)}) async-start(bf16[96,8,1000]{2,1,0:T(8,128)(2,1)} %param.11), calls=%async_computation.6 | async-start | bytes 1048576 | tf_op jit(solution)/shard_map/slice | solution.py:161
  299.0 12.9 %copy-start.9 = (f32[256,1000]{1,0:T(8,128)S(1)}, f32[256,1000]{1,0:T(8,128)}, u32[]{:S(2)}) copy-start(f32[256,1000]{1,0:T(8,128)} %copy.49) | copy-start | bytes 3072004
  311.9 14.7 %copy-start.1 = (f32[8,1000]{1,0:T(8,128)S(1)}, f32[8,1000]{1,0:T(8,128)}, u32[]{:S(2)}) copy-start(f32[8,1000]{1,0:T(8,128)} %param.13) | copy-start | bytes 96004
Sparse Core Ops, SparseCore 0:
  51.5 108.8 all-gather.3
  162.2 39.6 all-gather.5

commit v7 on v5

--- a/solution.py
+++ b/solution.py
@@ -91,7 +91,7 @@
     box_ids = lax.iota(jnp.int32, box_dev)
     send_hot = (slots[:, None] == box_ids[None, :]).astype(jnp.bfloat16)
     outgoing = pick(send_hot, orbitals)
-    half = (orb_dev * 2) // 3
+    half = (orb_dev * 7) // 12
     incoming_a = lax.all_to_all(
         outgoing[:half], "box", split_axis=1, concat_axis=1, tiled=True
     )

time: 307 us -> 309 us (level)
  the two profiles are of different devices: /device:TPU:64 before, /device:TPU:196 now
where the time goes in v7:
time: 309 us; the launch traced here: 304 us
  matrix products  138 us (45%)
  local copies, waits for them, and re-layouts  56.4 us (18%)
  waiting for transfers between devices  53.1 us (17%)
  starting transfers between devices  31 us (10%)
  between operations  14.7 us (5%)
  other arithmetic  10.8 us (3%)
    dot_general x30, matrix products, expand(): return jnp.dot(jnp.dot(left, mat, precision=hp), right, precision=hp)  50.8 us
    all_to_all x1, waiting for transfers between devices, shards(): lax.all_to_all(outgoing[:half], 'box', split_axis=1, concat_axis=1, tiled...  32.6 us
    dot_general x2, matrix products, face_part(): jnp.einsum('nfbc,fcd->nbd', moved, face_hi, preferred_element_type=jnp.fl...  29.9 us
    dot_general x2, matrix products, face_part(): jnp.einsum('nfbc,fcd->nbd', moved, face_lo, preferred_element_type=jnp.fl...  24.4 us
    all_gather x1, waiting for transfers between devices, shards(): lax.all_gather(compact.reshape(orb_dev, KEEP * width), 'orb', axis=0, til...  20.5 us
    dot_general x8, matrix products, dot_f32(): return jnp.dot(a, b, preferred_element_type=jnp.float32)  19.5 us
    all_to_all x1, starting transfers between devices, shards(): lax.all_to_all(later, 'box', split_axis=1, concat_axis=1, tiled=True)  18.2 us
    dot_general x4, matrix products, pick(): jnp.einsum('sb,nbc->nsc', onehot, block, preferred_element_type=jnp.float32)  13.8 us
  transfers between devices with their start and end apart: 3, of which 2 were waited for; matrix products, arithmetic and copies ran while one was open for 52% of the time, Pallas kernels for 0%

profile of v7, /device:TPU:196, one launch (start us, length us, event | category | flops | bytes accessed | tf_op | source)
XLA Modules:
  0.0 304.4 jit_solution(1516333981990420495)
XLA Ops:
  6.5 3.3 %convert_bitcast_fusion = bf16[96,32,1000]{2,1,0:T(8,128)(2,1)S(1)} fusion(bf16[96,8,1000]{2,1,0:T(8,128)(2,1)} %param.11, s32[32]{0:T(128)} %bitcast.220), kind=kOutput, calls=%fused_computation.24 | convolution fusion | flops 52224256 | bytes 7680128 | tf_op jit(solution)/shard_map/sb,nbc->nsc/dot_general | solution.py:67
  13.2 3.9 %copy.35 = bf16[56,32,1000]{2,0,1:T(8,128)(2,1)} copy(bf16[56,32,1000]{2,1,0:T(8,128)(2,1)S(1)} %slice.67) | data formatting | bytes 7168000 | tf_op jit(solution)/shard_map/slice | solution.py:96
  17.1 12.6 %all-to-all-start = ((bf16[56,32,1000]{2,0,1:T(8,128)(2,1)}), bf16[56,32,1000]{2,0,1:T(8,128)(2,1)}, u32[]{:S(2)}, u32[]{:S(2)}) async-start(bf16[56,32,1000]{2,0,1:T(8,128)(2,1)} %copy.35), calls=%async_computation | async-start | bytes 7340032 | tf_op jit(solution)/shard_map/all_to_all | solution.py:95
  39.4 3.6 %add_bitcast_fusion.1 = f32[768,1000]{0,1:T(8,128)} fusion(f32[1000,768]{1,0:T(8,128)S(1)} %fusion.53, f32[1000,1000]{1,0:T(8,128)S(1)} %multiply_multiply_fusion.1, bf16[96,8,1000]{2,1,0:T(8,128)(2,1)S(1)} %copy-done.5), kind=kOutput, calls=%fused_computation.78 | convolution fusion | flops 1538768000 | bytes 11680000 | tf_op jit(solution)/shard_map/dot_general | solution.py:50
  45.5 3.0 fusion.117
  48.5 3.3 %reshape.170 = bf16[96,4000]{1,0:T(8,128)(2,1)} reshape(bf16[96,4,1000]{2,1,0:T(4,128)(2,1)} %fusion.117) | data formatting | bytes 1536000 | tf_op jit(solution)/shard_map/reshape | solution.py:114
  57.7 3.1 %fusion.23 = f32[1000,1000]{1,0:T(8,128)S(1)} fusion(f32[1000,1000]{1,0:T(8,128)S(1)} %fusion.154, f32[1000,1000]{1,0:T(8,128)S(1)} %fusion.151, f32[1000,10]{0,1:T(8,128)S(1)} %fusion.121, s32[1000]{0:T(1024)S(1)} %add_select_fusion.3, s32[1000]{0:T(1024)S(1)} %get-tuple-element.25, s32[1000]{0:T(1024)S(1)} %get-tuple-element.24), kind=kOutput, calls=%fused_computation.54 | convolution fusion | flops 131010000 | bytes 12052000 | tf_op jit(solution)/shard_map/dot_general | solution.py:21
  68.7 2.8 copy.33
  71.5 3.0 copy.44
  84.9 3.8 %fusion.15 = f32[6,1000,1000]{2,1,0:T(8,128)} fusion(f32[1000,10]{0,1:T(8,128)S(1)} %fusion.134, s32[1000]{0:T(1024)S(1)} %get-tuple-element.25, s32[1000]{0:T(1024)S(1)} %get-tuple-element.24, s32[1000]{0:T(1024)S(1)} %add_select_fusion.3), kind=kOutput, calls=%fused_computation.46 | convolution fusion | flops 124010000 | bytes 4182016 | tf_op jit(solution)/shard_map/dot_general | solution.py:21
  88.7 3.8 %fusion.17 = f32[6,1000,1000]{2,1,0:T(8,128)} fusion(f32[6,1000,1000]{2,1,0:T(8,128)} %fusion.15, f32[1000,10]{0,1:T(8,128)S(1)} %fusion.133, s32[1000]{0:T(1024)S(1)} %get-tuple-element.25, s32[1000]{0:T(1024)S(1)} %get-tuple-element.24, s32[1000]{0:T(1024)S(1)} %add_select_fusion.3), kind=kOutput, calls=%fused_computation.48 | convolution fusion | flops 124010000 | bytes 4182016 | tf_op jit(solution)/shard_map/dot_general | solution.py:21
  92.5 3.8 %fusion.19 = f32[6,1000,1000]{2,1,0:T(8,128)} fusion(f32[6,1000,1000]{2,1,0:T(8,128)} %fusion.17, f32[1000,10]{0,1:T(8,128)S(1)} %fusion.129, s32[1000]{0:T(1024)S(1)} %add_select_fusion.3, s32[1000]{0:T(1024)S(1)} %get-tuple-element.24, s32[1000]{0:T(1024)S(1)} %get-tuple-element.25), kind=kOutput, calls=%fused_computation.50 | convolution fusion | flops 124010000 | bytes 4182016 | tf_op jit(solution)/shard_map/dot_general | solution.py:21
  96.2 3.8 %fusion.21 = f32[6,1000,1000]{2,1,0:T(8,128)} fusion(f32[6,1000,1000]{2,1,0:T(8,128)} %fusion.19, f32[1000,10]{0,1:T(8,128)S(1)} %fusion.128, s32[1000]{0:T(1024)S(1)} %add_select_fusion.3, s32[1000]{0:T(1024)S(1)} %get-tuple-element.24, s32[1000]{0:T(1024)S(1)} %get-tuple-element.25), kind=kOutput, calls=%fused_computation.52 | convolution fusion | flops 124010000 | bytes 4182016 | tf_op jit(solution)/shard_map/dot_general | solution.py:21
  100.0 3.9 %fusion.25 = f32[6,1000,1000]{2,1,0:T(8,128)} fusion(f32[6,1000,1000]{2,1,0:T(8,128)} %fusion.21, f32[1000,10]{0,1:T(8,128)S(1)} %fusion.124, s32[1000]{0:T(1024)S(1)} %add_select_fusion.3, s32[1000]{0:T(1024)S(1)} %get-tuple-element.25, s32[1000]{0:T(1024)S(1)} %get-tuple-element.24), kind=kOutput, calls=%fused_computation.56 | convolution fusion | flops 124010000 | bytes 4182016 | tf_op jit(solution)/shard_map/dot_general | solution.py:21
  104.0 3.8 %fusion.27 = f32[6,1000,1000]{2,1,0:T(8,128)} fusion(f32[6,1000,1000]{2,1,0:T(8,128)} %fusion.25, f32[1000,10]{0,1:T(8,128)S(1)} %fusion.123, s32[1000]{0:T(1024)S(1)} %add_select_fusion.3, s32[1000]{0:T(1024)S(1)} %get-tuple-element.25, s32[1000]{0:T(1024)S(1)} %get-tuple-element.24), kind=kOutput, calls=%fused_computation.58 | convolution fusion | flops 124010000 | bytes 4182016 | tf_op jit(solution)/shard_map/dot_general | solution.py:21
  107.8 4.1 %multiply_multiply_fusion = f32[1000,1000]{1,0:T(8,128)} fusion(f32[1000,1000]{1,0:T(8,128)S(1)} %fusion.155, f32[1000,1000]{1,0:T(8,128)S(1)} %fusion.152, f32[1000,10]{0,1:T(8,128)S(1)} %fusion.122, s32[1000]{0:T(1024)S(1)} %get-tuple-element.24), kind=kOutput, calls=%fused_computation.59 | convolution fusion | flops 122010000 | bytes 12044000 | tf_op jit(solution)/shard_map/dot_general | solution.py:21
  111.9 32.6 %all-to-all-done = bf16[56,32,1000]{2,0,1:T(8,128)(2,1)} async-done(((bf16[56,32,1000]{2,0,1:T(8,128)(2,1)}), bf16[56,32,1000]{2,0,1:T(8,128)(2,1)}, u32[]{:S(2)}, u32[]{:S(2)}) %all-to-all-start) | async-done | bytes 3584032 | tf_op jit(solution)/shard_map/all_to_all | solution.py:95
  144.5 5.9 %copy.36 = bf16[56,32,1000]{2,1,0:T(8,128)(2,1)} copy(bf16[56,32,1000]{2,0,1:T(8,128)(2,1)} %all-to-all-done) | data formatting | bytes 7168000 | tf_op jit(solution)/shard_map/optimization_barrier | solution.py:98
  150.4 2.9 copy.45
  153.3 18.2 %all-to-all-start.1 = ((bf16[40,32,1000]{2,0,1:T(8,128)(2,1)}), bf16[40,32,1000]{2,0,1:T(8,128)(2,1)}, u32[]{:S(2)}, u32[]{:S(2)}) async-start(bf16[40,32,1000]{2,0,1:T(8,128)(2,1)} %copy.45), calls=%async_computation.1 | async-start | bytes 5242880 | tf_op jit(solution)/shard_map/all_to_all | solution.py:99
  171.6 6.3 %fusion.40 = bf16[56,1000,48]{1,2,0:T(8,128)(2,1)} fusion(bf16[56,32,1000]{2,1,0:T(8,128)(2,1)} %copy.36, bf16[56,8,1000]{2,1,0:T(8,128)(2,1)S(1)} %slice-done.1, s32[48]{0:T(128)S(1)} %eq.741), kind=kOutput, calls=%fused_computation.69 | convolution fusion | flops 226689920 | bytes 9856192 | tf_op jit(solution)/shard_map/sb,nbc->nsc/dot_general | solution.py:67
  177.8 12.7 %fusion.3 = f32[56,8,1000,1]{2,1,3,0:T(8,128)S(1)} fusion(bf16[56,1000,48]{1,2,0:T(8,128)(2,1)} %fusion.40, f32[6,1000,1000]{2,1,0:T(8,128)} %fusion.27), kind=kOutput, calls=%fused_computation.31 | convolution fusion | flops 5393999872 | bytes 31168000 | tf_op jit(solution)/shard_map/nfbc,fcd->nbd/dot_general | solution.py:131
  190.6 16.1 %bitcast_add_fusion.1 = f32[56,8,1000]{2,1,0:T(8,128)} fusion(f32[56,8,1000,1]{2,1,3,0:T(8,128)S(1)} %fusion.3, f32[6,1000,1000]{2,1,0:T(8,128)} %fusion.27, bf16[56,1000,48]{1,2,0:T(8,128)(2,1)} %fusion.40), kind=kOutput, calls=%fused_computation.90 | convolution fusion | flops 5388448256 | bytes 32960000 | tf_op jit(solution)/shard_map/nfbc,fcd->nbd/dot_general | solution.py:129
  206.7 20.5 %all-gather.2.cloned.1.call-done = bf16[768,4000]{1,0:T(8,128)(2,1)} async-done(((bf16[96,4000]{1,0:T(8,128)(2,1)}), bf16[768,4000]{1,0:T(8,128)(2,1)}) %all-gather.2.cloned.1.call-update) | async-done | bytes 6144016 | tf_op jit(solution)/shard_map/all_gather | solution.py:113
  227.2 3.9 %convolution_bitcast_fusion = f32[96,4000]{1,0:T(8,128)S(1)} fusion(bf16[96,768]{1,0:T(8,128)(2,1)S(1)} %copy-done, bf16[768,4000]{1,0:T(8,128)(2,1)} %all-gather.2.cloned.1.call-done), kind=kOutput, calls=%fused_computation.35 | convolution fusion | flops 589824000 | bytes 7827456 | tf_op jit(solution)/shard_map/dot_general | solution.py:50
  236.0 3.7 %copy.69 = f32[96,8,1000]{2,1,0:T(8,128)S(1)} copy(f32[96,8,1000]{2,0,1:T(8,128)} %bitcast.218) | data formatting | bytes 6144000 | tf_op jit(solution)/shard_map/jit(_take)/gather | solution.py:136
  239.7 2.8 copy.41
  242.6 4.4 %select_subtract_fusion = f32[768,1000]{0,1:T(8,128)S(1)} fusion(f32[768,1000]{0,1:T(8,128)} %copy.41, f32[768,1000]{0,1:T(8,128)} %copy.33, f32[768,1000]{0,1:T(8,128)} %add_bitcast_fusion.1, pred[768]{0:T(1024)(128)(4,1)S(1)} %broadcast_in_dim.56, pred[768]{0:T(1024)(128)(4,1)S(1)} %broadcast_in_dim.53), kind=kLoop, calls=%fused_computation.77 | loop fusion | flops 3072000 | bytes 12289536 | tf_op jit(solution)/shard_map/sub | solution.py:139
  259.3 3.7 %fusion.60 = bf16[56,8,1000]{2,1,0:T(8,128)(2,1)} fusion(f32[56,8,1000]{2,1,0:T(8,128)} %bitcast_add_fusion.1, f32[448,1000]{1,0:T(8,128)S(1)} %copy-done.4, f32[448,1000]{1,0:T(8,128)} %copy.42, pred[8]{0:T(512)(128)(4,1)S(1)} %iota_compare_fusion.39), kind=kLoop, calls=%fused_computation.89 | loop fusion | flops 2240000 | bytes 6272008 | tf_op jit(solution)/shard_map/convert_element_type | solution.py:148
  263.0 3.2 %copy.48 = bf16[40,32,1000]{2,1,0:T(8,128)(2,1)S(1)} copy(bf16[40,32,1000]{2,0,1:T(8,128)(2,1)} %all-to-all-done.1) | data formatting | bytes 5120000 | tf_op jit(solution)/shard_map/optimization_barrier | solution.py:151
  269.5 11.6 %fusion.79 = f32[40,8,1000]{2,1,0:T(8,128)} fusion(f32[6,1000,1000]{2,1,0:T(8,128)} %fusion.27, bf16[40,1000,48]{1,2,0:T(8,128)(2,1)S(1)} %fusion.46), kind=kOutput, calls=%fused_computation.101 | convolution fusion | flops 3857999872 | bytes 29120000 | tf_op jit(solution)/shard_map/nfbc,fcd->nbd/dot_general | solution.py:131
  281.1 13.8 %fusion.112 = bf16[40,8,1000]{2,1,0:T(8,128)(2,1)S(1)} fusion(f32[40,8,1000]{2,1,0:T(8,128)} %fusion.79, f32[6,1000,1000]{2,1,0:T(8,128)} %fusion.27, bf16[40,1000,48]{1,2,0:T(8,128)(2,1)} %copy-done.2, f32[320,1000]{1,0:T(8,128)S(1)} %copy-done.8, f32[320,1000]{1,0:T(8,128)S(1)} %copy.46, pred[8]{0:T(512)(128)(4,1)S(1)} %iota_compare_fusion.39), kind=kOutput, calls=%fused_computation.108 | convolution fusion | flops 3853920000 | bytes 32320008 | tf_op jit(solution)/shard_map/nfbc,fcd->nbd/dot_general | solution.py:129
  (96 shorter events, 61.9 us)
Async XLA Ops:
  6.5 220.6 %copy-start = (bf16[96,768]{1,0:T(8,128)(2,1)S(1)}, bf16[96,768]{1,0:T(8,128)(2,1)}, u32[]{:S(2)}) copy-start(bf16[96,768]{1,0:T(8,128)(2,1)} %param.14) | copy-start | bytes 442372
  9.8 2.7 copy-start.1
  17.1 12.9 %copy-start.12 = (f32[10,10]{1,0:T(8,128)S(1)}, f32[10,10]{1,0:T(8,128)}, u32[]{:S(2)}) copy-start(f32[10,10]{1,0:T(8,128)} %param.15) | copy-start | bytes 1204
  17.1 127.4 %all-to-all-start = ((bf16[56,32,1000]{2,0,1:T(8,128)(2,1)}), bf16[56,32,1000]{2,0,1:T(8,128)(2,1)}, u32[]{:S(2)}, u32[]{:S(2)}) async-start(bf16[56,32,1000]{2,0,1:T(8,128)(2,1)} %copy.35), calls=%async_computation | async-start | bytes 7340032 | tf_op jit(solution)/shard_map/all_to_all | solution.py:95
  29.7 197.5 %all-gather.2.cloned.1.call-start = ((), (), s32[]{:S(2)}) async-start(), calls=%async_computation.2 | async-start | bytes 7077888 | tf_op jit(solution)/shard_map/all_gather | solution.py:113
  35.1 2.2 copy-start.5
  42.9 2.4 copy-start.14
  51.8 0.7 copy-start.10
  57.7 3.2 %copy-start.6 = (bf16[96,8,1000]{2,1,0:T(8,128)(2,1)S(1)}, bf16[96,8,1000]{2,1,0:T(8,128)(2,1)}, u32[]{:S(2)}) copy-start(bf16[96,8,1000]{2,1,0:T(8,128)(2,1)} %param.11) | copy-start | bytes 4608004
  64.8 3.2 %copy-start.11 = (s32[6,8]{1,0:T(8,128)S(1)}, s32[6,8]{1,0:T(8,128)}, u32[]{:S(2)}) copy-start(s32[6,8]{1,0:T(8,128)} %param.21) | copy-start | bytes 580
  64.8 3.5 %copy-start.9 = (f32[8,1000]{1,0:T(8,128)S(1)}, f32[8,1000]{1,0:T(8,128)}, u32[]{:S(2)}) copy-start(f32[8,1000]{1,0:T(8,128)} %param.13) | copy-start | bytes 96004
  71.5 3.6 %copy-start.7 = (f32[320,1000]{0,1:T(8,128)S(1)}, f32[320,1000]{0,1:T(8,128)}, u32[]{:S(2)}) copy-start(f32[320,1000]{0,1:T(8,128)} %slice.71) | copy-start | bytes 3840004
  71.5 8.2 %copy-start.13 = (f32[10,10]{1,0:T(8,128)S(1)}, f32[10,10]{1,0:T(8,128)}, u32[]{:S(2)}) copy-start(f32[10,10]{1,0:T(8,128)} %param.16) | copy-start | bytes 1204
  111.9 38.5 %slice-start = ((bf16[96,32,1000]{2,1,0:T(8,128)(2,1)}), bf16[40,32,1000]{2,1,0:T(8,128)(2,1)S(1)}, s32[]{:S(2)}) async-start(bf16[96,32,1000]{2,1,0:T(8,128)(2,1)} %copy-done.1), calls=%async_computation.3 | async-start | bytes 5242880 | tf_op jit(solution)/shard_map/slice | solution.py:98
  153.3 18.2 %slice-start.1 = ((bf16[96,8,1000]{2,1,0:T(8,128)(2,1)}), bf16[56,8,1000]{2,1,0:T(8,128)(2,1)S(1)}, s32[]{:S(2)}) async-start(bf16[96,8,1000]{2,1,0:T(8,128)(2,1)} %param.11), calls=%async_computation.4 | async-start | bytes 1835008 | tf_op jit(solution)/shard_map/slice | solution.py:133
  153.3 109.7 %all-to-all-start.1 = ((bf16[40,32,1000]{2,0,1:T(8,128)(2,1)}), bf16[40,32,1000]{2,0,1:T(8,128)(2,1)}, u32[]{:S(2)}, u32[]{:S(2)}) async-start(bf16[40,32,1000]{2,0,1:T(8,128)(2,1)} %copy.45), calls=%async_computation.1 | async-start | bytes 5242880 | tf_op jit(solution)/shard_map/all_to_all | solution.py:99
  242.6 4.8 %copy-start.3 = (f32[1000,1000]{1,0:T(8,128)S(1)}, f32[1000,1000]{1,0:T(8,128)}, u32[]{:S(2)}) copy-start(f32[1000,1000]{1,0:T(8,128)} %multiply_multiply_fusion) | copy-start | bytes 12000004
  257.3 2.0 copy-start.4
  263.0 3.3 %slice-start.2 = ((bf16[96,8,1000]{2,1,0:T(8,128)(2,1)}), bf16[40,8,1000]{2,1,0:T(8,128)(2,1)S(1)}, s32[]{:S(2)}) async-start(bf16[96,8,1000]{2,1,0:T(8,128)(2,1)} %param.11), calls=%async_computation.5 | async-start | bytes 1310720 | tf_op jit(solution)/shard_map/slice | solution.py:152
  267.6 1.9 copy-start.2
  269.5 11.6 %copy-start.8 = (f32[320,1000]{1,0:T(8,128)S(1)}, f32[320,1000]{1,0:T(8,128)}, u32[]{:S(2)}) copy-start(f32[320,1000]{1,0:T(8,128)} %copy.47) | copy-start | bytes 3840004
Sparse Core Ops, SparseCore 0:
  52.0 175.1 all-gather.1

commit v8 on v7

--- a/solution.py
+++ b/solution.py
@@ -91,7 +91,7 @@
     box_ids = lax.iota(jnp.int32, box_dev)
     send_hot = (slots[:, None] == box_ids[None, :]).astype(jnp.bfloat16)
     outgoing = pick(send_hot, orbitals)
-    half = (orb_dev * 7) // 12
+    half = orb_dev // 2
     incoming_a = lax.all_to_all(
         outgoing[:half], "box", split_axis=1, concat_axis=1, tiled=True
     )

time: 309 us -> 308 us (level)
  the two profiles are of different devices: /device:TPU:196 before, /device:TPU:90 now
where the time goes in v8:
time: 308 us; the launch traced here: 303 us
  matrix products  126 us (41%)
  local copies, waits for them, and re-layouts  69 us (22%)
  waiting for transfers between devices  53.6 us (17%)
  starting transfers between devices  30.9 us (10%)
  between operations  14.9 us (5%)
  other arithmetic  8.88 us (3%)
    all_gather x1, waiting for transfers between devices, shards(): lax.all_gather(compact.reshape(orb_dev, KEEP * width), 'orb', axis=0, til...  50.4 us
    dot_general x30, matrix products, expand(): return jnp.dot(jnp.dot(left, mat, precision=hp), right, precision=hp)  41.7 us
    dot_general x8, matrix products, dot_f32(): return jnp.dot(a, b, preferred_element_type=jnp.float32)  25 us
    dot_general x2, matrix products, face_part(): jnp.einsum('nfbc,fcd->nbd', moved, face_hi, preferred_element_type=jnp.fl...  24.5 us
    dot_general x2, matrix products, face_part(): jnp.einsum('nfbc,fcd->nbd', moved, face_lo, preferred_element_type=jnp.fl...  23.4 us
    all_to_all x1, starting transfers between devices, shards(): lax.all_to_all(later, 'box', split_axis=1, concat_axis=1, tiled=True)  18.4 us
    all_to_all x1, starting transfers between devices, shards(): lax.all_to_all(outgoing[:half], 'box', split_axis=1, concat_axis=1, tiled...  12.2 us
    dot_general x4, matrix products, pick(): jnp.einsum('sb,nbc->nsc', onehot, block, preferred_element_type=jnp.float32)  11.5 us
  transfers between devices with their start and end apart: 3, of which 2 were waited for; matrix products, arithmetic and copies ran while one was open for 50% of the time, Pallas kernels for 0%

profile of v8, /device:TPU:90, one launch (start us, length us, event | category | flops | bytes accessed | tf_op | source)
XLA Modules:
  0.0 303.4 jit_solution(3900899390850465925)
XLA Ops:
  6.5 3.3 %convert_bitcast_fusion = bf16[96,32,1000]{2,1,0:T(8,128)(2,1)S(1)} fusion(bf16[96,8,1000]{2,1,0:T(8,128)(2,1)} %param.11, s32[32]{0:T(128)} %bitcast.190), kind=kOutput, calls=%fused_computation.24 | convolution fusion | flops 52224256 | bytes 7680128 | tf_op jit(solution)/shard_map/sb,nbc->nsc/dot_general | solution.py:67
  12.3 3.3 %copy.35 = bf16[48,32,1000]{2,0,1:T(8,128)(2,1)} copy(bf16[48,32,1000]{2,1,0:T(8,128)(2,1)S(1)} %get-tuple-element.17) | data formatting | bytes 6144000 | tf_op jit(solution)/shard_map/slice | solution.py:96
  15.7 12.2 %all-to-all-start = ((bf16[48,32,1000]{2,0,1:T(8,128)(2,1)}), bf16[48,32,1000]{2,0,1:T(8,128)(2,1)S(1)}, u32[]{:S(2)}, u32[]{:S(2)}) async-start(bf16[48,32,1000]{2,0,1:T(8,128)(2,1)} %copy.35), calls=%async_computation | async-start | bytes 6291456 | tf_op jit(solution)/shard_map/all_to_all | solution.py:95
  37.7 3.7 %add_bitcast_fusion.1 = f32[768,1000]{0,1:T(8,128)} fusion(f32[1000,768]{1,0:T(8,128)S(1)} %fusion.53, f32[1000,1000]{1,0:T(8,128)S(1)} %multiply_multiply_fusion.1, bf16[96,8,1000]{2,1,0:T(8,128)(2,1)S(1)} %copy-done.5), kind=kOutput, calls=%fused_computation.77 | convolution fusion | flops 1538768000 | bytes 11680000 | tf_op jit(solution)/shard_map/dot_general | solution.py:50
  41.4 3.9 %copy.34 = f32[768,1000]{1,0:T(8,128)} copy(f32[768,1000]{0,1:T(8,128)} %add_bitcast_fusion.1) | data formatting | bytes 6144000 | tf_op jit(solution)/shard_map/add | solution.py:55
  45.5 3.9 %fusion.86 = bf16[96,4,1000]{2,1,0:T(4,128)(2,1)} fusion(f32[768,1000]{1,0:T(8,128)} %copy.34, bf16[96,8,1000]{2,1,0:T(8,128)(2,1)} %param.12, pred[8]{0:T(512)(128)(4,1)S(1)} %get-tuple-element.31, s32[8]{0:T(128)S(1)} %get-tuple-element.29), kind=kOutput, calls=%fused_computation.107 | convolution fusion | flops 9600064 | bytes 5376040 | tf_op jit(solution)/shard_map/sb,nbc->nsc/dot_general | solution.py:67
  49.4 3.1 %reshape.170 = bf16[96,4000]{1,0:T(8,128)(2,1)} reshape(bf16[96,4,1000]{2,1,0:T(4,128)(2,1)} %fusion.86) | data formatting | bytes 1536000 | tf_op jit(solution)/shard_map/reshape | solution.py:114
  59.8 3.3 %fusion.23 = f32[1000,1000]{1,0:T(8,128)S(1)} fusion(f32[1000,1000]{1,0:T(8,128)S(1)} %fusion.123, f32[1000,1000]{1,0:T(8,128)S(1)} %fusion.120, f32[1000,10]{0,1:T(8,128)S(1)} %fusion.90, s32[1000]{0:T(1024)S(1)} %add_select_fusion.3, s32[1000]{0:T(1024)S(1)} %get-tuple-element.33, s32[1000]{0:T(1024)S(1)} %get-tuple-element.32), kind=kOutput, calls=%fused_computation.54 | convolution fusion | flops 131010000 | bytes 12052000 | tf_op jit(solution)/shard_map/dot_general | solution.py:21
  63.1 3.6 %fusion.49 = f32[1000,768]{1,0:T(8,128)} fusion(f32[1000,1000]{1,0:T(8,128)S(1)} %fusion.23, bf16[96,8,1000]{2,1,0:T(8,128)(2,1)S(1)} %copy-done.6), kind=kOutput, calls=%fused_computation.80 | convolution fusion | flops 1539000064 | bytes 8608000 | tf_op jit(solution)/shard_map/dot_general | solution.py:50
  67.1 3.7 %copy.33 = f32[768,1000]{0,1:T(8,128)} copy(f32[768,1000]{1,0:T(8,128)} %broadcast_bitcast_fusion) | data formatting | bytes 6144000 | tf_op jit(solution)/shard_map/mul | solution.py:139
  70.8 5.5 %add_bitcast_fusion = f32[768,1000]{0,1:T(8,128)S(1)} fusion(f32[1000,768]{1,0:T(8,128)} %fusion.49, f32[1000,1000]{1,0:T(8,128)} %copy-done.19, bf16[96,8,1000]{2,1,0:T(8,128)(2,1)} %param.11), kind=kOutput, calls=%fused_computation.74 | convolution fusion | flops 1538768000 | bytes 11680000 | tf_op jit(solution)/shard_map/dot_general | solution.py:50
  78.2 3.1 %copy.44 = f32[384,1000]{1,0:T(8,128)} copy(f32[384,1000]{0,1:T(8,128)} %get-tuple-element.22) | data formatting | bytes 3072000 | tf_op jit(solution)/shard_map/slice | solution.py:150
  81.9 3.1 %copy.47 = f32[384,1000]{1,0:T(8,128)} copy(f32[384,1000]{0,1:T(8,128)} %get-tuple-element.21) | data formatting | bytes 3072000 | tf_op jit(solution)/shard_map/slice | solution.py:153
  89.5 2.6 fusion.170
  109.4 8.2 %copy-done.18 = f32[6,1000,1000]{2,1,0:T(8,128)} copy-done((f32[6,1000,1000]{2,1,0:T(8,128)}, f32[6,1000,1000]{2,1,0:T(8,128)S(1)}, u32[]{:S(2)}) %copy-start.18) | copy-done | bytes 24000024
  117.7 4.1 %multiply_multiply_fusion = f32[1000,1000]{1,0:T(8,128)} fusion(f32[1000,1000]{1,0:T(8,128)S(1)} %fusion.124, f32[1000,1000]{1,0:T(8,128)S(1)} %fusion.121, f32[1000,10]{0,1:T(8,128)S(1)} %fusion.91, s32[1000]{0:T(1024)S(1)} %get-tuple-element.32), kind=kOutput, calls=%fused_computation.59 | convolution fusion | flops 122010000 | bytes 12044000 | tf_op jit(solution)/shard_map/dot_general | solution.py:21
  121.8 3.2 %all-to-all-done = bf16[48,32,1000]{2,0,1:T(8,128)(2,1)S(1)} async-done(((bf16[48,32,1000]{2,0,1:T(8,128)(2,1)}), bf16[48,32,1000]{2,0,1:T(8,128)(2,1)S(1)}, u32[]{:S(2)}, u32[]{:S(2)}) %all-to-all-start) | async-done | bytes 3072032 | tf_op jit(solution)/shard_map/all_to_all | solution.py:95
  125.0 3.6 %copy.36 = bf16[48,32,1000]{2,1,0:T(8,128)(2,1)} copy(bf16[48,32,1000]{2,0,1:T(8,128)(2,1)S(1)} %all-to-all-done) | data formatting | bytes 6144000 | tf_op jit(solution)/shard_map/optimization_barrier | solution.py:98
  128.6 3.3 %copy.45 = bf16[48,32,1000]{2,0,1:T(8,128)(2,1)} copy(bf16[48,32,1000]{2,1,0:T(8,128)(2,1)S(1)} %copy-done.3) | data formatting | bytes 6144000 | tf_op jit(solution)/shard_map/optimization_barrier | solution.py:98
  131.9 18.4 %all-to-all-start.1 = ((bf16[48,32,1000]{2,0,1:T(8,128)(2,1)}), bf16[48,32,1000]{2,0,1:T(8,128)(2,1)}, u32[]{:S(2)}, u32[]{:S(2)}) async-start(bf16[48,32,1000]{2,0,1:T(8,128)(2,1)} %copy.45), calls=%async_computation.1 | async-start | bytes 6291456 | tf_op jit(solution)/shard_map/all_to_all | solution.py:99
  150.3 2.7 fusion.46
  153.0 11.2 %fusion.7 = f32[48,8,1000,1]{2,1,3,0:T(8,128)S(1)} fusion(bf16[48,1000,48]{1,2,0:T(8,128)(2,1)S(1)} %fusion.46, f32[6,1000,1000]{2,1,0:T(8,128)} %copy-done.18), kind=kOutput, calls=%fused_computation.36 | convolution fusion | flops 4625999872 | bytes 30144000 | tf_op jit(solution)/shard_map/nfbc,fcd->nbd/dot_general | solution.py:131
  164.2 12.0 %bitcast_add_fusion.2 = f32[48,8,1000]{2,1,0:T(8,128)} fusion(f32[48,8,1000,1]{2,1,3,0:T(8,128)S(1)} %fusion.7, f32[6,1000,1000]{2,1,0:T(8,128)} %copy-done.18, bf16[48,1000,48]{1,2,0:T(8,128)(2,1)S(1)} %fusion.46), kind=kOutput, calls=%fused_computation.98 | convolution fusion | flops 4620384256 | bytes 31680000 | tf_op jit(solution)/shard_map/nfbc,fcd->nbd/dot_general | solution.py:129
  176.3 50.4 %all-gather.2.cloned.1.call-done = bf16[768,4000]{1,0:T(8,128)(2,1)} async-done(((bf16[96,4000]{1,0:T(8,128)(2,1)}), bf16[768,4000]{1,0:T(8,128)(2,1)}) %all-gather.2.cloned.1.call-update) | async-done | bytes 6144016 | tf_op jit(solution)/shard_map/all_gather | solution.py:113
  226.7 3.9 %convolution_bitcast_fusion = f32[96,4000]{1,0:T(8,128)S(1)} fusion(bf16[96,768]{1,0:T(8,128)(2,1)S(1)} %copy-done, bf16[768,4000]{1,0:T(8,128)(2,1)} %all-gather.2.cloned.1.call-done), kind=kOutput, calls=%fused_computation.31 | convolution fusion | flops 589824000 | bytes 7827456 | tf_op jit(solution)/shard_map/dot_general | solution.py:50
  235.5 3.7 %copy.69 = f32[96,8,1000]{2,1,0:T(8,128)S(1)} copy(f32[96,8,1000]{2,0,1:T(8,128)} %bitcast.188) | data formatting | bytes 6144000 | tf_op jit(solution)/shard_map/jit(_take)/gather | solution.py:136
  241.8 4.4 %select_subtract_fusion = f32[768,1000]{0,1:T(8,128)S(1)} fusion(f32[768,1000]{0,1:T(8,128)} %copy.41, f32[768,1000]{0,1:T(8,128)} %copy.33, f32[768,1000]{0,1:T(8,128)} %add_bitcast_fusion.1, pred[768]{0:T(1024)(128)(4,1)S(1)} %broadcast_in_dim.52, pred[768]{0:T(1024)(128)(4,1)S(1)} %broadcast_in_dim.49), kind=kLoop, calls=%fused_computation.76 | loop fusion | flops 3072000 | bytes 12289536 | tf_op jit(solution)/shard_map/sub | solution.py:139
  256.7 3.0 copy.46
  259.7 2.9 fusion.67
  262.6 3.7 %copy.48 = bf16[48,32,1000]{2,1,0:T(8,128)(2,1)S(1)} copy(bf16[48,32,1000]{2,0,1:T(8,128)(2,1)} %all-to-all-done.1) | data formatting | bytes 6144000 | tf_op jit(solution)/shard_map/optimization_barrier | solution.py:151
  270.0 12.2 %fusion.3 = f32[48,8,1000,1]{2,1,3,0:T(8,128)} fusion(bf16[48,1000,48]{1,2,0:T(8,128)(2,1)S(1)} %fusion.43, f32[6,1000,1000]{2,1,0:T(8,128)} %copy-done.18), kind=kOutput, calls=%fused_computation.32 | convolution fusion | flops 4625999872 | bytes 30144000 | tf_op jit(solution)/shard_map/nfbc,fcd->nbd/dot_general | solution.py:131
  282.3 12.5 %fusion.63 = bf16[48,8,1000]{2,1,0:T(8,128)(2,1)S(1)} fusion(f32[48,8,1000,1]{2,1,3,0:T(8,128)} %fusion.3, f32[384,1000]{1,0:T(8,128)S(1)} %copy-done.10, f32[384,1000]{1,0:T(8,128)S(1)} %copy-done.11, f32[6,1000,1000]{2,1,0:T(8,128)} %copy-done.18, bf16[48,1000,48]{1,2,0:T(8,128)(2,1)} %copy-done.7, pred[8]{0:T(512)(128)(4,1)S(1)} %iota_compare_fusion.39), kind=kOutput, calls=%fused_computation.92 | convolution fusion | flops 4622304256 | bytes 33984008 | tf_op jit(solution)/shard_map/nfbc,fcd->nbd/dot_general | solution.py:129
  (99 shorter events, 66.5 us)
Async XLA Ops:
  6.5 220.1 %copy-start = (bf16[96,768]{1,0:T(8,128)(2,1)S(1)}, bf16[96,768]{1,0:T(8,128)(2,1)}, u32[]{:S(2)}) copy-start(bf16[96,768]{1,0:T(8,128)(2,1)} %param.14) | copy-start | bytes 442372
  15.7 12.6 %copy-start.15 = (f32[10,10]{1,0:T(8,128)S(1)}, f32[10,10]{1,0:T(8,128)}, u32[]{:S(2)}) copy-start(f32[10,10]{1,0:T(8,128)} %param.15) | copy-start | bytes 1204
  15.7 109.3 %all-to-all-start = ((bf16[48,32,1000]{2,0,1:T(8,128)(2,1)}), bf16[48,32,1000]{2,0,1:T(8,128)(2,1)S(1)}, u32[]{:S(2)}, u32[]{:S(2)}) async-start(bf16[48,32,1000]{2,0,1:T(8,128)(2,1)} %copy.35), calls=%async_computation | async-start | bytes 6291456 | tf_op jit(solution)/shard_map/all_to_all | solution.py:95
  27.9 198.7 %all-gather.2.cloned.1.call-start = ((), (), s32[]{:S(2)}) async-start(), calls=%async_computation.2 | async-start | bytes 7077888 | tf_op jit(solution)/shard_map/all_gather | solution.py:113
  33.4 2.2 copy-start.5
  41.4 3.9 %copy-start.17 = (s32[8]{0:T(128)S(1)}, s32[8]{0:T(128)}, u32[]{:S(2)}) copy-start(s32[8]{0:T(128)} %param.19) | copy-start | bytes 100
  45.3 7.3 %copy-start.13 = (f32[3,10,10]{2,0,1:T(4,128)S(1)}, f32[3,10,10]{2,0,1:T(4,128)}, u32[]{:S(2)}) copy-start(f32[3,10,10]{2,0,1:T(4,128)} %param.17) | copy-start | bytes 3604
  45.5 8.6 %copy-start.12 = (f32[8,1000]{1,0:T(8,128)S(1)}, f32[8,1000]{1,0:T(8,128)}, u32[]{:S(2)}) copy-start(f32[8,1000]{1,0:T(8,128)} %param.13) | copy-start | bytes 96004
  59.8 3.3 %copy-start.6 = (bf16[96,8,1000]{2,1,0:T(8,128)(2,1)S(1)}, bf16[96,8,1000]{2,1,0:T(8,128)(2,1)}, u32[]{:S(2)}) copy-start(bf16[96,8,1000]{2,1,0:T(8,128)(2,1)} %param.11) | copy-start | bytes 4608004
  63.1 3.7 %copy-start.19 = (f32[1000,1000]{1,0:T(8,128)}, f32[1000,1000]{1,0:T(8,128)S(1)}, u32[]{:S(2)}) copy-start(f32[1000,1000]{1,0:T(8,128)S(1)} %fusion.23) | copy-start | bytes 12000004
  63.1 3.7 %copy-start.14 = (s32[6,8]{1,0:T(8,128)S(1)}, s32[6,8]{1,0:T(8,128)}, u32[]{:S(2)}) copy-start(s32[6,8]{1,0:T(8,128)} %param.21) | copy-start | bytes 580
  78.2 9.8 %copy-start.16 = (f32[10,10]{1,0:T(8,128)S(1)}, f32[10,10]{1,0:T(8,128)}, u32[]{:S(2)}) copy-start(f32[10,10]{1,0:T(8,128)} %param.16) | copy-start | bytes 1204
  109.4 8.2 %copy-start.18 = (f32[6,1000,1000]{2,1,0:T(8,128)}, f32[6,1000,1000]{2,1,0:T(8,128)S(1)}, u32[]{:S(2)}) copy-start(f32[6,1000,1000]{2,1,0:T(8,128)S(1)} %fusion.27) | copy-start | bytes 72000000
  125.0 3.6 %copy-start.3 = (bf16[48,32,1000]{2,1,0:T(8,128)(2,1)S(1)}, bf16[48,32,1000]{2,1,0:T(8,128)(2,1)}, u32[]{:S(2)}) copy-start(bf16[48,32,1000]{2,1,0:T(8,128)(2,1)} %get-tuple-element.14) | copy-start | bytes 9216004
  131.9 18.4 %copy-start.2 = (bf16[48,32,1000]{2,1,0:T(8,128)(2,1)S(1)}, bf16[48,32,1000]{2,1,0:T(8,128)(2,1)}, u32[]{:S(2)}) copy-start(bf16[48,32,1000]{2,1,0:T(8,128)(2,1)} %copy.36) | copy-start | bytes 9216004
  131.9 130.7 %all-to-all-start.1 = ((bf16[48,32,1000]{2,0,1:T(8,128)(2,1)}), bf16[48,32,1000]{2,0,1:T(8,128)(2,1)}, u32[]{:S(2)}, u32[]{:S(2)}) async-start(bf16[48,32,1000]{2,0,1:T(8,128)(2,1)} %copy.45), calls=%async_computation.1 | async-start | bytes 6291456 | tf_op jit(solution)/shard_map/all_to_all | solution.py:99
  241.8 4.8 %copy-start.1 = (f32[1000,1000]{1,0:T(8,128)S(1)}, f32[1000,1000]{1,0:T(8,128)}, u32[]{:S(2)}) copy-start(f32[1000,1000]{1,0:T(8,128)} %multiply_multiply_fusion) | copy-start | bytes 12000004
  254.7 5.0 %copy-start.4 = (f32[384,1000]{1,0:T(8,128)S(1)}, f32[384,1000]{1,0:T(8,128)}, u32[]{:S(2)}) copy-start(f32[384,1000]{1,0:T(8,128)} %copy.44) | copy-start | bytes 4608004
  262.6 3.7 %copy-start.8 = (bf16[48,8,1000]{2,1,0:T(8,128)(2,1)S(1)}, bf16[48,8,1000]{2,1,0:T(8,128)(2,1)}, u32[]{:S(2)}) copy-start(bf16[48,8,1000]{2,1,0:T(8,128)(2,1)} %get-tuple-element.23) | copy-start | bytes 2304004
  267.9 2.1 copy-start.7
  270.0 12.2 %copy-start.10 = (f32[384,1000]{1,0:T(8,128)S(1)}, f32[384,1000]{1,0:T(8,128)}, u32[]{:S(2)}) copy-start(f32[384,1000]{1,0:T(8,128)} %copy.47) | copy-start | bytes 4608004
  270.0 12.2 %copy-start.11 = (f32[384,1000]{1,0:T(8,128)S(1)}, f32[384,1000]{1,0:T(8,128)}, u32[]{:S(2)}) copy-start(f32[384,1000]{1,0:T(8,128)} %copy.46) | copy-start | bytes 4608004
  282.3 12.5 %copy-start.9 = (bf16[48,8,1000]{2,1,0:T(8,128)(2,1)S(1)}, bf16[48,8,1000]{2,1,0:T(8,128)(2,1)}, u32[]{:S(2)}) copy-start(bf16[48,8,1000]{2,1,0:T(8,128)(2,1)} %fusion.67) | copy-start | bytes 2304004
Sparse Core Ops, SparseCore 0:
  52.7 173.9 all-gather.1
